TPU v7x, 128 devices: a whole 4x4x4 slice. The times are simulated.
128 devices in a mesh: dp: 4 (over x), ctx: 8 (over z, core), head: 4 (over y).
Axes of the slice: x: 4, y: 4, z: 4, core: 2. Of those that a mesh axis runs over, the one named last changes fastest.
Arguments:
- token_values: bfloat16 [4, 4096, 8192], P('dp', 'ctx', 'head'), may hold values from -6 to 6
- gate_values: bfloat16 [4, 4096, 8192], P('dp', 'ctx', 'head'), may hold values from -6 to 6
- state_maps: bfloat16 [4, 4096, 8, 512], P('dp', 'ctx', 'head'), may hold values from -6 to 6
- step_raw: bfloat16 [4, 4096, 128], P('dp', 'ctx', 'head'), may hold values from -6.7 to 9.683792
- log_rate: float32 [128], P('head'), may hold values from -6 to 3
- skip_gain: float32 [128], P('head'), may hold values from 0.5 to 1.5
- conv_values: float32 [4, 8192], P(None, 'head'), may hold values from -3 to 3
- conv_maps: float32 [4, 8, 512], P(None, 'head'), may hold values from -3 to 3
- piece_shift: int32 [32], replicated, may hold values from 0 to 31, as said below
- doc_start: int32 [4, 4096], P('dp', 'ctx'), may hold values 0 or 1
- norm_gain: float32 [8192], P('head'), may hold values from 0.1 to 1.9
- out_weight: bfloat16 [8192, 4096], P('head'), may hold values from -0.0625 to 0.0625
Outputs:
- mixed: bfloat16 [4, 4096, 4096], P('dp', 'ctx', 'head')
Inputs may be any that keep to these rules, and one draw needn't show every extreme that they name: `piece_shift`: no value occurs more than 2 times and some value occurs exactly 2 times.
All inputs are finite; a program needn't handle non-finite values. No bound on the sum of `doc_start` on one device may be relied on, other than what follows from the above.
Results may differ from a plain program's by a relative error of at most 0.014.
Values may be sent and summed in bfloat16 or wider, within the bound.
No kernel may reach another device: no remote copies, remote signals or barrier semaphores. Data moves between devices by JAX's collectives and lax.ppermute only.
A program may use at most 256 MiB of HBM per device.

v0:
```python
import jax
import jax.numpy as jnp
from jax import lax
from jax.sharding import PartitionSpec as P

BLOCK_LEN = 128


eps = 1e-05


def passed_along(block, axis, distance):
    devices = range(lax.axis_size(axis))
    route = [(i - distance, i) for i in devices if i - distance in devices]
    return lax.ppermute(block, axis, route)


def prefix(shard, axis, join, neutral):
    place = lax.axis_index(axis)
    gathered = jax.tree.map(
        lambda a, kind: lax.all_gather(a.astype(kind), axis),
        shard,
        jax.tree.map(lambda a: jnp.bfloat16 if a.dtype == jnp.float32 else a.dtype, shard),
    )
    state = jax.tree.map(lambda a, e: jnp.zeros_like(a) + jnp.asarray(e, a.dtype), shard, neutral)

    def one(turn, state):
        return join(
            state,
            jax.tree.map(
                lambda a, own: lax.dynamic_index_in_dim(a, turn, 0, False).astype(own.dtype),
                gathered,
                shard,
            ),
        )

    return lax.fori_loop(0, place, one, state)


def conv_core(ext_values, weight, free_ext, length):
    tap_count = weight.shape[0]
    summed = jnp.zeros((length,) + ext_values.shape[1:], jnp.float32)
    keeping = jnp.ones((length,), jnp.float32)
    bshape = (length,) + (1,) * (ext_values.ndim - 1)
    for back in range(tap_count):
        if back > 0:
            keeping = keeping * free_ext[tap_count - back : tap_count - back + length]
        sample = ext_values[tap_count - 1 - back : tap_count - 1 - back + length].astype(
            jnp.float32
        )
        summed = summed + weight[tap_count - 1 - back] * sample * keeping.reshape(bshape)
    return jax.nn.silu(summed).astype(jnp.bfloat16)


def body(
    token_values,
    gate_values,
    state_maps,
    step_raw,
    log_rate,
    skip_gain,
    conv_values,
    conv_maps,
    piece_shift,
    doc_start,
    norm_gain,
    out_weight,
):
    owners = lax.axis_size(("dp", "ctx"))
    myself = lax.axis_index(("dp", "ctx"))
    slots = piece_shift.shape[0]
    rows = token_values.shape[1]
    piece_rows = rows // slots
    most = 2 * slots // owners
    slot_ids = jnp.arange(slots, dtype=jnp.int32)
    matching = piece_shift[:, None] == piece_shift[None, :]
    ranking = jnp.sum(
        (matching & (slot_ids[None, :] < slot_ids[:, None])).astype(jnp.int32), axis=1
    )
    offsets = (jnp.arange(owners, dtype=jnp.int32) - myself) % owners
    chosen = (piece_shift[None, None, :] == offsets[:, None, None]) & (
        ranking[None, None, :] == jnp.arange(most, dtype=jnp.int32)[None, :, None]
    )
    send_slot = jnp.sum(chosen.astype(jnp.int32) * slot_ids[None, None, :], axis=2)

    def outgoing(local):
        pieces = local[0].reshape((slots, piece_rows) + local.shape[2:])
        return pieces[send_slot]

    incoming = (
        lax.all_to_all(
            outgoing(token_values), ("dp", "ctx"), split_axis=0, concat_axis=0, tiled=True
        ),
        lax.all_to_all(
            outgoing(gate_values), ("dp", "ctx"), split_axis=0, concat_axis=0, tiled=True
        ),
        lax.all_to_all(
            outgoing(state_maps), ("dp", "ctx"), split_axis=0, concat_axis=0, tiled=True
        ),
        lax.all_to_all(outgoing(step_raw), ("dp", "ctx"), split_axis=0, concat_axis=0, tiled=True),
    )
    source = (myself - piece_shift) % owners

    def placed(received):
        return received[source, ranking].reshape((rows,) + received.shape[3:])

    x_pack = placed(incoming[0])
    z_pack = placed(incoming[1])
    map_pack = placed(incoming[2])
    dt_pack = placed(incoming[3])
    margin = conv_values.shape[0] - 1
    flags = doc_start[0].astype(jnp.bfloat16)
    rim_x, rim_maps, rim_flags = passed_along(
        (x_pack[rows - margin :], map_pack[rows - margin :], flags[rows - margin :]), "ctx", 1
    )
    free_ext = 1.0 - jnp.concatenate([rim_flags, flags]).astype(jnp.float32)
    x_conv = conv_core(jnp.concatenate([rim_x, x_pack]), conv_values, free_ext, rows)
    map_conv = conv_core(jnp.concatenate([rim_maps, map_pack]), conv_maps, free_ext, rows)
    heads_local = log_rate.shape[0]
    groups_local = map_pack.shape[1]
    per_group = heads_local // groups_local
    width = x_pack.shape[1] // heads_local
    state = map_pack.shape[2] // 2
    span = BLOCK_LEN
    blocks = rows // span
    step_dt = jax.nn.softplus(dt_pack.astype(jnp.float32))
    log_decay = step_dt * (-jnp.exp(log_rate))[None, :]
    cum_t = jnp.cumsum(log_decay.reshape(blocks, span, heads_local), axis=1).transpose(0, 2, 1)
    dt_t = step_dt.reshape(blocks, span, heads_local).transpose(0, 2, 1)
    segment = jnp.cumsum(doc_start[0].reshape(blocks, span), axis=1)
    x_blocks = x_conv.reshape(blocks, span, groups_local, per_group, width)
    b_blocks = map_conv[:, :, :state].reshape(blocks, span, groups_local, state)
    c_blocks = map_conv[:, :, state:].reshape(blocks, span, groups_local, state)
    scores = jnp.einsum("bqgn,bsgn->bgqs", c_blocks, b_blocks, preferred_element_type=jnp.float32)
    later = jnp.arange(span)[:, None] >= jnp.arange(span)[None, :]
    allowed = later[None] & (segment[:, :, None] == segment[:, None, :])
    spread = cum_t[:, :, :, None] - cum_t[:, :, None, :]
    decay = jnp.exp(jnp.where(allowed[:, None], spread, -jnp.inf))
    weights = (
        decay.reshape(blocks, groups_local, per_group, span, span)
        * scores[:, :, None]
        * dt_t.reshape(blocks, groups_local, per_group, 1, span)
    ).astype(jnp.bfloat16)
    y_diag = jnp.einsum("bghts,bsghp->btghp", weights, x_blocks, preferred_element_type=jnp.float32)
    same_end = (segment == segment[:, -1:]).astype(jnp.float32)
    carry_coef = jnp.exp(cum_t[:, :, -1:] - cum_t) * dt_t * same_end[:, None, :]
    x_weighted = (
        x_blocks.astype(jnp.float32)
        * carry_coef.transpose(0, 2, 1).reshape(blocks, span, groups_local, per_group, 1)
    ).astype(jnp.bfloat16)
    block_states = jnp.einsum(
        "bsghp,bsgn->bghpn", x_weighted, b_blocks, preferred_element_type=jnp.float32
    ).reshape(blocks, heads_local, width, state)
    block_gates = jnp.exp(cum_t[:, :, -1]) * (segment[:, -1] == 0).astype(jnp.float32)[:, None]

    def advance(carry, item):
        factor, summed = carry
        gate_now, state_now = item
        return ((factor * gate_now, gate_now[:, None, None] * summed + state_now), (factor, summed))

    start_pair = (
        jnp.ones((heads_local,), jnp.float32),
        jnp.zeros((heads_local, width, state), jnp.float32),
    )
    slab_pair, prior_pair = lax.scan(advance, start_pair, (block_gates, block_states))
    prior_gate, prior_state = prior_pair

    def combine(earlier, latter):
        return (earlier[0] * latter[0], latter[0][:, None, None] * earlier[1] + latter[1])

    arriving = prefix(slab_pair, "ctx", combine, start_pair)[1]
    entering = (
        (prior_state + prior_gate[:, :, None, None] * arriving[None])
        .astype(jnp.bfloat16)
        .reshape(blocks, groups_local, per_group, width, state)
    )
    y_off = jnp.einsum("bqgn,bghpn->bqghp", c_blocks, entering, preferred_element_type=jnp.float32)
    reach = (
        (jnp.exp(cum_t) * (segment == 0).astype(jnp.float32)[:, None, :])
        .transpose(0, 2, 1)
        .reshape(blocks, span, groups_local, per_group, 1)
    )
    mixed_y = (
        y_diag
        + y_off * reach
        + skip_gain.reshape(groups_local, per_group, 1) * x_blocks.astype(jnp.float32)
    )
    gated = mixed_y * jax.nn.silu(
        z_pack.astype(jnp.float32).reshape(blocks, span, groups_local, per_group, width)
    )
    power = jnp.mean(gated * gated, axis=(3, 4), keepdims=True)
    normed = (
        (gated * lax.rsqrt(power + eps) * norm_gain.reshape(groups_local, per_group, width))
        .astype(jnp.bfloat16)
        .reshape(rows, heads_local * width)
    )
    partial_value = jnp.dot(normed, out_weight, preferred_element_type=jnp.float32)
    result = lax.psum_scatter(
        partial_value.astype(jnp.bfloat16), "head", scatter_dimension=1, tiled=True
    )
    return result[None]


def solution(mesh):
    return jax.shard_map(
        body,
        mesh=mesh,
        in_specs=(
            P("dp", "ctx", "head"),
            P("dp", "ctx", "head"),
            P("dp", "ctx", "head", None),
            P("dp", "ctx", "head"),
            P("head"),
            P("head"),
            P(None, "head"),
            P(None, "head", None),
            P(),
            P("dp", "ctx"),
            P("head"),
            P("head", None),
        ),
        out_specs=P("dp", "ctx", "head"),
        check_vma=False,
    )
```

profile of v0, /device:TPU:2, one launch (start us, length us, event | category | flops | bytes accessed | tf_op | source)
XLA Modules:
  0.0 386.3 jit_solution(13866198227325960065)
XLA Ops:
  11.0 8.5 %all-to-all-start.1 = ((bf16[32,2,512]{2,1,0:T(2,128)(2,1)}), bf16[32,2,512]{2,1,0:T(2,128)(2,1)S(1)}, u32[]{:S(2)}, u32[]{:S(2)}) async-start(bf16[32,2,512]{2,1,0:T(2,128)(2,1)} %reshape.334), calls=%async_computation.1 | async-start | bytes 131072 | tf_op jit(solution)/shard_map/all_to_all | solution.py:100
  25.8 5.8 %all-to-all-start.2 = ((bf16[32,2,16,2,512]{4,2,3,1,0:T(8,128)(2,1)}), bf16[32,2,16,2,512]{4,2,3,1,0:T(8,128)(2,1)}, u32[]{:S(2)}, u32[]{:S(2)}) async-start(bf16[32,2,16,2,512]{4,2,3,1,0:T(8,128)(2,1)} %bitcast.108), calls=%async_computation.2 | async-start | bytes 4194304 | tf_op jit(solution)/shard_map/all_to_all | solution.py:97
  34.4 23.2 %all-to-all-done.2 = bf16[32,2,16,2,512]{4,2,3,1,0:T(8,128)(2,1)} async-done(((bf16[32,2,16,2,512]{4,2,3,1,0:T(8,128)(2,1)}), bf16[32,2,16,2,512]{4,2,3,1,0:T(8,128)(2,1)}, u32[]{:S(2)}, u32[]{:S(2)}) %all-to-all-start.2) | async-done | bytes 2097184 | tf_op jit(solution)/shard_map/all_to_all | solution.py:97
  57.6 7.9 %all-to-all-start = ((bf16[32,2,16,2048]{3,2,1,0:T(8,128)(2,1)}), bf16[32,2,16,2048]{3,2,1,0:T(8,128)(2,1)}, u32[]{:S(2)}, u32[]{:S(2)}) async-start(bf16[32,2,16,2048]{3,2,1,0:T(8,128)(2,1)} %bitcast.103), calls=%async_computation | async-start | bytes 8388608 | tf_op jit(solution)/shard_map/all_to_all | solution.py:91
  76.7 41.8 %collective-permute-start.2 = (bf16[3,2,512]{2,0,1:T(4,128)(2,1)S(1)}, bf16[3,2,512]{2,0,1:T(4,128)(2,1)S(1)}, u32[]{:S(2)}, u32[]{:S(2)}) collective-permute-start(bf16[3,2,512]{2,0,1:T(4,128)(2,1)S(1)} %slice.127), channel_id=1, source_target_pairs={{0,4},{4,8},{8,12},{12,16},{16,20},{20,24},{24,28},{1,5},{5,9},{9,... | collective-permute-start | bytes 18440 | tf_op jit(solution)/shard_map/ppermute | solution.py:15
  119.8 3.9 multiply_convert_fusion.4
  123.7 4.2 %gather_fusion.1 = bf16[32,16,2048]{2,1,0:T(8,128)(2,1)} fusion(bf16[32,2,16,2048]{3,2,1,0:T(8,128)(2,1)} %all-to-all-done, s32[32]{0:T(128)S(1)} %fusion.39), kind=kCustom, calls=%fused_computation.1 | custom fusion | bytes 4194560 | tf_op jit(solution)/shard_map/gather | solution.py:105
  128.6 5.0 %collective-permute-start = (bf16[3,2048]{1,0:T(4,128)(2,1)S(1)}, bf16[3,2048]{1,0:T(4,128)(2,1)S(1)}, u32[]{:S(2)}, u32[]{:S(2)}) collective-permute-start(bf16[3,2048]{1,0:T(4,128)(2,1)S(1)} %slice.121), channel_id=1, source_target_pairs={{0,4},{4,8},{8,12},{12,16},{16,20},{20,24},{24,28},{1,5},{5,9},{9,... | collective-permute-start | bytes 36872 | tf_op jit(solution)/shard_map/ppermute | solution.py:15
  134.9 9.1 %multiply_convert_fusion.3 = bf16[512,2048]{1,0:T(8,128)(2,1)} fusion(bf16[512,2048]{1,0:T(8,128)(2,1)} %bitcast.106, bf16[3,2048]{1,0:T(4,128)(2,1)S(1)} %collective-permute-done, f32[512]{0:T(512)S(1)} %get-tuple-element.144, f32[2048]{0:T(1024)} %bitcast.129, f32[512]{0:T(512)} %get-tuple-element.145, f32[2048]{0:T(1024)} %bitcast.130, ...), kind=kLoop, calls=%fused_computation.35 | loop fusion | flops 29360128 | bytes 4245504 | tf_op jit(solution)/shard_map/convert_element_type | solution.py:52
  144.0 7.1 %reshape.323 = bf16[4,128,2,16,64]{4,3,2,1,0:T(8,128)(2,1)} reshape(bf16[512,2048]{1,0:T(8,128)(2,1)} %multiply_convert_fusion.3) | data formatting | bytes 4194304 | tf_op jit(solution)/shard_map/reshape | solution.py:131
  151.1 6.5 %copy.168 = bf16[4,128,2,16,64]{1,4,3,2,0:T(8,128)(2,1)} copy(bf16[4,128,2,16,64]{4,3,2,1,0:T(8,128)(2,1)} %reshape.323) | data formatting | bytes 4194304 | tf_op jit(solution)/shard_map/reshape | solution.py:131
  157.6 6.1 %fusion.16 = f32[4,2,16,64,256]{4,3,2,1,0:T(8,128)} fusion(bf16[4,128,2,16,64]{1,4,3,2,0:T(8,128)(2,1)} %copy.168, f32[4,128,2,16]{1,3,2,0:T(8,128)S(1)} %get-tuple-element.152, bf16[4,128,2,256,1]{3,1,0,2,4:T(8,128)(2,1)S(1)} %bitcast.109), kind=kOutput, calls=%fused_computation.41 | convolution fusion | flops 540016640 | bytes 11075584 | tf_op jit(solution)/shard_map/bsghp,bsgn->bghpn/dot_general | solution.py:151
  163.7 21.3 %while.30 = (s32[]{:T(128)}, f32[32]{0:T(128)S(1)}, f32[32,64,256]{2,1,0:T(8,128)S(1)}, f32[4,32]{1,0:T(4,128)}, f32[4,32,64,256]{3,2,1,0:T(8,128)}, /*index=5*/...) while((s32[]{:T(128)}, f32[32]{0:T(128)S(1)}, f32[32,64,256]{2,1,0:T(8,128)S(1)}, ...), condition=%wide.region_5.6_spmd.clone, body=%wide.region_4.5_spmd.clone.sunk | while | flops 2097219 | bytes 10487413 | solution.py:165
  186.1 4.4 %gather_fusion.6 = bf16[64,16,2048]{2,1,0:T(8,128)(2,1)} fusion(bf16[32,16,2048]{2,1,0:T(8,128)(2,1)} %bitcast.107, s32[1024]{0:T(1024)S(1)} %pad_clamp_fusion), kind=kCustom, calls=%fused_computation.6 | custom fusion | bytes 8388864 | tf_op jit(solution)/shard_map/gather | solution.py:88
  190.5 9.4 %all-to-all-start.3 = ((bf16[32,2,16,2048]{3,2,1,0:T(8,128)(2,1)}), bf16[32,2,16,2048]{3,2,1,0:T(8,128)(2,1)}, u32[]{:S(2)}, u32[]{:S(2)}) async-start(bf16[32,2,16,2048]{3,2,1,0:T(8,128)(2,1)} %bitcast.104), calls=%async_computation.3 | async-start | bytes 8388608 | tf_op jit(solution)/shard_map/all_to_all | solution.py:94
  204.0 52.5 %all-to-all-done.3 = bf16[32,2,16,2048]{3,2,1,0:T(8,128)(2,1)} async-done(((bf16[32,2,16,2048]{3,2,1,0:T(8,128)(2,1)}), bf16[32,2,16,2048]{3,2,1,0:T(8,128)(2,1)}, u32[]{:S(2)}, u32[]{:S(2)}) %all-to-all-start.3) | async-done | bytes 4194336 | tf_op jit(solution)/shard_map/all_to_all | solution.py:94
  259.5 5.5 %reshape.247 = f32[4,128,2,16,64]{4,3,2,1,0:T(8,128)} reshape(bf16[32,16,2048]{2,1,0:T(8,128)(2,1)S(1)} %gather_fusion.7) | data formatting | bytes 6291456 | tf_op jit(solution)/shard_map/convert_element_type | solution.py:189
  265.0 8.2 %copy.180 = f32[4,128,2,16,64]{1,4,3,2,0:T(8,128)} copy(f32[4,128,2,16,64]{4,3,2,1,0:T(8,128)} %reshape.247) | data formatting | bytes 8388608 | tf_op jit(solution)/shard_map/convert_element_type | solution.py:189
  273.5 17.1 %all-reduce = bf16[256]{0:T(256)(128)(2,1)S(1)} all-reduce(bf16[256]{0:T(256)(128)(2,1)S(1)} %dynamic-update-slice), channel_id=2, replica_groups=mesh['dp'=4,'ctx'=8,'head'=4] {'ctx'}, use_global_device_ids=true, to_apply=%add | all-reduce | flops 256 | bytes 1024
  290.7 6.0 %fusion.3 = f32[4,2,16,64,128]{4,3,2,1,0:T(8,128)} fusion(bf16[4,128,2,16,64]{1,4,3,2,0:T(8,128)(2,1)S(1)} %copy-done.2, f32[4,2,16,128]{3,2,1,0:T(8,128)S(1)} %bitcast.125, f32[4,2,128,128]{3,2,1,0:T(8,128)S(1)} %copy-done.5, f32[4,2,16,128]{3,2,1,0:T(8,128)S(1)} %bitcast.126, pred[4,128,128]{2,1,0:T(8,128)(4,1)S(1)} %copy-done.7), kind=kOutput, calls=%fused_computation.22 | convolution fusion | flops 278921216 | bytes 7012352 | tf_op jit(solution)/shard_map/bghts,bsghp->btghp/dot_general | solution.py:144
  297.6 4.3 %add_convert_fusion = bf16[4,32,64,256]{3,2,1,0:T(8,128)(2,1)S(1)} fusion(f32[4,32,64,256]{3,2,1,0:T(8,128)} %get-tuple-element.89, f32[32,64,256]{2,1,0:T(8,128)S(1)} %get-tuple-element.93, f32[4,32]{1,0:T(4,128)S(1)} %copy-done.15), kind=kLoop, calls=%fused_computation.17 | loop fusion | flops 6291456 | bytes 14680576 | tf_op jit(solution)/shard_map/convert_element_type | solution.py:174
  302.8 3.8 multiply_reduce_fusion
  309.4 14.1 %convolution_convert_fusion = bf16[512,4096]{1,0:T(8,128)(2,1)} fusion(bf16[2048,4096]{1,0:T(8,128)(2,1)} %param.27, bf16[256,8,4,128]{3,2,1,0:T(4,128)(2,1)S(1)} %bitcast.117), kind=kOutput, calls=%fused_computation.19 | convolution fusion | flops 8592031744 | bytes 23068672 | tf_op jit(solution)/shard_map/dot_general | solution.py:197
  323.5 56.0 %reduce-scatter.2.cloned.1.call-done = bf16[512,1024]{1,0:T(8,128)(2,1)} async-done(((bf16[512,4096]{1,0:T(8,128)(2,1)}), bf16[512,1024]{1,0:T(8,128)(2,1)}) %reduce-scatter.2.cloned.1.call-update) | async-done | bytes 1048592 | tf_op jit(solution)/shard_map/reduce_scatter | solution.py:198
  (134 shorter events, 61.5 us)
Async XLA Ops:
  6.5 25.1 %copy-start = (bf16[1,512,2048]{2,1,0:T(8,128)(2,1)S(1)}, bf16[1,512,2048]{2,1,0:T(8,128)(2,1)}, u32[]{:S(2)}) copy-start(bf16[1,512,2048]{2,1,0:T(8,128)(2,1)} %param.16) | copy-start | bytes 6291460
  11.0 14.8 %all-to-all-start.1 = ((bf16[32,2,512]{2,1,0:T(2,128)(2,1)}), bf16[32,2,512]{2,1,0:T(2,128)(2,1)S(1)}, u32[]{:S(2)}, u32[]{:S(2)}) async-start(bf16[32,2,512]{2,1,0:T(2,128)(2,1)} %reshape.334), calls=%async_computation.1 | async-start | bytes 131072 | tf_op jit(solution)/shard_map/all_to_all | solution.py:100
  25.8 31.8 %all-to-all-start.2 = ((bf16[32,2,16,2,512]{4,2,3,1,0:T(8,128)(2,1)}), bf16[32,2,16,2,512]{4,2,3,1,0:T(8,128)(2,1)}, u32[]{:S(2)}, u32[]{:S(2)}) async-start(bf16[32,2,16,2,512]{4,2,3,1,0:T(8,128)(2,1)} %bitcast.108), calls=%async_computation.2 | async-start | bytes 4194304 | tf_op jit(solution)/shard_map/all_to_all | solution.py:97
  57.6 8.0 %copy-start.10 = (s32[1,512]{1,0:T(1,128)S(1)}, s32[1,512]{1,0:T(1,128)}, u32[]{:S(2)}) copy-start(s32[1,512]{1,0:T(1,128)} %param.25) | copy-start | bytes 6148
  57.6 11.3 %copy-start.16 = (f32[32]{0:T(128)S(1)}, f32[32]{0:T(128)}, u32[]{:S(2)}) copy-start(f32[32]{0:T(128)} %param.20) | copy-start | bytes 388
  57.6 11.4 %copy-start.14 = (s32[32]{0:T(128)S(1)}, s32[32]{0:T(128)}, u32[]{:S(2)}) copy-start(s32[32]{0:T(128)} %param.24) | copy-start | bytes 388
  57.6 11.5 %copy-start.11 = (f32[4,2,512]{2,1,0:T(2,128)S(1)}, f32[4,2,512]{2,1,0:T(2,128)}, u32[]{:S(2)}) copy-start(f32[4,2,512]{2,1,0:T(2,128)} %param.23) | copy-start | bytes 49156
  57.6 12.1 %copy-start.9 = (f32[4,2048]{1,0:T(4,128)S(1)}, f32[4,2048]{1,0:T(4,128)}, u32[]{:S(2)}) copy-start(f32[4,2048]{1,0:T(4,128)} %param.22) | copy-start | bytes 98308
  57.6 66.0 %all-to-all-start = ((bf16[32,2,16,2048]{3,2,1,0:T(8,128)(2,1)}), bf16[32,2,16,2048]{3,2,1,0:T(8,128)(2,1)}, u32[]{:S(2)}, u32[]{:S(2)}) async-start(bf16[32,2,16,2048]{3,2,1,0:T(8,128)(2,1)} %bitcast.103), calls=%async_computation | async-start | bytes 8388608 | tf_op jit(solution)/shard_map/all_to_all | solution.py:91
  65.5 231.1 %all-gather.4.cloned.1.call-start = ((), (), s32[]{:S(2)}) async-start(), calls=%async_computation.6 | async-start | bytes 9437184 | tf_op jit(solution)/shard_map/all_gather | solution.py:21
  65.7 4.6 %collective-permute-start.1 = (bf16[3]{0:T(256)(128)(2,1)S(1)}, bf16[3]{0:T(256)(128)(2,1)S(1)}, u32[]{:S(2)}, u32[]{:S(2)}) collective-permute-start(bf16[3]{0:T(256)(128)(2,1)S(1)} %slice_bitcast_fusion.4), channel_id=1, source_target_pairs={{0,4},{4,8},{8,12},{12,16},{16,20},{20,24},{24,28},{1,5},{5,9},{9,... | collective-permute-start | bytes 26 | tf_op jit(solution)/shard_map/ppermute | solution.py:15
  76.7 43.1 %collective-permute-start.2 = (bf16[3,2,512]{2,0,1:T(4,128)(2,1)S(1)}, bf16[3,2,512]{2,0,1:T(4,128)(2,1)S(1)}, u32[]{:S(2)}, u32[]{:S(2)}) collective-permute-start(bf16[3,2,512]{2,0,1:T(4,128)(2,1)S(1)} %slice.127), channel_id=1, source_target_pairs={{0,4},{4,8},{8,12},{12,16},{16,20},{20,24},{24,28},{1,5},{5,9},{9,... | collective-permute-start | bytes 18440 | tf_op jit(solution)/shard_map/ppermute | solution.py:15
  128.6 6.3 %collective-permute-start = (bf16[3,2048]{1,0:T(4,128)(2,1)S(1)}, bf16[3,2048]{1,0:T(4,128)(2,1)S(1)}, u32[]{:S(2)}, u32[]{:S(2)}) collective-permute-start(bf16[3,2048]{1,0:T(4,128)(2,1)S(1)} %slice.121), channel_id=1, source_target_pairs={{0,4},{4,8},{8,12},{12,16},{16,20},{20,24},{24,28},{1,5},{5,9},{9,... | collective-permute-start | bytes 36872 | tf_op jit(solution)/shard_map/ppermute | solution.py:15
  157.6 6.1 %copy-start.12 = (f32[32]{0:T(128)S(1)}, f32[32]{0:T(128)}, u32[]{:S(2)}) copy-start(f32[32]{0:T(128)} %custom-call.8) | copy-start | bytes 388
  190.5 9.4 %copy-start.17 = (f32[32]{0:T(128)S(1)}, f32[32]{0:T(128)}, u32[]{:S(2)}) copy-start(f32[32]{0:T(128)} %param.21) | copy-start | bytes 388
  190.5 9.5 %copy-start.13 = (f32[2048]{0:T(1024)S(1)}, f32[2048]{0:T(1024)}, u32[]{:S(2)}) copy-start(f32[2048]{0:T(1024)} %param.26) | copy-start | bytes 24580
  190.5 9.6 %copy-start.18 = (u32[128]{0:T(128)S(1)}, u32[128]{0:T(128)}, u32[]{:S(2)}) copy-start(u32[128]{0:T(128)} %constant.160) | copy-start | bytes 1540
  190.5 66.0 %all-to-all-start.3 = ((bf16[32,2,16,2048]{3,2,1,0:T(8,128)(2,1)}), bf16[32,2,16,2048]{3,2,1,0:T(8,128)(2,1)}, u32[]{:S(2)}, u32[]{:S(2)}) async-start(bf16[32,2,16,2048]{3,2,1,0:T(8,128)(2,1)} %bitcast.104), calls=%async_computation.3 | async-start | bytes 8388608 | tf_op jit(solution)/shard_map/all_to_all | solution.py:94
  199.8 179.6 %reduce-scatter.2.cloned.1.call-start = ((), (), s32[]{:S(2)}) async-start(), calls=%async_computation.5 | async-start | bytes 5242880 | tf_op jit(solution)/shard_map/reduce_scatter | solution.py:198
  265.0 25.6 %copy-start.2 = (bf16[4,128,2,16,64]{1,4,3,2,0:T(8,128)(2,1)S(1)}, bf16[4,128,2,16,64]{1,4,3,2,0:T(8,128)(2,1)}, u32[]{:S(2)}) copy-start(bf16[4,128,2,16,64]{1,4,3,2,0:T(8,128)(2,1)} %copy.168) | copy-start | bytes 6291460
  265.0 25.7 %copy-start.5 = (f32[4,2,128,128]{3,2,1,0:T(8,128)S(1)}, f32[4,2,128,128]{3,2,1,0:T(8,128)}, u32[]{:S(2)}) copy-start(f32[4,2,128,128]{3,2,1,0:T(8,128)} %fusion.25) | copy-start | bytes 1572868
  265.0 25.7 %copy-start.6 = (f32[4,32,128]{2,1,0:T(8,128)S(1)}, f32[4,32,128]{2,1,0:T(8,128)}, u32[]{:S(2)}) copy-start(f32[4,32,128]{2,1,0:T(8,128)} %copy.162) | copy-start | bytes 196612
  265.0 25.7 %copy-start.7 = (pred[4,128,128]{2,1,0:T(8,128)(4,1)S(1)}, pred[4,128,128]{2,1,0:T(8,128)(4,1)}, u32[]{:S(2)}) copy-start(pred[4,128,128]{2,1,0:T(8,128)(4,1)} %compare_and_fusion) | copy-start | bytes 196612
  309.4 70.1 %copy-start.1 = (bf16[1,512,2048]{2,1,0:T(8,128)(2,1)S(1)}, bf16[1,512,2048]{2,1,0:T(8,128)(2,1)}, u32[]{:S(2)}) copy-start(bf16[1,512,2048]{2,1,0:T(8,128)(2,1)} %param.16) | copy-start | bytes 6291460
  (4 other events, 15.4 us)
Sparse Core Ops, SparseCore 0:
  186.2 97.7 all-gather.3
  323.6 55.8 reduce-scatter.1
where the time goes:
time: 389 us; the launch traced here: 386 us
  waiting for transfers between devices  135 us (35%)
  starting transfers between devices  80.4 us (21%)
  local copies, waits for them, and re-layouts  65.8 us (17%)
  other arithmetic  42.6 us (11%)
  matrix products  31.1 us (8%)
  blocking collectives  17.1 us (4%)
  between operations  14.5 us (4%)
    reduce_scatter x1, waiting for transfers between devices, body(): lax.psum_scatter(partial_value.astype(jnp.bfloat16), 'head', scatter_dime...  56 us
    all_to_all x1, waiting for transfers between devices, body(): lax.all_to_all(outgoing(gate_values), ('dp', 'ctx'), split_axis=0, concat...  52.5 us
    ppermute x3, starting transfers between devices, passed_along(): return lax.ppermute(block, axis, route)  48.8 us
    all_to_all x1, waiting for transfers between devices, body(): lax.all_to_all(outgoing(state_maps), ('dp', 'ctx'), split_axis=0, concat_...  23.2 us
    unnamed x1, blocking collectives  17.1 us
    dot_general x1, matrix products, body(): jnp.dot(normed, out_weight, preferred_element_type=jnp.float32)  14.1 us
    convert_element_type x2, local copies, waits for them, and re-layouts, body(): z_pack.astype(jnp.float32)  13.7 us
    reshape x2, local copies, waits for them, and re-layouts, body(): x_blocks = x_conv.reshape(blocks, span, groups_local, per_group, width)  13.5 us
  transfers between devices with their start and end apart: 9, of which 4 were waited for; matrix products, arithmetic and copies ran while one was open for 14% of the time, Pallas kernels for 0%

commit v1 on v0

--- a/solution.py
+++ b/solution.py
@@ -15,26 +15,30 @@
     return lax.ppermute(block, axis, route)
 
 
-def prefix(shard, axis, join, neutral):
+def chain(gate, summed, axis):
     place = lax.axis_index(axis)
-    gathered = jax.tree.map(
-        lambda a, kind: lax.all_gather(a.astype(kind), axis),
-        shard,
-        jax.tree.map(lambda a: jnp.bfloat16 if a.dtype == jnp.float32 else a.dtype, shard),
-    )
-    state = jax.tree.map(lambda a, e: jnp.zeros_like(a) + jnp.asarray(e, a.dtype), shard, neutral)
-
-    def one(turn, state):
-        return join(
-            state,
-            jax.tree.map(
-                lambda a, own: lax.dynamic_index_in_dim(a, turn, 0, False).astype(own.dtype),
-                gathered,
-                shard,
-            ),
+
+    def join(earlier, latter):
+        return (earlier[0] * latter[0], latter[0][:, None, None] * earlier[1] + latter[1])
+
+    def fetch(pair, distance):
+        gate_in, summed_in = passed_along(
+            (pair[0], pair[1].astype(jnp.bfloat16)), axis, distance
         )
-
-    return lax.fori_loop(0, place, one, state)
+        gate_in = jnp.where(place >= distance, gate_in, 1.0)
+        return gate_in, summed_in.astype(jnp.float32)
+
+    local = (gate, summed)
+    before = fetch(local, 1)
+    window = join(before, local)
+    distance = 2
+    while distance < lax.axis_size(axis):
+        received = fetch(window, distance)
+        before = join(received, before)
+        distance *= 2
+        if distance < lax.axis_size(axis):
+            window = join(received, window)
+    return before[1]
 
 
 def conv_core(ext_values, weight, free_ext, length):
@@ -87,32 +91,38 @@
         pieces = local[0].reshape((slots, piece_rows) + local.shape[2:])
         return pieces[send_slot]
 
-    incoming = (
-        lax.all_to_all(
-            outgoing(token_values), ("dp", "ctx"), split_axis=0, concat_axis=0, tiled=True
-        ),
-        lax.all_to_all(
-            outgoing(gate_values), ("dp", "ctx"), split_axis=0, concat_axis=0, tiled=True
-        ),
-        lax.all_to_all(
-            outgoing(state_maps), ("dp", "ctx"), split_axis=0, concat_axis=0, tiled=True
-        ),
-        lax.all_to_all(outgoing(step_raw), ("dp", "ctx"), split_axis=0, concat_axis=0, tiled=True),
+    features = token_values.shape[2]
+    map_shape = state_maps.shape[2:]
+    map_width = map_shape[0] * map_shape[1]
+    joined = jnp.concatenate(
+        [token_values[0], state_maps[0].reshape(rows, map_width), step_raw[0]], axis=1
+    )
+    incoming = lax.all_to_all(
+        outgoing(joined[None]), ("dp", "ctx"), split_axis=0, concat_axis=0, tiled=True
+    )
+    incoming_z = lax.all_to_all(
+        outgoing(gate_values), ("dp", "ctx"), split_axis=0, concat_axis=0, tiled=True
     )
     source = (myself - piece_shift) % owners
 
     def placed(received):
         return received[source, ranking].reshape((rows,) + received.shape[3:])
 
-    x_pack = placed(incoming[0])
-    z_pack = placed(incoming[1])
-    map_pack = placed(incoming[2])
-    dt_pack = placed(incoming[3])
+    joined_pack = placed(incoming)
+    z_pack = placed(incoming_z)
     margin = conv_values.shape[0] - 1
     flags = doc_start[0].astype(jnp.bfloat16)
-    rim_x, rim_maps, rim_flags = passed_along(
-        (x_pack[rows - margin :], map_pack[rows - margin :], flags[rows - margin :]), "ctx", 1
-    )
+    rim = passed_along(
+        jnp.concatenate([joined_pack[rows - margin :], flags[rows - margin :, None]], axis=1),
+        "ctx",
+        1,
+    )
+    rim_x = rim[:, :features]
+    rim_maps = rim[:, features : features + map_width].reshape((margin,) + map_shape)
+    rim_flags = rim[:, -1]
+    x_pack = joined_pack[:, :features]
+    map_pack = joined_pack[:, features : features + map_width].reshape((rows,) + map_shape)
+    dt_pack = joined_pack[:, features + map_width :]
     free_ext = 1.0 - jnp.concatenate([rim_flags, flags]).astype(jnp.float32)
     x_conv = conv_core(jnp.concatenate([rim_x, x_pack]), conv_values, free_ext, rows)
     map_conv = conv_core(jnp.concatenate([rim_maps, map_pack]), conv_maps, free_ext, rows)
@@ -153,24 +163,16 @@
     ).reshape(blocks, heads_local, width, state)
     block_gates = jnp.exp(cum_t[:, :, -1]) * (segment[:, -1] == 0).astype(jnp.float32)[:, None]
 
-    def advance(carry, item):
-        factor, summed = carry
-        gate_now, state_now = item
-        return ((factor * gate_now, gate_now[:, None, None] * summed + state_now), (factor, summed))
-
-    start_pair = (
-        jnp.ones((heads_local,), jnp.float32),
-        jnp.zeros((heads_local, width, state), jnp.float32),
-    )
-    slab_pair, prior_pair = lax.scan(advance, start_pair, (block_gates, block_states))
-    prior_gate, prior_state = prior_pair
-
-    def combine(earlier, latter):
-        return (earlier[0] * latter[0], latter[0][:, None, None] * earlier[1] + latter[1])
-
-    arriving = prefix(slab_pair, "ctx", combine, start_pair)[1]
+    prior_states = [jnp.zeros_like(block_states[0])]
+    prior_gates = [jnp.ones_like(block_gates[0])]
+    for b in range(1, blocks):
+        prior_states.append(block_gates[b - 1][:, None, None] * prior_states[-1] + block_states[b - 1])
+        prior_gates.append(prior_gates[-1] * block_gates[b - 1])
+    slab_state = block_gates[-1][:, None, None] * prior_states[-1] + block_states[-1]
+    slab_gate = prior_gates[-1] * block_gates[-1]
+    arriving = chain(slab_gate, slab_state, "ctx")
     entering = (
-        (prior_state + prior_gate[:, :, None, None] * arriving[None])
+        (jnp.stack(prior_states) + jnp.stack(prior_gates)[:, :, None, None] * arriving[None])
         .astype(jnp.bfloat16)
         .reshape(blocks, groups_local, per_group, width, state)
     )

time: 389 us -> 368 us (0.946)
  blocking collectives: 17.1 us -> 0 us
  waiting for transfers between devices: 135 us -> 143 us
  other arithmetic: 42.6 us -> 37.2 us
  local copies, waits for them, and re-layouts: 65.8 us -> 61.5 us
    all_to_all x1, waiting for transfers between devices: 52.5 us -> 0.01 us  [body(): lax.all_to_all(outgoing(gate_values), ('dp', 'ctx'), split_axis=0, concat...]
    all_to_all x3 -> x1, waiting for transfers between devices: 26.1 us -> 75.1 us  [body(): lax.all_to_all(outgoing(joined[None]), ('dp', 'ctx'), split_axis=0, conca...]
    ppermute x3 -> x6, waiting for transfers between devices: 0.01 us -> 20.4 us  [passed_along(): return lax.ppermute(block, axis, route)]
    unnamed x1 -> x0, blocking collectives: 17.1 us -> none
    all_to_all x3 -> x1, starting transfers between devices: 22.2 us -> 8.65 us  [body(): lax.all_to_all(outgoing(joined[None]), ('dp', 'ctx'), split_axis=0, conca...]
    ppermute x3 -> x6, starting transfers between devices: 48.8 us -> 57.8 us  [passed_along(): return lax.ppermute(block, axis, route)]
    reduce_scatter x1, waiting for transfers between devices: 56 us -> 47.4 us  [body(): lax.psum_scatter(partial_value.astype(jnp.bfloat16), 'head', scatter_dime...]
    all_to_all x1, starting transfers between devices: 9.36 us -> 16.5 us  [body(): lax.all_to_all(outgoing(gate_values), ('dp', 'ctx'), split_axis=0, concat...]
  transfers between devices with their start and end apart: 9 -> 9, of which waited for: 4 -> 4; matrix products, arithmetic and copies ran while one was open for 14% -> 24% of each run, Pallas kernels for 0% -> 0%
where the time goes in v1:
time: 368 us; the launch traced here: 366 us
  waiting for transfers between devices  143 us (39%)
  starting transfers between devices  82.9 us (23%)
  local copies, waits for them, and re-layouts  61.5 us (17%)
  other arithmetic  37.2 us (10%)
  matrix products  27.5 us (7%)
  between operations  13.9 us (4%)
    all_to_all x1, waiting for transfers between devices, body(): lax.all_to_all(outgoing(joined[None]), ('dp', 'ctx'), split_axis=0, conca...  75.1 us
    ppermute x6, starting transfers between devices, passed_along(): return lax.ppermute(block, axis, route)  57.8 us
    reduce_scatter x1, waiting for transfers between devices, body(): lax.psum_scatter(partial_value.astype(jnp.bfloat16), 'head', scatter_dime...  47.4 us
    ppermute x6, waiting for transfers between devices, passed_along(): return lax.ppermute(block, axis, route)  20.4 us
    all_to_all x1, starting transfers between devices, body(): lax.all_to_all(outgoing(gate_values), ('dp', 'ctx'), split_axis=0, concat...  16.5 us
    convert_element_type x2, local copies, waits for them, and re-layouts, body(): z_pack.astype(jnp.float32)  15.4 us
    dot_general x1, matrix products, body(): jnp.dot(normed, out_weight, preferred_element_type=jnp.float32)  14 us
    reshape x2, local copies, waits for them, and re-layouts, body(): x_blocks = x_conv.reshape(blocks, span, groups_local, per_group, width)  11 us
  transfers between devices with their start and end apart: 9, of which 4 were waited for; matrix products, arithmetic and copies ran while one was open for 24% of the time, Pallas kernels for 0%

profile of v1, /device:TPU:2, one launch (start us, length us, event | category | flops | bytes accessed | tf_op | source)
XLA Modules:
  0.0 366.0 jit_solution(17062110401856821631)
XLA Ops:
  10.6 3.0 pad_maximum_fusion
  13.6 5.9 %gather_fusion = bf16[64,16,3104]{2,1,0:T(8,128)(2,1)} fusion(bf16[32,16,3104]{2,1,0:T(8,128)(2,1)} %pad_maximum_fusion, s32[1024]{0:T(1024)S(1)} %pad_clamp_fusion), kind=kCustom, calls=%fused_computation | custom fusion | bytes 12714240 | tf_op jit(solution)/shard_map/gather | solution.py:92
  19.5 8.6 %all-to-all-start = ((bf16[32,2,16,3104]{3,2,1,0:T(8,128)(2,1)}), bf16[32,2,16,3104]{3,2,1,0:T(8,128)(2,1)}, u32[]{:S(2)}, u32[]{:S(2)}) async-start(bf16[32,2,16,3104]{3,2,1,0:T(8,128)(2,1)} %bitcast.124), calls=%async_computation | async-start | bytes 13107200 | tf_op jit(solution)/shard_map/all_to_all | solution.py:100
  28.4 2.8 gather_fusion.2
  32.7 75.1 %all-to-all-done = bf16[32,2,16,3104]{3,2,1,0:T(8,128)(2,1)} async-done(((bf16[32,2,16,3104]{3,2,1,0:T(8,128)(2,1)}), bf16[32,2,16,3104]{3,2,1,0:T(8,128)(2,1)}, u32[]{:S(2)}, u32[]{:S(2)}) %all-to-all-start) | async-done | bytes 6357024 | tf_op jit(solution)/shard_map/all_to_all | solution.py:100
  107.8 16.5 %all-to-all-start.1 = ((bf16[32,2,16,2048]{3,2,1,0:T(8,128)(2,1)}), bf16[32,2,16,2048]{3,2,1,0:T(8,128)(2,1)}, u32[]{:S(2)}, u32[]{:S(2)}) async-start(bf16[32,2,16,2048]{3,2,1,0:T(8,128)(2,1)} %bitcast.125), calls=%async_computation.1 | async-start | bytes 8388608 | tf_op jit(solution)/shard_map/all_to_all | solution.py:103
  124.3 5.5 %gather_fusion.1 = bf16[32,16,3104]{2,1,0:T(8,128)(2,1)} fusion(bf16[32,2,16,3104]{3,2,1,0:T(8,128)(2,1)} %all-to-all-done, s32[32]{0:T(128)S(1)} %fusion.55), kind=kCustom, calls=%fused_computation.1 | custom fusion | bytes 6357248 | tf_op jit(solution)/shard_map/gather | solution.py:109
  137.8 3.2 slice.170
  143.4 7.7 %multiply_convert_fusion.3 = bf16[512,2048]{1,0:T(8,128)(2,1)S(1)} fusion(bf16[512,2048]{1,0:T(8,128)(2,1)} %slice.170, bf16[3,2048]{1,0:T(4,128)(2,1)S(1)} %slice.173, f32[512]{0:T(512)S(1)} %get-tuple-element.17, f32[2048]{0:T(1024)S(1)} %bitcast.150, f32[512]{0:T(512)S(1)} %get-tuple-element.18, f32[2048]{0:T(1024)S(1)} %bitcast.151, ...), kind=kLoop, calls=%fused_computation.23 | loop fusion | flops 29360128 | bytes 4245504 | tf_op jit(solution)/shard_map/convert_element_type | solution.py:56
  151.1 5.4 %reshape.346 = bf16[4,128,2,16,64]{4,3,2,1,0:T(8,128)(2,1)} reshape(bf16[512,2048]{1,0:T(8,128)(2,1)S(1)} %multiply_convert_fusion.3) | data formatting | bytes 4194304 | tf_op jit(solution)/shard_map/reshape | solution.py:141
  156.5 5.6 %copy.72 = bf16[4,128,2,16,64]{1,4,3,2,0:T(8,128)(2,1)S(1)} copy(bf16[4,128,2,16,64]{4,3,2,1,0:T(8,128)(2,1)} %reshape.346) | data formatting | bytes 4194304 | tf_op jit(solution)/shard_map/reshape | solution.py:141
  166.2 4.5 %fusion.20 = f32[4,2,16,64,256]{4,3,2,1,0:T(8,128)} fusion(bf16[4,128,2,16,64]{1,4,3,2,0:T(8,128)(2,1)S(1)} %copy.72, f32[4,128,2,16]{1,3,2,0:T(8,128)S(1)} %get-tuple-element.29, bf16[4,128,2,256,1]{3,1,0,2,4:T(8,128)(2,1)S(1)} %bitcast.130), kind=kOutput, calls=%fused_computation.39 | convolution fusion | flops 540016640 | bytes 11075584 | tf_op jit(solution)/shard_map/bsghp,bsgn->bghpn/dot_general | solution.py:161
  170.7 7.9 %multiply_add_fusion = (f32[1,2,16,64,256]{4,3,2,1,0:T(8,128)}, f32[1,2,16,64,256]{4,3,2,1,0:T(8,128)}, f32[1,2,16,64,256]{4,3,2,1,0:T(8,128)}, f32[1,2,16,64,25...) fusion(f32[2,16]{1,0:T(2,128)S(1)} %copy-done.32, ...), kind=kLoop, calls=%fused_computation.50 | loop fusion | flops 2621440 | bytes 23069056 | tf_op jit(solution)/shard_map/add | solution.py:169
  181.1 28.5 %collective-permute-start.3 = (bf16[32,64,256]{2,1,0:T(8,128)(2,1)S(1)}, bf16[32,64,256]{2,1,0:T(8,128)(2,1)S(1)}, u32[]{:S(2)}, u32[]{:S(2)}) collective-permute-start(bf16[32,64,256]{2,1,0:T(8,128)(2,1)S(1)} %get-tuple-element.12), channel_id=1, source_target_pairs={{0,4},{4,8},{8,12},{12,16},{16,20},{20,24},{24,28},{1,5},{5,9},{9,... | collective-permute-start | bytes 3145736 | tf_op jit(solution)/shard_map/ppermute | solution.py:15
  213.1 17.3 %collective-permute-start.4 = (bf16[32,64,256]{2,1,0:T(8,128)(2,1)}, bf16[32,64,256]{2,1,0:T(8,128)(2,1)}, u32[]{:S(2)}, u32[]{:S(2)}) collective-permute-start(bf16[32,64,256]{2,1,0:T(8,128)(2,1)} %fusion.28), channel_id=1, source_target_pairs={{0,8},{4,12},{8,16},{12,20},{16,24},{20,28},{1,9},{5,13},{9,17},{1... | collective-permute-start | bytes 3145736 | tf_op jit(solution)/shard_map/ppermute | solution.py:15
  231.4 4.2 %gather_fusion.3 = bf16[32,16,2048]{2,1,0:T(8,128)(2,1)} fusion(bf16[32,2,16,2048]{3,2,1,0:T(8,128)(2,1)} %all-to-all-done.1, s32[32]{0:T(128)S(1)} %fusion.55), kind=kCustom, calls=%fused_computation.3 | custom fusion | bytes 4194560 | tf_op jit(solution)/shard_map/gather | solution.py:109
  237.1 7.4 %reshape.308 = f32[4,128,2,16,64]{4,3,2,1,0:T(8,128)} reshape(bf16[32,16,2048]{2,1,0:T(8,128)(2,1)} %gather_fusion.3) | data formatting | bytes 6291456 | tf_op jit(solution)/shard_map/convert_element_type | solution.py:191
  244.5 8.0 %copy.80 = f32[4,128,2,16,64]{1,4,3,2,0:T(8,128)} copy(f32[4,128,2,16,64]{4,3,2,1,0:T(8,128)} %reshape.308) | data formatting | bytes 8388608 | tf_op jit(solution)/shard_map/convert_element_type | solution.py:191
  255.2 6.6 %collective-permute-start.5 = (bf16[32,64,256]{2,1,0:T(8,128)(2,1)}, bf16[32,64,256]{2,1,0:T(8,128)(2,1)}, u32[]{:S(2)}, u32[]{:S(2)}) collective-permute-start(bf16[32,64,256]{2,1,0:T(8,128)(2,1)} %fusion.17), channel_id=1, source_target_pairs={{0,16},{4,20},{8,24},{12,28},{1,17},{5,21},{9,25},{13,29},{2,18},{... | collective-permute-start | bytes 3145736 | tf_op jit(solution)/shard_map/ppermute | solution.py:15
  264.8 18.2 %collective-permute-done.2 = f32[32]{0:T(128)S(1)} collective-permute-done((f32[32]{0:T(128)S(1)}, f32[32]{0:T(128)S(1)}, u32[]{:S(2)}, u32[]{:S(2)}) %collective-permute-start.2) | collective-permute-done | bytes 160 | tf_op jit(solution)/shard_map/ppermute | solution.py:15
  284.5 4.5 %fusion.1 = f32[4,2,16,64,128]{4,3,2,1,0:T(8,128)S(1)} fusion(bf16[4,128,2,16,64]{1,4,3,2,0:T(8,128)(2,1)S(1)} %copy-done.3, f32[4,2,16,128]{3,2,1,0:T(8,128)S(1)} %bitcast.146, f32[4,2,128,128]{3,2,1,0:T(8,128)S(1)} %fusion.35, f32[4,2,16,128]{3,2,1,0:T(8,128)S(1)} %bitcast.145, pred[4,128,128]{2,1,0:T(8,128)(4,1)} %compare_and_fusion), kind=kOutput, calls=%fused_computation.10 | convolution fusion | flops 278921216 | bytes 7012352 | tf_op jit(solution)/shard_map/bghts,bsghp->btghp/dot_general | solution.py:154
  292.0 3.0 multiply_reduce_fusion
  297.8 14.0 %convolution_convert_fusion = bf16[512,4096]{1,0:T(8,128)(2,1)} fusion(bf16[2048,4096]{1,0:T(8,128)(2,1)} %param.23, bf16[256,8,4,128]{3,2,1,0:T(4,128)(2,1)S(1)} %bitcast.139), kind=kOutput, calls=%fused_computation.7 | convolution fusion | flops 8592031744 | bytes 23068672 | tf_op jit(solution)/shard_map/dot_general | solution.py:199
  311.8 47.4 %reduce-scatter.2.cloned.1.call-done = bf16[512,1024]{1,0:T(8,128)(2,1)} async-done(((bf16[512,4096]{1,0:T(8,128)(2,1)}), bf16[512,1024]{1,0:T(8,128)(2,1)}) %reduce-scatter.2.cloned.1.call-update) | async-done | bytes 1048592 | tf_op jit(solution)/shard_map/reduce_scatter | solution.py:200
  (149 shorter events, 41.2 us)
Async XLA Ops:
  6.5 21.8 %copy-start = (bf16[1,512,2048]{2,1,0:T(8,128)(2,1)S(1)}, bf16[1,512,2048]{2,1,0:T(8,128)(2,1)}, u32[]{:S(2)}) copy-start(bf16[1,512,2048]{2,1,0:T(8,128)(2,1)} %param.13) | copy-start | bytes 6291460
  19.5 8.7 %copy-start.14 = (s32[1,512]{1,0:T(1,128)S(1)}, s32[1,512]{1,0:T(1,128)}, u32[]{:S(2)}) copy-start(s32[1,512]{1,0:T(1,128)} %param.21) | copy-start | bytes 6148
  19.5 88.3 %all-to-all-start = ((bf16[32,2,16,3104]{3,2,1,0:T(8,128)(2,1)}), bf16[32,2,16,3104]{3,2,1,0:T(8,128)(2,1)}, u32[]{:S(2)}, u32[]{:S(2)}) async-start(bf16[32,2,16,3104]{3,2,1,0:T(8,128)(2,1)} %bitcast.124), calls=%async_computation | async-start | bytes 13107200 | tf_op jit(solution)/shard_map/all_to_all | solution.py:100
  107.8 123.6 %all-to-all-start.1 = ((bf16[32,2,16,2048]{3,2,1,0:T(8,128)(2,1)}), bf16[32,2,16,2048]{3,2,1,0:T(8,128)(2,1)}, u32[]{:S(2)}, u32[]{:S(2)}) async-start(bf16[32,2,16,2048]{3,2,1,0:T(8,128)(2,1)} %bitcast.125), calls=%async_computation.1 | async-start | bytes 8388608 | tf_op jit(solution)/shard_map/all_to_all | solution.py:103
  124.3 234.9 %reduce-scatter.2.cloned.1.call-start = ((), (), s32[]{:S(2)}) async-start(), calls=%async_computation.3 | async-start | bytes 5242880 | tf_op jit(solution)/shard_map/reduce_scatter | solution.py:200
  130.7 12.3 %collective-permute-start = (bf16[3,3105]{1,0:T(4,128)(2,1)S(1)}, bf16[3,3105]{1,0:T(4,128)(2,1)S(1)}, u32[]{:S(2)}, u32[]{:S(2)}) collective-permute-start(bf16[3,3105]{1,0:T(4,128)(2,1)S(1)} %pad_maximum_fusion.3), channel_id=1, source_target_pairs={{0,4},{4,8},{8,12},{12,16},{16,20},{20,24},{24,28},{1,5},{5,9},{9,... | collective-permute-start | bytes 55898 | tf_op jit(solution)/shard_map/ppermute | solution.py:15
  134.0 7.0 %copy-start.6 = (f32[512,32]{1,0:T(8,128)}, f32[512,32]{1,0:T(8,128)S(1)}, u32[]{:S(2)}) copy-start(f32[512,32]{1,0:T(8,128)S(1)} %get-tuple-element.24) | copy-start | bytes 196612
  170.7 7.9 %copy-start.22 = (f32[32]{0:T(128)S(1)}, f32[32]{0:T(128)}, u32[]{:S(2)}) copy-start(f32[32]{0:T(128)} %get-tuple-element.50) | copy-start | bytes 388
  170.7 7.9 %copy-start.23 = (f32[32]{0:T(128)S(1)}, f32[32]{0:T(128)}, u32[]{:S(2)}) copy-start(f32[32]{0:T(128)} %get-tuple-element.41) | copy-start | bytes 388
  170.7 7.9 %copy-start.24 = (f32[32]{0:T(128)S(1)}, f32[32]{0:T(128)}, u32[]{:S(2)}) copy-start(f32[32]{0:T(128)} %get-tuple-element.44) | copy-start | bytes 388
  170.7 7.9 %copy-start.25 = (f32[32]{0:T(128)S(1)}, f32[32]{0:T(128)}, u32[]{:S(2)}) copy-start(f32[32]{0:T(128)} %get-tuple-element.45) | copy-start | bytes 388
  178.7 33.1 %copy-start.20 = (f32[32]{0:T(128)S(1)}, f32[32]{0:T(128)}, u32[]{:S(2)}) copy-start(f32[32]{0:T(128)} %get-tuple-element.49) | copy-start | bytes 388
  181.1 30.7 %collective-permute-start.3 = (bf16[32,64,256]{2,1,0:T(8,128)(2,1)S(1)}, bf16[32,64,256]{2,1,0:T(8,128)(2,1)S(1)}, u32[]{:S(2)}, u32[]{:S(2)}) collective-permute-start(bf16[32,64,256]{2,1,0:T(8,128)(2,1)S(1)} %get-tuple-element.12), channel_id=1, source_target_pairs={{0,4},{4,8},{8,12},{12,16},{16,20},{20,24},{24,28},{1,5},{5,9},{9,... | collective-permute-start | bytes 3145736 | tf_op jit(solution)/shard_map/ppermute | solution.py:15
  211.8 18.6 %copy-start.34 = (f32[32]{0:T(128)S(1)}, f32[32]{0:T(128)}, u32[]{:S(2)}) copy-start(f32[32]{0:T(128)} %param.17) | copy-start | bytes 388
  211.8 18.7 %copy-start.21 = (f32[2048]{0:T(1024)S(1)}, f32[2048]{0:T(1024)}, u32[]{:S(2)}) copy-start(f32[2048]{0:T(1024)} %param.22) | copy-start | bytes 24580
  213.1 39.4 %collective-permute-start.4 = (bf16[32,64,256]{2,1,0:T(8,128)(2,1)}, bf16[32,64,256]{2,1,0:T(8,128)(2,1)}, u32[]{:S(2)}, u32[]{:S(2)}) collective-permute-start(bf16[32,64,256]{2,1,0:T(8,128)(2,1)} %fusion.28), channel_id=1, source_target_pairs={{0,8},{4,12},{8,16},{12,20},{16,24},{20,28},{1,9},{5,13},{9,17},{1... | collective-permute-start | bytes 3145736 | tf_op jit(solution)/shard_map/ppermute | solution.py:15
  235.6 16.9 %collective-permute-start.1 = (f32[32]{0:T(128)S(1)}, f32[32]{0:T(128)S(1)}, u32[]{:S(2)}, u32[]{:S(2)}) collective-permute-start(f32[32]{0:T(128)S(1)} %copy-done.20), channel_id=1, source_target_pairs={{0,4},{4,8},{8,12},{12,16},{16,20},{20,24},{24,28},{1,5},{5,9},{9,... | collective-permute-start | bytes 392 | tf_op jit(solution)/shard_map/ppermute | solution.py:15
  252.5 9.4 %copy-start.27 = (f32[1,32]{1,0:T(1,128)S(1)}, f32[1,32]{1,0:T(1,128)}, u32[]{:S(2)}) copy-start(f32[1,32]{1,0:T(1,128)} %get-tuple-element.40) | copy-start | bytes 388
  252.5 9.4 %copy-start.28 = (f32[1,32]{1,0:T(1,128)S(1)}, f32[1,32]{1,0:T(1,128)}, u32[]{:S(2)}) copy-start(f32[1,32]{1,0:T(1,128)} %get-tuple-element.42) | copy-start | bytes 388
  252.5 9.4 %copy-start.29 = (f32[1,32]{1,0:T(1,128)S(1)}, f32[1,32]{1,0:T(1,128)}, u32[]{:S(2)}) copy-start(f32[1,32]{1,0:T(1,128)} %get-tuple-element.43) | copy-start | bytes 388
  255.2 29.3 %copy-start.3 = (bf16[4,128,2,16,64]{1,4,3,2,0:T(8,128)(2,1)S(1)}, bf16[4,128,2,16,64]{1,4,3,2,0:T(8,128)(2,1)}, u32[]{:S(2)}) copy-start(bf16[4,128,2,16,64]{1,4,3,2,0:T(8,128)(2,1)} %copy-done.2) | copy-start | bytes 6291460
  255.2 33.9 %collective-permute-start.5 = (bf16[32,64,256]{2,1,0:T(8,128)(2,1)}, bf16[32,64,256]{2,1,0:T(8,128)(2,1)}, u32[]{:S(2)}, u32[]{:S(2)}) collective-permute-start(bf16[32,64,256]{2,1,0:T(8,128)(2,1)} %fusion.17), channel_id=1, source_target_pairs={{0,16},{4,20},{8,24},{12,28},{1,17},{5,21},{9,25},{13,29},{2,18},{... | collective-permute-start | bytes 3145736 | tf_op jit(solution)/shard_map/ppermute | solution.py:15
  262.0 20.9 %collective-permute-start.2 = (f32[32]{0:T(128)S(1)}, f32[32]{0:T(128)S(1)}, u32[]{:S(2)}, u32[]{:S(2)}) collective-permute-start(f32[32]{0:T(128)S(1)} %get-tuple-element.10), channel_id=1, source_target_pairs={{0,8},{4,12},{8,16},{12,20},{16,24},{20,28},{1,9},{5,13},{9,17},{1... | collective-permute-start | bytes 392 | tf_op jit(solution)/shard_map/ppermute | solution.py:15
  311.8 47.4 %copy-start.1 = (bf16[1,512,2048]{2,1,0:T(8,128)(2,1)S(1)}, bf16[1,512,2048]{2,1,0:T(8,128)(2,1)}, u32[]{:S(2)}) copy-start(bf16[1,512,2048]{2,1,0:T(8,128)(2,1)} %param.13) | copy-start | bytes 6291460
  (20 other events, 88.3 us)
Sparse Core Ops, SparseCore 0:
  311.9 47.2 reduce-scatter.1

commit v2 on v1

--- a/solution.py
+++ b/solution.py
@@ -82,14 +82,25 @@
         (matching & (slot_ids[None, :] < slot_ids[:, None])).astype(jnp.int32), axis=1
     )
     offsets = (jnp.arange(owners, dtype=jnp.int32) - myself) % owners
-    chosen = (piece_shift[None, None, :] == offsets[:, None, None]) & (
+    chosen = (piece_shift[None, None, :] == jnp.arange(owners, dtype=jnp.int32)[:, None, None]) & (
         ranking[None, None, :] == jnp.arange(most, dtype=jnp.int32)[None, :, None]
     )
-    send_slot = jnp.sum(chosen.astype(jnp.int32) * slot_ids[None, None, :], axis=2)
-
-    def outgoing(local):
-        pieces = local[0].reshape((slots, piece_rows) + local.shape[2:])
-        return pieces[send_slot]
+    slot_of = jnp.sum(chosen.astype(jnp.int32) * slot_ids[None, None, :], axis=2)
+    send_slots = [slot_of[offsets, rank] for rank in range(most)]
+    source = (myself - piece_shift) % owners
+
+    def routed(local):
+        pieces = local.reshape((slots, piece_rows) + local.shape[1:])
+        result = None
+        for rank in range(most):
+            received = lax.all_to_all(
+                pieces[send_slots[rank]], ("dp", "ctx"), split_axis=0, concat_axis=0, tiled=True
+            )[source]
+            if result is None:
+                result = received
+            else:
+                result = jnp.where((ranking == rank)[:, None, None], received, result)
+        return result.reshape((rows,) + local.shape[1:])
 
     features = token_values.shape[2]
     map_shape = state_maps.shape[2:]
@@ -97,19 +108,8 @@
     joined = jnp.concatenate(
         [token_values[0], state_maps[0].reshape(rows, map_width), step_raw[0]], axis=1
     )
-    incoming = lax.all_to_all(
-        outgoing(joined[None]), ("dp", "ctx"), split_axis=0, concat_axis=0, tiled=True
-    )
-    incoming_z = lax.all_to_all(
-        outgoing(gate_values), ("dp", "ctx"), split_axis=0, concat_axis=0, tiled=True
-    )
-    source = (myself - piece_shift) % owners
-
-    def placed(received):
-        return received[source, ranking].reshape((rows,) + received.shape[3:])
-
-    joined_pack = placed(incoming)
-    z_pack = placed(incoming_z)
+    joined_pack = routed(joined)
+    z_pack = routed(gate_values[0])
     margin = conv_values.shape[0] - 1
     flags = doc_start[0].astype(jnp.bfloat16)
     rim = passed_along(

time: 368 us -> 385 us (1.046)
  local copies, waits for them, and re-layouts: 61.5 us -> 92.8 us
  starting transfers between devices: 82.9 us -> 65.9 us
  other arithmetic: 37.2 us -> 45.2 us
  waiting for transfers between devices: 143 us -> 138 us
    gather x4 -> x14, local copies, waits for them, and re-layouts: 18.4 us -> 58.4 us  [the longest x8 43.7 us: routed(): lax.all_to_all(pieces[send_slots[rank]], ('dp', 'ctx'), split_axis=0, con...]
    ppermute x6, starting transfers between devices: 57.8 us -> 31.3 us  [passed_along(): return lax.ppermute(block, axis, route)]
    convert_element_type x2 -> x0, local copies, waits for them, and re-layouts: 15.4 us -> none  [body(): z_pack.astype(jnp.float32)]
    all_to_all x2 -> x4, waiting for transfers between devices: 75.1 us -> 63.3 us  [routed(): lax.all_to_all(pieces[send_slots[rank]], ('dp', 'ctx'), split_axis=0, con...]
    reduce_scatter x1, waiting for transfers between devices: 47.4 us -> 56.9 us  [body(): lax.psum_scatter(partial_value.astype(jnp.bfloat16), 'head', scatter_dime...]
    all_to_all x2 -> x4, starting transfers between devices: 25.1 us -> 34.5 us  [routed(): lax.all_to_all(pieces[send_slots[rank]], ('dp', 'ctx'), split_axis=0, con...]
  transfers between devices with their start and end apart: 9 -> 11, of which waited for: 4 -> 4; matrix products, arithmetic and copies ran while one was open for 24% -> 33% of each run, Pallas kernels for 0% -> 0%
where the time goes in v2:
time: 385 us; the launch traced here: 383 us
  waiting for transfers between devices  138 us (36%)
  local copies, waits for them, and re-layouts  92.8 us (24%)
  starting transfers between devices  65.9 us (17%)
  other arithmetic  45.2 us (12%)
  matrix products  26.9 us (7%)
  between operations  14 us (4%)
    all_to_all x4, waiting for transfers between devices, routed(): lax.all_to_all(pieces[send_slots[rank]], ('dp', 'ctx'), split_axis=0, con...  63.3 us
    reduce_scatter x1, waiting for transfers between devices, body(): lax.psum_scatter(partial_value.astype(jnp.bfloat16), 'head', scatter_dime...  56.9 us
    gather x8, local copies, waits for them, and re-layouts, routed(): lax.all_to_all(pieces[send_slots[rank]], ('dp', 'ctx'), split_axis=0, con...  43.7 us
    all_to_all x4, starting transfers between devices, routed(): lax.all_to_all(pieces[send_slots[rank]], ('dp', 'ctx'), split_axis=0, con...  34.5 us
    ppermute x6, starting transfers between devices, passed_along(): return lax.ppermute(block, axis, route)  31.3 us
    ppermute x6, waiting for transfers between devices, passed_along(): return lax.ppermute(block, axis, route)  17.5 us
    dot_general x1, matrix products, body(): jnp.dot(normed, out_weight, preferred_element_type=jnp.float32)  14 us
    reshape x2, local copies, waits for them, and re-layouts, body(): x_blocks = x_conv.reshape(blocks, span, groups_local, per_group, width)  13.5 us
  transfers between devices with their start and end apart: 11, of which 4 were waited for; matrix products, arithmetic and copies ran while one was open for 33% of the time, Pallas kernels for 0%

profile of v2, /device:TPU:2, one launch (start us, length us, event | category | flops | bytes accessed | tf_op | source)
XLA Modules:
  0.0 382.6 jit_solution(14377760082834010314)
XLA Ops:
  14.1 4.5 %gather_fusion.4 = bf16[32,16,3104]{2,1,0:T(8,128)(2,1)} fusion(bf16[32,16,3104]{2,1,0:T(8,128)(2,1)} %pad_maximum_fusion, s32[1024]{0:T(1024)S(1)} %pad_clamp_fusion), kind=kCustom, calls=%fused_computation.4 | custom fusion | bytes 6357120 | tf_op jit(solution)/shard_map/gather | solution.py:97
  18.6 8.5 %all-to-all-start.1 = ((bf16[32,16,3104]{2,1,0:T(8,128)(2,1)}), bf16[32,16,3104]{2,1,0:T(8,128)(2,1)}, u32[]{:S(2)}, u32[]{:S(2)}) async-start(bf16[32,16,3104]{2,1,0:T(8,128)(2,1)} %gather_fusion.4), calls=%async_computation.1 | async-start | bytes 6553600 | tf_op jit(solution)/shard_map/all_to_all | solution.py:96
  27.9 4.5 %gather_fusion.1 = bf16[32,16,3104]{2,1,0:T(8,128)(2,1)} fusion(bf16[32,16,3104]{2,1,0:T(8,128)(2,1)} %pad_maximum_fusion, s32[1024]{0:T(1024)S(1)} %pad_clamp_fusion.2), kind=kCustom, calls=%fused_computation.1 | custom fusion | bytes 6357120 | tf_op jit(solution)/shard_map/gather | solution.py:97
  32.4 33.2 %all-to-all-done.1 = bf16[32,16,3104]{2,1,0:T(8,128)(2,1)} async-done(((bf16[32,16,3104]{2,1,0:T(8,128)(2,1)}), bf16[32,16,3104]{2,1,0:T(8,128)(2,1)}, u32[]{:S(2)}, u32[]{:S(2)}) %all-to-all-start.1) | async-done | bytes 3178528 | tf_op jit(solution)/shard_map/all_to_all | solution.py:96
  65.6 7.7 %all-to-all-start = ((bf16[32,16,3104]{2,1,0:T(8,128)(2,1)}), bf16[32,16,3104]{2,1,0:T(8,128)(2,1)}, u32[]{:S(2)}, u32[]{:S(2)}) async-start(bf16[32,16,3104]{2,1,0:T(8,128)(2,1)} %gather_fusion.1), calls=%async_computation | async-start | bytes 6553600 | tf_op jit(solution)/shard_map/all_to_all | solution.py:96
  77.4 4.5 %gather_fusion.5 = bf16[32,16,3104]{2,1,0:T(8,128)(2,1)} fusion(bf16[32,16,3104]{2,1,0:T(8,128)(2,1)} %all-to-all-done.1, s32[1024]{0:T(1024)S(1)} %pad_clamp_fusion.1), kind=kCustom, calls=%fused_computation.5 | custom fusion | bytes 6357120 | tf_op jit(solution)/shard_map/gather | solution.py:96
  81.9 30.1 %all-to-all-done = bf16[32,16,3104]{2,1,0:T(8,128)(2,1)} async-done(((bf16[32,16,3104]{2,1,0:T(8,128)(2,1)}), bf16[32,16,3104]{2,1,0:T(8,128)(2,1)}, u32[]{:S(2)}, u32[]{:S(2)}) %all-to-all-start) | async-done | bytes 3178528 | tf_op jit(solution)/shard_map/all_to_all | solution.py:96
  112.0 7.6 %all-to-all-start.3 = ((bf16[32,16,2048]{2,1,0:T(8,128)(2,1)}), bf16[32,16,2048]{2,1,0:T(8,128)(2,1)}, u32[]{:S(2)}, u32[]{:S(2)}) async-start(bf16[32,16,2048]{2,1,0:T(8,128)(2,1)} %gather_fusion.8), calls=%async_computation.3 | async-start | bytes 4194304 | tf_op jit(solution)/shard_map/all_to_all | solution.py:96
  119.6 4.6 %gather_fusion.2 = bf16[32,16,3104]{2,1,0:T(8,128)(2,1)} fusion(bf16[32,16,3104]{2,1,0:T(8,128)(2,1)} %all-to-all-done, s32[1024]{0:T(1024)S(1)} %pad_clamp_fusion.1), kind=kCustom, calls=%fused_computation.2 | custom fusion | bytes 6357120 | tf_op jit(solution)/shard_map/gather | solution.py:96
  143.1 8.8 %multiply_convert_fusion.3 = bf16[512,2048]{1,0:T(8,128)(2,1)} fusion(bf16[512,2048]{1,0:T(8,128)(2,1)} %slice.182, bf16[3,2048]{1,0:T(4,128)(2,1)S(1)} %slice.185, f32[512]{0:T(512)S(1)} %get-tuple-element.17, f32[2048]{0:T(1024)S(1)} %bitcast.142, f32[512]{0:T(512)S(1)} %get-tuple-element.18, f32[2048]{0:T(1024)S(1)} %bitcast.143, ...), kind=kLoop, calls=%fused_computation.34 | loop fusion | flops 29360128 | bytes 4245504 | tf_op jit(solution)/shard_map/convert_element_type | solution.py:56
  151.9 7.0 %reshape.432 = bf16[4,128,2,16,64]{4,3,2,1,0:T(8,128)(2,1)} reshape(bf16[512,2048]{1,0:T(8,128)(2,1)} %multiply_convert_fusion.3) | data formatting | bytes 4194304 | tf_op jit(solution)/shard_map/reshape | solution.py:141
  159.0 6.5 %copy.92 = bf16[4,128,2,16,64]{1,4,3,2,0:T(8,128)(2,1)} copy(bf16[4,128,2,16,64]{4,3,2,1,0:T(8,128)(2,1)} %reshape.432) | data formatting | bytes 4194304 | tf_op jit(solution)/shard_map/reshape | solution.py:141
  170.1 4.5 %fusion.23 = f32[4,2,16,64,256]{4,3,2,1,0:T(8,128)} fusion(bf16[4,128,2,16,64]{1,4,3,2,0:T(8,128)(2,1)S(1)} %copy-done.4, f32[4,128,2,16]{1,3,2,0:T(8,128)S(1)} %get-tuple-element.29, bf16[4,128,2,256,1]{3,1,0,2,4:T(8,128)(2,1)S(1)} %bitcast.123), kind=kOutput, calls=%fused_computation.51 | convolution fusion | flops 540016640 | bytes 11075584 | tf_op jit(solution)/shard_map/bsghp,bsgn->bghpn/dot_general | solution.py:161
  174.6 7.9 %multiply_add_fusion = (f32[1,2,16,64,256]{4,3,2,1,0:T(8,128)}, f32[1,2,16,64,256]{4,3,2,1,0:T(8,128)}, f32[1,2,16,64,256]{4,3,2,1,0:T(8,128)}, f32[1,2,16,64,25...) fusion(f32[2,16]{1,0:T(2,128)S(1)} %copy-done.34, ...), kind=kLoop, calls=%fused_computation.62 | loop fusion | flops 2621440 | bytes 23069056 | tf_op jit(solution)/shard_map/add | solution.py:169
  192.1 10.7 %all-to-all-start.2 = ((bf16[32,16,2048]{2,1,0:T(8,128)(2,1)}), bf16[32,16,2048]{2,1,0:T(8,128)(2,1)}, u32[]{:S(2)}, u32[]{:S(2)}) async-start(bf16[32,16,2048]{2,1,0:T(8,128)(2,1)} %gather_fusion.6), calls=%async_computation.2 | async-start | bytes 4194304 | tf_op jit(solution)/shard_map/all_to_all | solution.py:96
  204.2 13.4 %collective-permute-start.4 = (bf16[32,64,256]{2,1,0:T(8,128)(2,1)}, bf16[32,64,256]{2,1,0:T(8,128)(2,1)}, u32[]{:S(2)}, u32[]{:S(2)}) collective-permute-start(bf16[32,64,256]{2,1,0:T(8,128)(2,1)} %fusion.31), channel_id=1, source_target_pairs={{0,8},{4,12},{8,16},{12,20},{16,24},{20,28},{1,9},{5,13},{9,17},{1... | collective-permute-start | bytes 3145736 | tf_op jit(solution)/shard_map/ppermute | solution.py:15
  223.6 7.1 %gather.57 = bf16[4,128,2,16,64]{4,3,2,1,0:T(8,128)(2,1)} reshape(bf16[32,16,2048]{2,1,0:T(8,128)(2,1)} %gather_fusion.9) | data formatting | bytes 4194304 | tf_op jit(solution)/shard_map/gather | solution.py:96
  230.7 6.5 %copy.100 = bf16[4,128,2,16,64]{1,4,3,2,0:T(8,128)(2,1)} copy(bf16[4,128,2,16,64]{4,3,2,1,0:T(8,128)(2,1)} %gather.57) | data formatting | bytes 4194304 | tf_op jit(solution)/shard_map/gather | solution.py:96
  242.2 7.1 %gather.54 = bf16[4,128,2,16,64]{4,3,2,1,0:T(8,128)(2,1)} reshape(bf16[32,16,2048]{2,1,0:T(8,128)(2,1)} %gather_fusion.7) | data formatting | bytes 4194304 | tf_op jit(solution)/shard_map/gather | solution.py:96
  249.3 6.5 %copy.99 = bf16[4,128,2,16,64]{1,4,3,2,0:T(8,128)(2,1)} copy(bf16[4,128,2,16,64]{4,3,2,1,0:T(8,128)(2,1)} %gather.54) | data formatting | bytes 4194304 | tf_op jit(solution)/shard_map/gather | solution.py:96
  259.1 9.5 %collective-permute-start.5 = (bf16[32,64,256]{2,1,0:T(8,128)(2,1)}, bf16[32,64,256]{2,1,0:T(8,128)(2,1)}, u32[]{:S(2)}, u32[]{:S(2)}) collective-permute-start(bf16[32,64,256]{2,1,0:T(8,128)(2,1)} %fusion.20), channel_id=1, source_target_pairs={{0,16},{4,20},{8,24},{12,28},{1,17},{5,21},{9,25},{13,29},{2,18},{... | collective-permute-start | bytes 3145736 | tf_op jit(solution)/shard_map/ppermute | solution.py:15
  272.4 17.5 %collective-permute-done.2 = f32[32]{0:T(128)S(1)} collective-permute-done((f32[32]{0:T(128)}, f32[32]{0:T(128)S(1)}, u32[]{:S(2)}, u32[]{:S(2)}) %collective-permute-start.2) | collective-permute-done | bytes 160 | tf_op jit(solution)/shard_map/ppermute | solution.py:15
  304.9 14.0 %convolution_convert_fusion = bf16[512,4096]{1,0:T(8,128)(2,1)} fusion(bf16[2048,4096]{1,0:T(8,128)(2,1)} %param.23, bf16[256,8,4,128]{3,2,1,0:T(4,128)(2,1)S(1)} %bitcast.131), kind=kOutput, calls=%fused_computation.13 | convolution fusion | flops 8592031744 | bytes 23068672 | tf_op jit(solution)/shard_map/dot_general | solution.py:199
  318.9 56.9 %reduce-scatter.2.cloned.1.call-done = bf16[512,1024]{1,0:T(8,128)(2,1)} async-done(((bf16[512,4096]{1,0:T(8,128)(2,1)}), bf16[512,1024]{1,0:T(8,128)(2,1)}) %reduce-scatter.2.cloned.1.call-update) | async-done | bytes 1048592 | tf_op jit(solution)/shard_map/reduce_scatter | solution.py:200
  (186 shorter events, 79.7 us)
Async XLA Ops:
  6.5 67.4 %copy-start = (bf16[1,512,2048]{2,1,0:T(8,128)(2,1)S(1)}, bf16[1,512,2048]{2,1,0:T(8,128)(2,1)}, u32[]{:S(2)}) copy-start(bf16[1,512,2048]{2,1,0:T(8,128)(2,1)} %param.13) | copy-start | bytes 6291460
  18.6 47.1 %all-to-all-start.1 = ((bf16[32,16,3104]{2,1,0:T(8,128)(2,1)}), bf16[32,16,3104]{2,1,0:T(8,128)(2,1)}, u32[]{:S(2)}, u32[]{:S(2)}) async-start(bf16[32,16,3104]{2,1,0:T(8,128)(2,1)} %gather_fusion.4), calls=%async_computation.1 | async-start | bytes 6553600 | tf_op jit(solution)/shard_map/all_to_all | solution.py:96
  32.4 41.1 %copy-start.17 = (s32[1,512]{1,0:T(1,128)S(1)}, s32[1,512]{1,0:T(1,128)}, u32[]{:S(2)}) copy-start(s32[1,512]{1,0:T(1,128)} %param.21) | copy-start | bytes 6148
  65.6 46.3 %all-to-all-start = ((bf16[32,16,3104]{2,1,0:T(8,128)(2,1)}), bf16[32,16,3104]{2,1,0:T(8,128)(2,1)}, u32[]{:S(2)}, u32[]{:S(2)}) async-start(bf16[32,16,3104]{2,1,0:T(8,128)(2,1)} %gather_fusion.1), calls=%async_computation | async-start | bytes 6553600 | tf_op jit(solution)/shard_map/all_to_all | solution.py:96
  76.5 43.1 %copy-start.19 = (s32[1024]{0:T(1024)}, s32[1024]{0:T(1024)S(1)}, u32[]{:S(2)}) copy-start(s32[1024]{0:T(1024)S(1)} %pad_clamp_fusion.1) | copy-start | bytes 12292
  112.0 80.2 %all-to-all-start.3 = ((bf16[32,16,2048]{2,1,0:T(8,128)(2,1)}), bf16[32,16,2048]{2,1,0:T(8,128)(2,1)}, u32[]{:S(2)}, u32[]{:S(2)}) async-start(bf16[32,16,2048]{2,1,0:T(8,128)(2,1)} %gather_fusion.8), calls=%async_computation.3 | async-start | bytes 4194304 | tf_op jit(solution)/shard_map/all_to_all | solution.py:96
  127.6 13.1 %collective-permute-start = (bf16[3,3105]{1,0:T(4,128)(2,1)S(1)}, bf16[3,3105]{1,0:T(4,128)(2,1)}, u32[]{:S(2)}, u32[]{:S(2)}) collective-permute-start(bf16[3,3105]{1,0:T(4,128)(2,1)S(1)} %pad_maximum_fusion.3), channel_id=1, source_target_pairs={{0,4},{4,8},{8,12},{12,16},{16,20},{20,24},{24,28},{1,5},{5,9},{9,... | collective-permute-start | bytes 55898 | tf_op jit(solution)/shard_map/ppermute | solution.py:15
  186.6 16.2 %collective-permute-start.3 = (bf16[32,64,256]{2,1,0:T(8,128)(2,1)}, bf16[32,64,256]{2,1,0:T(8,128)(2,1)S(1)}, u32[]{:S(2)}, u32[]{:S(2)}) collective-permute-start(bf16[32,64,256]{2,1,0:T(8,128)(2,1)} %get-tuple-element.12), channel_id=1, source_target_pairs={{0,4},{4,8},{8,12},{12,16},{16,20},{20,24},{24,28},{1,5},{5,9},{9,... | collective-permute-start | bytes 3145736 | tf_op jit(solution)/shard_map/ppermute | solution.py:15
  192.1 10.8 %copy-start.2 = (f32[32,64,256]{2,1,0:T(8,128)S(1)}, f32[32,64,256]{2,1,0:T(8,128)}, u32[]{:S(2)}) copy-start(f32[32,64,256]{2,1,0:T(8,128)} %get-tuple-element.13) | copy-start | bytes 6291460
  192.1 10.8 %copy-start.20 = (f32[32]{0:T(128)S(1)}, f32[32]{0:T(128)}, u32[]{:S(2)}) copy-start(f32[32]{0:T(128)} %get-tuple-element.49) | copy-start | bytes 388
  192.1 45.0 %all-to-all-start.2 = ((bf16[32,16,2048]{2,1,0:T(8,128)(2,1)}), bf16[32,16,2048]{2,1,0:T(8,128)(2,1)}, u32[]{:S(2)}, u32[]{:S(2)}) async-start(bf16[32,16,2048]{2,1,0:T(8,128)(2,1)} %gather_fusion.6), calls=%async_computation.2 | async-start | bytes 4194304 | tf_op jit(solution)/shard_map/all_to_all | solution.py:96
  202.8 172.9 %reduce-scatter.2.cloned.1.call-start = ((), (), s32[]{:S(2)}) async-start(), calls=%async_computation.5 | async-start | bytes 5242880 | tf_op jit(solution)/shard_map/reduce_scatter | solution.py:200
  202.9 14.7 %copy-start.37 = (pred[32]{0:T(512)(128)(4,1)S(1)}, pred[32]{0:T(512)(128)(4,1)}, u32[]{:S(2)}) copy-start(pred[32]{0:T(512)(128)(4,1)} %copy-done.36) | copy-start | bytes 100
  202.9 15.5 %copy-start.40 = (f32[32]{0:T(128)S(1)}, f32[32]{0:T(128)}, u32[]{:S(2)}) copy-start(f32[32]{0:T(128)} %param.17) | copy-start | bytes 388
  202.9 16.7 %copy-start.21 = (f32[2048]{0:T(1024)S(1)}, f32[2048]{0:T(1024)}, u32[]{:S(2)}) copy-start(f32[2048]{0:T(1024)} %param.22) | copy-start | bytes 24580
  204.2 52.1 %collective-permute-start.4 = (bf16[32,64,256]{2,1,0:T(8,128)(2,1)}, bf16[32,64,256]{2,1,0:T(8,128)(2,1)}, u32[]{:S(2)}, u32[]{:S(2)}) collective-permute-start(bf16[32,64,256]{2,1,0:T(8,128)(2,1)} %fusion.31), channel_id=1, source_target_pairs={{0,8},{4,12},{8,16},{12,20},{16,24},{20,28},{1,9},{5,13},{9,17},{1... | collective-permute-start | bytes 3145736 | tf_op jit(solution)/shard_map/ppermute | solution.py:15
  240.9 14.9 %collective-permute-start.1 = (f32[32]{0:T(128)S(1)}, f32[32]{0:T(128)S(1)}, u32[]{:S(2)}, u32[]{:S(2)}) collective-permute-start(f32[32]{0:T(128)S(1)} %copy-done.20), channel_id=1, source_target_pairs={{0,4},{4,8},{8,12},{12,16},{16,20},{20,24},{24,28},{1,5},{5,9},{9,... | collective-permute-start | bytes 392 | tf_op jit(solution)/shard_map/ppermute | solution.py:15
  256.3 12.2 %copy-start.29 = (f32[1,32]{1,0:T(1,128)S(1)}, f32[1,32]{1,0:T(1,128)}, u32[]{:S(2)}) copy-start(f32[1,32]{1,0:T(1,128)} %get-tuple-element.40) | copy-start | bytes 388
  256.3 12.2 %copy-start.30 = (f32[1,32]{1,0:T(1,128)S(1)}, f32[1,32]{1,0:T(1,128)}, u32[]{:S(2)}) copy-start(f32[1,32]{1,0:T(1,128)} %get-tuple-element.42) | copy-start | bytes 388
  256.3 12.2 %copy-start.31 = (f32[1,32]{1,0:T(1,128)S(1)}, f32[1,32]{1,0:T(1,128)}, u32[]{:S(2)}) copy-start(f32[1,32]{1,0:T(1,128)} %get-tuple-element.43) | copy-start | bytes 388
  259.1 33.0 %copy-start.5 = (bf16[4,128,2,16,64]{1,4,3,2,0:T(8,128)(2,1)S(1)}, bf16[4,128,2,16,64]{1,4,3,2,0:T(8,128)(2,1)}, u32[]{:S(2)}) copy-start(bf16[4,128,2,16,64]{1,4,3,2,0:T(8,128)(2,1)} %copy.92) | copy-start | bytes 6291460
  259.1 36.8 %collective-permute-start.5 = (bf16[32,64,256]{2,1,0:T(8,128)(2,1)}, bf16[32,64,256]{2,1,0:T(8,128)(2,1)}, u32[]{:S(2)}, u32[]{:S(2)}) collective-permute-start(bf16[32,64,256]{2,1,0:T(8,128)(2,1)} %fusion.20), channel_id=1, source_target_pairs={{0,16},{4,20},{8,24},{12,28},{1,17},{5,21},{9,25},{13,29},{2,18},{... | collective-permute-start | bytes 3145736 | tf_op jit(solution)/shard_map/ppermute | solution.py:15
  269.3 20.6 %collective-permute-start.2 = (f32[32]{0:T(128)}, f32[32]{0:T(128)S(1)}, u32[]{:S(2)}, u32[]{:S(2)}) collective-permute-start(f32[32]{0:T(128)} %copy-done.24), channel_id=1, source_target_pairs={{0,8},{4,12},{8,16},{12,20},{16,24},{20,28},{1,9},{5,13},{9,17},{1... | collective-permute-start | bytes 392 | tf_op jit(solution)/shard_map/ppermute | solution.py:15
  318.8 56.9 %copy-start.1 = (bf16[1,512,2048]{2,1,0:T(8,128)(2,1)S(1)}, bf16[1,512,2048]{2,1,0:T(8,128)(2,1)}, u32[]{:S(2)}) copy-start(bf16[1,512,2048]{2,1,0:T(8,128)(2,1)} %param.13) | copy-start | bytes 6291460
  (31 other events, 129.2 us)
Sparse Core Ops, SparseCore 0:
  319.0 56.6 reduce-scatter.1

commit v3 on v1

--- a/solution.py
+++ b/solution.py
@@ -39,6 +39,28 @@
         if distance < lax.axis_size(axis):
             window = join(received, window)
     return before[1]
+
+
+def ring_scatter(partial_value, axis):
+    count = lax.axis_size(axis)
+    place = lax.axis_index(axis)
+    rows, total = partial_value.shape
+    half = rows // 2
+    by_block = partial_value.reshape(rows, count, total // count)
+
+    def block(lo, index):
+        return lax.dynamic_index_in_dim(by_block[lo : lo + half], index % count, 1, False)
+
+    upward = [(i, (i + 1) % count) for i in range(count)]
+    downward = [(i, (i - 1) % count) for i in range(count)]
+    rising = block(0, place - 1)
+    falling = block(half, place + 1)
+    for step in range(1, count):
+        rising = lax.ppermute(rising.astype(jnp.bfloat16), axis, upward)
+        falling = lax.ppermute(falling.astype(jnp.bfloat16), axis, downward)
+        rising = rising.astype(jnp.float32) + block(0, place - step - 1)
+        falling = falling.astype(jnp.float32) + block(half, place + step + 1)
+    return jnp.concatenate([rising, falling], axis=0).astype(jnp.bfloat16)
 
 
 def conv_core(ext_values, weight, free_ext, length):
@@ -197,9 +219,7 @@
         .reshape(rows, heads_local * width)
     )
     partial_value = jnp.dot(normed, out_weight, preferred_element_type=jnp.float32)
-    result = lax.psum_scatter(
-        partial_value.astype(jnp.bfloat16), "head", scatter_dimension=1, tiled=True
-    )
+    result = ring_scatter(partial_value, "head")
     return result[None]
 
 

time: 368 us -> 373 us (1.014)
  local copies, waits for them, and re-layouts: 61.5 us -> 95.3 us
  waiting for transfers between devices: 143 us -> 114 us
  between operations: 13.9 us -> 0.85 us
  starting transfers between devices: 82.9 us -> 93.4 us
    reduce_scatter x1 -> x0, waiting for transfers between devices: 47.4 us -> none  [body(): lax.psum_scatter(partial_value.astype(jnp.bfloat16), 'head', scatter_dime...]
    ppermute x0 -> x6, waiting for transfers between devices: none -> 18.2 us  [the longest x3 18.2 us: ring_scatter(): rising = lax.ppermute(rising.astype(jnp.bfloat16), axis, upward)]
    dynamic_slice x0 -> x4, local copies, waits for them, and re-layouts: none -> 17.7 us  [block(): lax.dynamic_index_in_dim(by_block[lo:lo + half], index % count, 1, False)]
    slice x0 -> x3, local copies, waits for them, and re-layouts: none -> 16 us  [block(): by_block[lo:lo + half]]
    ppermute x0 -> x6, starting transfers between devices: none -> 10.3 us  [the longest x3 7.77 us: ring_scatter(): falling = lax.ppermute(falling.astype(jnp.bfloat16), axis, downward)]
  transfers between devices with their start and end apart: 9 -> 14, of which waited for: 4 -> 5; matrix products, arithmetic and copies ran while one was open for 24% -> 30% of each run, Pallas kernels for 0% -> 0%
where the time goes in v3:
time: 373 us; the launch traced here: 369 us
  waiting for transfers between devices  114 us (31%)
  local copies, waits for them, and re-layouts  95.3 us (26%)
  starting transfers between devices  93.4 us (25%)
  other arithmetic  40.1 us (11%)
  matrix products  25.2 us (7%)
    all_to_all x1, waiting for transfers between devices, body(): lax.all_to_all(outgoing(joined[None]), ('dp', 'ctx'), split_axis=0, conca...  75.2 us
    ppermute x6, starting transfers between devices, passed_along(): return lax.ppermute(block, axis, route)  58 us
    ppermute x6, waiting for transfers between devices, passed_along(): return lax.ppermute(block, axis, route)  20.7 us
    ppermute x3, waiting for transfers between devices, ring_scatter(): rising = lax.ppermute(rising.astype(jnp.bfloat16), axis, upward)  18.2 us
    dynamic_slice x4, local copies, waits for them, and re-layouts, block(): lax.dynamic_index_in_dim(by_block[lo:lo + half], index % count, 1, False)  17.7 us
    all_to_all x1, starting transfers between devices, body(): lax.all_to_all(outgoing(gate_values), ('dp', 'ctx'), split_axis=0, concat...  16.5 us
    slice x3, local copies, waits for them, and re-layouts, block(): by_block[lo:lo + half]  16 us
    convert_element_type x2, local copies, waits for them, and re-layouts, body(): z_pack.astype(jnp.float32)  15.4 us
  transfers between devices with their start and end apart: 14, of which 5 were waited for; matrix products, arithmetic and copies ran while one was open for 30% of the time, Pallas kernels for 0%

profile of v3, /device:TPU:2, one launch (start us, length us, event | category | flops | bytes accessed | tf_op | source)
XLA Modules:
  0.0 369.0 jit_solution(15702349896586279465)
XLA Ops:
  7.1 5.9 %gather_fusion = bf16[64,16,3104]{2,1,0:T(8,128)(2,1)} fusion(bf16[32,16,3104]{2,1,0:T(8,128)(2,1)} %pad_maximum_fusion, s32[1024]{0:T(1024)S(1)} %pad_clamp_fusion), kind=kCustom, calls=%fused_computation | custom fusion | bytes 12714240 | tf_op jit(solution)/shard_map/gather | solution.py:114
  13.0 8.6 %all-to-all-start = ((bf16[32,2,16,3104]{3,2,1,0:T(8,128)(2,1)}), bf16[32,2,16,3104]{3,2,1,0:T(8,128)(2,1)}, u32[]{:S(2)}, u32[]{:S(2)}) async-start(bf16[32,2,16,3104]{3,2,1,0:T(8,128)(2,1)} %bitcast.161), calls=%async_computation | async-start | bytes 13107200 | tf_op jit(solution)/shard_map/all_to_all | solution.py:122
  26.1 75.2 %all-to-all-done = bf16[32,2,16,3104]{3,2,1,0:T(8,128)(2,1)} async-done(((bf16[32,2,16,3104]{3,2,1,0:T(8,128)(2,1)}), bf16[32,2,16,3104]{3,2,1,0:T(8,128)(2,1)}, u32[]{:S(2)}, u32[]{:S(2)}) %all-to-all-start) | async-done | bytes 6357024 | tf_op jit(solution)/shard_map/all_to_all | solution.py:122
  101.3 16.5 %all-to-all-start.1 = ((bf16[32,2,16,2048]{3,2,1,0:T(8,128)(2,1)}), bf16[32,2,16,2048]{3,2,1,0:T(8,128)(2,1)}, u32[]{:S(2)}, u32[]{:S(2)}) async-start(bf16[32,2,16,2048]{3,2,1,0:T(8,128)(2,1)} %bitcast.162), calls=%async_computation.1 | async-start | bytes 8388608 | tf_op jit(solution)/shard_map/all_to_all | solution.py:125
  117.8 5.5 %gather_fusion.1 = bf16[32,16,3104]{2,1,0:T(8,128)(2,1)} fusion(bf16[32,2,16,3104]{3,2,1,0:T(8,128)(2,1)} %all-to-all-done, s32[32]{0:T(128)S(1)} %fusion.66), kind=kCustom, calls=%fused_computation.1 | custom fusion | bytes 6357248 | tf_op jit(solution)/shard_map/gather | solution.py:131
  136.6 7.7 %multiply_convert_fusion.3 = bf16[512,2048]{1,0:T(8,128)(2,1)S(1)} fusion(bf16[512,2048]{1,0:T(8,128)(2,1)} %slice.192, bf16[3,2048]{1,0:T(4,128)(2,1)S(1)} %slice.195, f32[512]{0:T(512)S(1)} %get-tuple-element.17, f32[2048]{0:T(1024)S(1)} %bitcast.189, f32[512]{0:T(512)S(1)} %get-tuple-element.18, f32[2048]{0:T(1024)S(1)} %bitcast.190, ...), kind=kLoop, calls=%fused_computation.22 | loop fusion | flops 29360128 | bytes 4245504 | tf_op jit(solution)/shard_map/convert_element_type | solution.py:78
  144.3 5.3 %reshape.382 = bf16[4,128,2,16,64]{4,3,2,1,0:T(8,128)(2,1)} reshape(bf16[512,2048]{1,0:T(8,128)(2,1)S(1)} %multiply_convert_fusion.3) | data formatting | bytes 4194304 | tf_op jit(solution)/shard_map/reshape | solution.py:163
  149.7 5.6 %copy.78 = bf16[4,128,2,16,64]{1,4,3,2,0:T(8,128)(2,1)S(1)} copy(bf16[4,128,2,16,64]{4,3,2,1,0:T(8,128)(2,1)} %reshape.382) | data formatting | bytes 4194304 | tf_op jit(solution)/shard_map/reshape | solution.py:163
  159.4 4.5 %fusion.20 = f32[4,2,16,64,256]{4,3,2,1,0:T(8,128)} fusion(bf16[4,128,2,16,64]{1,4,3,2,0:T(8,128)(2,1)S(1)} %copy.78, f32[4,128,2,16]{1,3,2,0:T(8,128)S(1)} %get-tuple-element.37, bf16[4,128,2,256,1]{3,1,0,2,4:T(8,128)(2,1)S(1)} %bitcast.167), kind=kOutput, calls=%fused_computation.38 | convolution fusion | flops 540016640 | bytes 11075584 | tf_op jit(solution)/shard_map/bsghp,bsgn->bghpn/dot_general | solution.py:183
  163.9 7.9 %multiply_add_fusion = (f32[1,2,16,64,256]{4,3,2,1,0:T(8,128)}, f32[1,2,16,64,256]{4,3,2,1,0:T(8,128)}, f32[1,2,16,64,256]{4,3,2,1,0:T(8,128)}, f32[1,2,16,64,25...) fusion(f32[2,16]{1,0:T(2,128)S(1)} %copy-done.33, ...), kind=kLoop, calls=%fused_computation.50 | loop fusion | flops 2621440 | bytes 23069056 | tf_op jit(solution)/shard_map/add | solution.py:191
  174.2 28.8 %collective-permute-start.3 = (bf16[32,64,256]{2,1,0:T(8,128)(2,1)S(1)}, bf16[32,64,256]{2,1,0:T(8,128)(2,1)S(1)}, u32[]{:S(2)}, u32[]{:S(2)}) collective-permute-start(bf16[32,64,256]{2,1,0:T(8,128)(2,1)S(1)} %get-tuple-element.12), channel_id=1, source_target_pairs={{0,4},{4,8},{8,12},{12,16},{16,20},{20,24},{24,28},{1,5},{5,9},{9,... | collective-permute-start | bytes 3145736 | tf_op jit(solution)/shard_map/ppermute | solution.py:15
  206.5 17.3 %collective-permute-start.4 = (bf16[32,64,256]{2,1,0:T(8,128)(2,1)}, bf16[32,64,256]{2,1,0:T(8,128)(2,1)}, u32[]{:S(2)}, u32[]{:S(2)}) collective-permute-start(bf16[32,64,256]{2,1,0:T(8,128)(2,1)} %fusion.29), channel_id=1, source_target_pairs={{0,8},{4,12},{8,16},{12,20},{16,24},{20,28},{1,9},{5,13},{9,17},{1... | collective-permute-start | bytes 3145736 | tf_op jit(solution)/shard_map/ppermute | solution.py:15
  224.8 4.2 %gather_fusion.3 = bf16[32,16,2048]{2,1,0:T(8,128)(2,1)} fusion(bf16[32,2,16,2048]{3,2,1,0:T(8,128)(2,1)} %all-to-all-done.1, s32[32]{0:T(128)S(1)} %fusion.66), kind=kCustom, calls=%fused_computation.3 | custom fusion | bytes 4194560 | tf_op jit(solution)/shard_map/gather | solution.py:131
  230.7 7.4 %reshape.344 = f32[4,128,2,16,64]{4,3,2,1,0:T(8,128)} reshape(bf16[32,16,2048]{2,1,0:T(8,128)(2,1)} %gather_fusion.3) | data formatting | bytes 6291456 | tf_op jit(solution)/shard_map/convert_element_type | solution.py:213
  238.1 8.0 %copy.86 = f32[4,128,2,16,64]{1,4,3,2,0:T(8,128)} copy(f32[4,128,2,16,64]{4,3,2,1,0:T(8,128)} %reshape.344) | data formatting | bytes 8388608 | tf_op jit(solution)/shard_map/convert_element_type | solution.py:213
  248.8 6.5 %collective-permute-start.5 = (bf16[32,64,256]{2,1,0:T(8,128)(2,1)}, bf16[32,64,256]{2,1,0:T(8,128)(2,1)}, u32[]{:S(2)}, u32[]{:S(2)}) collective-permute-start(bf16[32,64,256]{2,1,0:T(8,128)(2,1)} %fusion.17), channel_id=1, source_target_pairs={{0,16},{4,20},{8,24},{12,28},{1,17},{5,21},{9,25},{13,29},{2,18},{... | collective-permute-start | bytes 3145736 | tf_op jit(solution)/shard_map/ppermute | solution.py:15
  258.2 18.5 %collective-permute-done.2 = f32[32]{0:T(128)S(1)} collective-permute-done((f32[32]{0:T(128)S(1)}, f32[32]{0:T(128)S(1)}, u32[]{:S(2)}, u32[]{:S(2)}) %collective-permute-start.2) | collective-permute-done | bytes 160 | tf_op jit(solution)/shard_map/ppermute | solution.py:15
  278.2 4.5 %fusion.1 = f32[4,2,16,64,128]{4,3,2,1,0:T(8,128)S(1)} fusion(bf16[4,128,2,16,64]{1,4,3,2,0:T(8,128)(2,1)S(1)} %copy-done.4, f32[4,2,16,128]{3,2,1,0:T(8,128)S(1)} %bitcast.185, f32[4,2,128,128]{3,2,1,0:T(8,128)S(1)} %fusion.46, f32[4,2,16,128]{3,2,1,0:T(8,128)S(1)} %bitcast.184, pred[4,128,128]{2,1,0:T(8,128)(4,1)} %compare_and_fusion), kind=kOutput, calls=%fused_computation.9 | convolution fusion | flops 278921216 | bytes 7012352 | tf_op jit(solution)/shard_map/bghts,bsghp->btghp/dot_general | solution.py:176
  291.5 11.7 %fusion.22 = f32[512,4096]{1,0:T(8,128)S(1)} fusion(bf16[2048,4096]{1,0:T(8,128)(2,1)} %param.23, bf16[256,8,4,128]{3,2,1,0:T(4,128)(2,1)S(1)} %bitcast.176), kind=kOutput, calls=%fused_computation.39 | convolution fusion | flops 8589934592 | bytes 27262976 | tf_op jit(solution)/shard_map/dot_general | solution.py:221
  306.9 6.1 %slice.181 = f32[256,4,1024]{2,1,0:T(4,128)} reshape(f32[256,4096]{1,0:T(8,128)} %get-tuple-element.19) | data formatting | bytes 8388608 | tf_op jit(solution)/shard_map/slice | solution.py:52
  318.3 6.0 %slice.183 = f32[256,4,1024]{2,1,0:T(4,128)} reshape(f32[256,4096]{1,0:T(8,128)} %get-tuple-element.20) | data formatting | bytes 8388608 | tf_op jit(solution)/shard_map/slice | solution.py:52
  329.5 8.0 %constant_dynamic-slice_fusion.6 = (f32[256,1,1024]{2,1,0:T(1,128)S(1)}, f32[256,1,1024]{2,1,0:T(1,128)S(1)}, f32[256,1,1024]{2,1,0:T(1,128)S(1)}) fusion(f32[256,4,1024]{2,1,0:T(4,128)} %slice.181, s32[]{:T(128)S(6)} %select_n.137, s32[]{:T(128)S(6)} %select_n.141, s32[]{:T(128)S(6)} %select_n.139), kind=kLoop, calls=%fused_computation.129 | loop fusion | bytes 6291468 | tf_op jit(solution)/shard_map/jit(dynamic_index_in_dim)/dynamic_slice | solution.py:52
  344.8 9.5 %collective-permute-done.7 = bf16[256,1024]{1,0:T(8,128)(2,1)S(1)} collective-permute-done((bf16[256,1024]{1,0:T(8,128)(2,1)S(1)}, bf16[256,1024]{1,0:T(8,128)(2,1)S(1)}, u32[]{:S(2)}, u32[]{:S(2)}) %collective-permute-start.7) | collective-permute-done | bytes 524320 | tf_op jit(solution)/shard_map/ppermute | solution.py:59
  358.4 8.7 %collective-permute-done.8 = bf16[256,1024]{1,0:T(8,128)(2,1)S(1)} collective-permute-done((bf16[256,1024]{1,0:T(8,128)(2,1)S(1)}, bf16[256,1024]{1,0:T(8,128)(2,1)S(1)}, u32[]{:S(2)}, u32[]{:S(2)}) %collective-permute-start.8) | collective-permute-done | bytes 524320 | tf_op jit(solution)/shard_map/ppermute | solution.py:59
  (176 shorter events, 80.2 us)
Async XLA Ops:
  0.0 21.9 %copy-start = (bf16[1,512,2048]{2,1,0:T(8,128)(2,1)S(1)}, bf16[1,512,2048]{2,1,0:T(8,128)(2,1)}, u32[]{:S(2)}) copy-start(bf16[1,512,2048]{2,1,0:T(8,128)(2,1)} %param.13) | copy-start | bytes 6291460
  13.0 8.7 %copy-start.15 = (s32[1,512]{1,0:T(1,128)S(1)}, s32[1,512]{1,0:T(1,128)}, u32[]{:S(2)}) copy-start(s32[1,512]{1,0:T(1,128)} %param.21) | copy-start | bytes 6148
  13.0 88.3 %all-to-all-start = ((bf16[32,2,16,3104]{3,2,1,0:T(8,128)(2,1)}), bf16[32,2,16,3104]{3,2,1,0:T(8,128)(2,1)}, u32[]{:S(2)}, u32[]{:S(2)}) async-start(bf16[32,2,16,3104]{3,2,1,0:T(8,128)(2,1)} %bitcast.161), calls=%async_computation | async-start | bytes 13107200 | tf_op jit(solution)/shard_map/all_to_all | solution.py:122
  101.3 123.5 %all-to-all-start.1 = ((bf16[32,2,16,2048]{3,2,1,0:T(8,128)(2,1)}), bf16[32,2,16,2048]{3,2,1,0:T(8,128)(2,1)}, u32[]{:S(2)}, u32[]{:S(2)}) async-start(bf16[32,2,16,2048]{3,2,1,0:T(8,128)(2,1)} %bitcast.162), calls=%async_computation.1 | async-start | bytes 8388608 | tf_op jit(solution)/shard_map/all_to_all | solution.py:125
  124.1 12.2 %collective-permute-start = (bf16[3,3105]{1,0:T(4,128)(2,1)S(1)}, bf16[3,3105]{1,0:T(4,128)(2,1)S(1)}, u32[]{:S(2)}, u32[]{:S(2)}) collective-permute-start(bf16[3,3105]{1,0:T(4,128)(2,1)S(1)} %pad_maximum_fusion.4), channel_id=1, source_target_pairs={{0,4},{4,8},{8,12},{12,16},{16,20},{20,24},{24,28},{1,5},{5,9},{9,... | collective-permute-start | bytes 55898 | tf_op jit(solution)/shard_map/ppermute | solution.py:15
  171.8 33.4 %copy-start.21 = (f32[32]{0:T(128)S(1)}, f32[32]{0:T(128)}, u32[]{:S(2)}) copy-start(f32[32]{0:T(128)} %get-tuple-element.57) | copy-start | bytes 388
  174.2 31.0 %collective-permute-start.3 = (bf16[32,64,256]{2,1,0:T(8,128)(2,1)S(1)}, bf16[32,64,256]{2,1,0:T(8,128)(2,1)S(1)}, u32[]{:S(2)}, u32[]{:S(2)}) collective-permute-start(bf16[32,64,256]{2,1,0:T(8,128)(2,1)S(1)} %get-tuple-element.12), channel_id=1, source_target_pairs={{0,4},{4,8},{8,12},{12,16},{16,20},{20,24},{24,28},{1,5},{5,9},{9,... | collective-permute-start | bytes 3145736 | tf_op jit(solution)/shard_map/ppermute | solution.py:15
  205.2 18.6 %copy-start.35 = (f32[32]{0:T(128)S(1)}, f32[32]{0:T(128)}, u32[]{:S(2)}) copy-start(f32[32]{0:T(128)} %param.17) | copy-start | bytes 388
  205.2 18.7 %copy-start.22 = (f32[2048]{0:T(1024)S(1)}, f32[2048]{0:T(1024)}, u32[]{:S(2)}) copy-start(f32[2048]{0:T(1024)} %param.22) | copy-start | bytes 24580
  206.5 39.6 %collective-permute-start.4 = (bf16[32,64,256]{2,1,0:T(8,128)(2,1)}, bf16[32,64,256]{2,1,0:T(8,128)(2,1)}, u32[]{:S(2)}, u32[]{:S(2)}) collective-permute-start(bf16[32,64,256]{2,1,0:T(8,128)(2,1)} %fusion.29), channel_id=1, source_target_pairs={{0,8},{4,12},{8,16},{12,20},{16,24},{20,28},{1,9},{5,13},{9,17},{1... | collective-permute-start | bytes 3145736 | tf_op jit(solution)/shard_map/ppermute | solution.py:15
  229.0 17.1 %collective-permute-start.1 = (f32[32]{0:T(128)S(1)}, f32[32]{0:T(128)S(1)}, u32[]{:S(2)}, u32[]{:S(2)}) collective-permute-start(f32[32]{0:T(128)S(1)} %copy-done.21), channel_id=1, source_target_pairs={{0,4},{4,8},{8,12},{12,16},{16,20},{20,24},{24,28},{1,5},{5,9},{9,... | collective-permute-start | bytes 392 | tf_op jit(solution)/shard_map/ppermute | solution.py:15
  246.1 9.2 %copy-start.28 = (f32[1,32]{1,0:T(1,128)S(1)}, f32[1,32]{1,0:T(1,128)}, u32[]{:S(2)}) copy-start(f32[1,32]{1,0:T(1,128)} %get-tuple-element.48) | copy-start | bytes 388
  246.1 9.2 %copy-start.29 = (f32[1,32]{1,0:T(1,128)S(1)}, f32[1,32]{1,0:T(1,128)}, u32[]{:S(2)}) copy-start(f32[1,32]{1,0:T(1,128)} %get-tuple-element.50) | copy-start | bytes 388
  246.1 9.2 %copy-start.30 = (f32[1,32]{1,0:T(1,128)S(1)}, f32[1,32]{1,0:T(1,128)}, u32[]{:S(2)}) copy-start(f32[1,32]{1,0:T(1,128)} %get-tuple-element.51) | copy-start | bytes 388
  248.8 29.4 %copy-start.4 = (bf16[4,128,2,16,64]{1,4,3,2,0:T(8,128)(2,1)S(1)}, bf16[4,128,2,16,64]{1,4,3,2,0:T(8,128)(2,1)}, u32[]{:S(2)}) copy-start(bf16[4,128,2,16,64]{1,4,3,2,0:T(8,128)(2,1)} %copy-done.3) | copy-start | bytes 6291460
  248.8 34.0 %collective-permute-start.5 = (bf16[32,64,256]{2,1,0:T(8,128)(2,1)}, bf16[32,64,256]{2,1,0:T(8,128)(2,1)}, u32[]{:S(2)}, u32[]{:S(2)}) collective-permute-start(bf16[32,64,256]{2,1,0:T(8,128)(2,1)} %fusion.17), channel_id=1, source_target_pairs={{0,16},{4,20},{8,24},{12,28},{1,17},{5,21},{9,25},{13,29},{2,18},{... | collective-permute-start | bytes 3145736 | tf_op jit(solution)/shard_map/ppermute | solution.py:15
  255.5 21.2 %collective-permute-start.2 = (f32[32]{0:T(128)S(1)}, f32[32]{0:T(128)S(1)}, u32[]{:S(2)}, u32[]{:S(2)}) collective-permute-start(f32[32]{0:T(128)S(1)} %get-tuple-element.10), channel_id=1, source_target_pairs={{0,8},{4,12},{8,16},{12,20},{16,24},{20,28},{1,9},{5,13},{9,17},{1... | collective-permute-start | bytes 392 | tf_op jit(solution)/shard_map/ppermute | solution.py:15
  316.5 24.3 %collective-permute-start.6 = (bf16[256,1024]{1,0:T(8,128)(2,1)S(1)}, bf16[256,1024]{1,0:T(8,128)(2,1)S(1)}, u32[]{:S(2)}, u32[]{:S(2)}) collective-permute-start(bf16[256,1024]{1,0:T(8,128)(2,1)S(1)} %bitcast.180), channel_id=1, source_target_pairs={{0,1},{1,2},{2,3},{3,0},{4,5},{5,6},{6,7},{7,4},{8,9},{9,10},{10,1... | collective-permute-start | bytes 1572872 | tf_op jit(solution)/shard_map/ppermute | solution.py:59
  327.8 9.7 %copy-start.2 = (f32[256,4,1024]{2,1,0:T(4,128)S(1)}, f32[256,4,1024]{2,1,0:T(4,128)}, u32[]{:S(2)}) copy-start(f32[256,4,1024]{2,1,0:T(4,128)} %slice.183) | copy-start | bytes 12582916
  327.8 13.9 %collective-permute-start.9 = (bf16[256,1024]{1,0:T(8,128)(2,1)S(1)}, bf16[256,1024]{1,0:T(8,128)(2,1)S(1)}, u32[]{:S(2)}, u32[]{:S(2)}) collective-permute-start(bf16[256,1024]{1,0:T(8,128)(2,1)S(1)} %bitcast.181), channel_id=1, source_target_pairs={{0,3},{1,0},{2,1},{3,2},{4,7},{5,4},{6,5},{7,6},{8,11},{9,8},{10,9... | collective-permute-start | bytes 1572872 | tf_op jit(solution)/shard_map/ppermute | solution.py:60
  341.1 13.2 %collective-permute-start.7 = (bf16[256,1024]{1,0:T(8,128)(2,1)S(1)}, bf16[256,1024]{1,0:T(8,128)(2,1)S(1)}, u32[]{:S(2)}, u32[]{:S(2)}) collective-permute-start(bf16[256,1024]{1,0:T(8,128)(2,1)S(1)} %fusion.39), channel_id=1, source_target_pairs={{0,1},{1,2},{2,3},{3,0},{4,5},{5,6},{6,7},{7,4},{8,9},{9,10},{10,1... | collective-permute-start | bytes 1572872 | tf_op jit(solution)/shard_map/ppermute | solution.py:59
  342.0 12.7 %collective-permute-start.10 = (bf16[256,1024]{1,0:T(8,128)(2,1)S(1)}, bf16[256,1024]{1,0:T(8,128)(2,1)S(1)}, u32[]{:S(2)}, u32[]{:S(2)}) collective-permute-start(bf16[256,1024]{1,0:T(8,128)(2,1)S(1)} %fusion.36), channel_id=1, source_target_pairs={{0,3},{1,0},{2,1},{3,2},{4,7},{5,4},{6,5},{7,6},{8,11},{9,8},{10,9... | collective-permute-start | bytes 1572872 | tf_op jit(solution)/shard_map/ppermute | solution.py:60
  354.7 12.4 %collective-permute-start.8 = (bf16[256,1024]{1,0:T(8,128)(2,1)S(1)}, bf16[256,1024]{1,0:T(8,128)(2,1)S(1)}, u32[]{:S(2)}, u32[]{:S(2)}) collective-permute-start(bf16[256,1024]{1,0:T(8,128)(2,1)S(1)} %fusion.38), channel_id=1, source_target_pairs={{0,1},{1,2},{2,3},{3,0},{4,5},{5,6},{6,7},{7,4},{8,9},{9,10},{10,1... | collective-permute-start | bytes 1572872 | tf_op jit(solution)/shard_map/ppermute | solution.py:59
  355.1 12.3 %collective-permute-start.11 = (bf16[256,1024]{1,0:T(8,128)(2,1)S(1)}, bf16[256,1024]{1,0:T(8,128)(2,1)S(1)}, u32[]{:S(2)}, u32[]{:S(2)}) collective-permute-start(bf16[256,1024]{1,0:T(8,128)(2,1)S(1)} %fusion.35), channel_id=1, source_target_pairs={{0,3},{1,0},{2,1},{3,2},{4,7},{5,4},{6,5},{7,6},{8,11},{9,8},{10,9... | collective-permute-start | bytes 1572872 | tf_op jit(solution)/shard_map/ppermute | solution.py:60
  (26 other events, 133.9 us)

commit v4 on v1

--- a/solution.py
+++ b/solution.py
@@ -109,7 +109,6 @@
         return received[source, ranking].reshape((rows,) + received.shape[3:])
 
     joined_pack = placed(incoming)
-    z_pack = placed(incoming_z)
     margin = conv_values.shape[0] - 1
     flags = doc_start[0].astype(jnp.bfloat16)
     rim = passed_along(
@@ -170,6 +169,8 @@
         prior_gates.append(prior_gates[-1] * block_gates[b - 1])
     slab_state = block_gates[-1][:, None, None] * prior_states[-1] + block_states[-1]
     slab_gate = prior_gates[-1] * block_gates[-1]
+    slab_gate, slab_state, incoming_z = lax.optimization_barrier((slab_gate, slab_state, incoming_z))
+    z_pack = placed(incoming_z)
     arriving = chain(slab_gate, slab_state, "ctx")
     entering = (
         (jnp.stack(prior_states) + jnp.stack(prior_gates)[:, :, None, None] * arriving[None])

time: 368 us -> 366 us (level)
  transfers between devices with their start and end apart: 9 -> 9, of which waited for: 4 -> 5; matrix products, arithmetic and copies ran while one was open for 24% -> 23% of each run, Pallas kernels for 0% -> 0%
where the time goes in v4:
time: 366 us; the launch traced here: 365 us
  waiting for transfers between devices  141 us (39%)
  starting transfers between devices  84.3 us (23%)
  local copies, waits for them, and re-layouts  59.1 us (16%)
  other arithmetic  36.1 us (10%)
  matrix products  29.9 us (8%)
  between operations  14 us (4%)
    all_to_all x1, waiting for transfers between devices, body(): lax.all_to_all(outgoing(joined[None]), ('dp', 'ctx'), split_axis=0, conca...  75.2 us
    ppermute x6, starting transfers between devices, passed_along(): return lax.ppermute(block, axis, route)  59.1 us
    reduce_scatter x1, waiting for transfers between devices, body(): lax.psum_scatter(partial_value.astype(jnp.bfloat16), 'head', scatter_dime...  45.4 us
    ppermute x6, waiting for transfers between devices, passed_along(): return lax.ppermute(block, axis, route)  20.7 us
    all_to_all x1, starting transfers between devices, body(): lax.all_to_all(outgoing(gate_values), ('dp', 'ctx'), split_axis=0, concat...  16.5 us
    convert_element_type x2, local copies, waits for them, and re-layouts, body(): z_pack.astype(jnp.float32)  13.5 us
    dot_general x1, matrix products, body(): jnp.dot(normed, out_weight, preferred_element_type=jnp.float32)  11.1 us
    reshape x2, local copies, waits for them, and re-layouts, body(): x_blocks = x_conv.reshape(blocks, span, groups_local, per_group, width)  10.9 us
  transfers between devices with their start and end apart: 9, of which 5 were waited for; matrix products, arithmetic and copies ran while one was open for 23% of the time, Pallas kernels for 0%

profile of v4, /device:TPU:2, one launch (start us, length us, event | category | flops | bytes accessed | tf_op | source)
XLA Modules:
  0.0 364.7 jit_solution(11000725244677520698)
XLA Ops:
  10.0 3.0 pad_maximum_fusion
  13.1 5.9 %gather_fusion = bf16[64,16,3104]{2,1,0:T(8,128)(2,1)} fusion(bf16[32,16,3104]{2,1,0:T(8,128)(2,1)} %pad_maximum_fusion, s32[1024]{0:T(1024)S(1)} %pad_clamp_fusion), kind=kCustom, calls=%fused_computation | custom fusion | bytes 12714240 | tf_op jit(solution)/shard_map/gather | solution.py:92
  19.0 8.6 %all-to-all-start = ((bf16[32,2,16,3104]{3,2,1,0:T(8,128)(2,1)}), bf16[32,2,16,3104]{3,2,1,0:T(8,128)(2,1)}, u32[]{:S(2)}, u32[]{:S(2)}) async-start(bf16[32,2,16,3104]{3,2,1,0:T(8,128)(2,1)} %bitcast.120), calls=%async_computation | async-start | bytes 13107200 | tf_op jit(solution)/shard_map/all_to_all | solution.py:100
  32.0 75.2 %all-to-all-done = bf16[32,2,16,3104]{3,2,1,0:T(8,128)(2,1)} async-done(((bf16[32,2,16,3104]{3,2,1,0:T(8,128)(2,1)}), bf16[32,2,16,3104]{3,2,1,0:T(8,128)(2,1)}, u32[]{:S(2)}, u32[]{:S(2)}) %all-to-all-start) | async-done | bytes 6357024 | tf_op jit(solution)/shard_map/all_to_all | solution.py:100
  107.2 16.5 %all-to-all-start.1 = ((bf16[32,2,16,2048]{3,2,1,0:T(8,128)(2,1)}), bf16[32,2,16,2048]{3,2,1,0:T(8,128)(2,1)}, u32[]{:S(2)}, u32[]{:S(2)}) async-start(bf16[32,2,16,2048]{3,2,1,0:T(8,128)(2,1)} %bitcast.121), calls=%async_computation.1 | async-start | bytes 8388608 | tf_op jit(solution)/shard_map/all_to_all | solution.py:103
  123.8 5.4 %gather_fusion.1 = bf16[32,16,3104]{2,1,0:T(8,128)(2,1)} fusion(bf16[32,2,16,3104]{3,2,1,0:T(8,128)(2,1)} %all-to-all-done, s32[32]{0:T(128)S(1)} %fusion.55), kind=kCustom, calls=%fused_computation.1 | custom fusion | bytes 6357248 | tf_op jit(solution)/shard_map/gather | solution.py:109
  135.8 3.2 slice.170
  142.7 7.9 %multiply_convert_fusion.3 = bf16[512,2048]{1,0:T(8,128)(2,1)S(1)} fusion(bf16[512,2048]{1,0:T(8,128)(2,1)} %slice.170, bf16[3,2048]{1,0:T(4,128)(2,1)S(1)} %slice.173, f32[512]{0:T(512)S(1)} %get-tuple-element.21, f32[2048]{0:T(1024)S(1)} %bitcast.146, f32[512]{0:T(512)S(1)} %get-tuple-element.22, f32[2048]{0:T(1024)S(1)} %bitcast.147, ...), kind=kLoop, calls=%fused_computation.23 | loop fusion | flops 29360128 | bytes 4245504 | tf_op jit(solution)/shard_map/convert_element_type | solution.py:56
  150.5 5.3 %reshape.328 = bf16[4,128,2,16,64]{4,3,2,1,0:T(8,128)(2,1)} reshape(bf16[512,2048]{1,0:T(8,128)(2,1)S(1)} %multiply_convert_fusion.3) | data formatting | bytes 4194304 | tf_op jit(solution)/shard_map/reshape | solution.py:140
  155.8 5.6 %copy.72 = bf16[4,128,2,16,64]{1,4,3,2,0:T(8,128)(2,1)S(1)} copy(bf16[4,128,2,16,64]{4,3,2,1,0:T(8,128)(2,1)} %reshape.328) | data formatting | bytes 4194304 | tf_op jit(solution)/shard_map/reshape | solution.py:140
  165.5 4.5 %fusion.20 = f32[4,2,16,64,256]{4,3,2,1,0:T(8,128)} fusion(bf16[4,128,2,16,64]{1,4,3,2,0:T(8,128)(2,1)S(1)} %copy.72, f32[4,128,2,16]{1,3,2,0:T(8,128)S(1)} %get-tuple-element.34, bf16[4,128,2,256,1]{3,1,0,2,4:T(8,128)(2,1)S(1)} %bitcast.126), kind=kOutput, calls=%fused_computation.39 | convolution fusion | flops 540016640 | bytes 11075584 | tf_op jit(solution)/shard_map/bsghp,bsgn->bghpn/dot_general | solution.py:160
  170.1 7.7 %multiply_add_fusion = (f32[1,2,16,64,256]{4,3,2,1,0:T(8,128)}, f32[1,2,16,64,256]{4,3,2,1,0:T(8,128)}, f32[1,2,16,64,256]{4,3,2,1,0:T(8,128)}, f32[1,2,16,64,25...) fusion(f32[2,16]{1,0:T(2,128)S(1)} %copy-done.27, ...), kind=kLoop, calls=%fused_computation.50 | loop fusion | flops 2621440 | bytes 23069056 | tf_op jit(solution)/shard_map/add | solution.py:168
  177.8 2.8 bitcast_add_fusion
  180.8 28.7 %collective-permute-start.3 = (bf16[32,64,256]{2,1,0:T(8,128)(2,1)S(1)}, bf16[32,64,256]{2,1,0:T(8,128)(2,1)S(1)}, u32[]{:S(2)}, u32[]{:S(2)}) collective-permute-start(bf16[32,64,256]{2,1,0:T(8,128)(2,1)S(1)} %convert_element_type.126), channel_id=1, source_target_pairs={{0,4},{4,8},{8,12},{12,16},{16,20},{20,24},{24,28},{1,5},{5,9},{9,... | collective-permute-start | bytes 3145736 | tf_op jit(solution)/shard_map/ppermute | solution.py:15
  213.0 17.3 %collective-permute-start.4 = (bf16[32,64,256]{2,1,0:T(8,128)(2,1)}, bf16[32,64,256]{2,1,0:T(8,128)(2,1)}, u32[]{:S(2)}, u32[]{:S(2)}) collective-permute-start(bf16[32,64,256]{2,1,0:T(8,128)(2,1)} %fusion.28), channel_id=1, source_target_pairs={{0,8},{4,12},{8,16},{12,20},{16,24},{20,28},{1,9},{5,13},{9,17},{1... | collective-permute-start | bytes 3145736 | tf_op jit(solution)/shard_map/ppermute | solution.py:15
  233.3 17.8 %collective-permute-done.4 = bf16[32,64,256]{2,1,0:T(8,128)(2,1)} collective-permute-done((bf16[32,64,256]{2,1,0:T(8,128)(2,1)}, bf16[32,64,256]{2,1,0:T(8,128)(2,1)}, u32[]{:S(2)}, u32[]{:S(2)}) %collective-permute-start.4) | collective-permute-done | bytes 1048608 | tf_op jit(solution)/shard_map/ppermute | solution.py:15
  253.8 7.8 %collective-permute-start.5 = (bf16[32,64,256]{2,1,0:T(8,128)(2,1)}, bf16[32,64,256]{2,1,0:T(8,128)(2,1)}, u32[]{:S(2)}, u32[]{:S(2)}) collective-permute-start(bf16[32,64,256]{2,1,0:T(8,128)(2,1)} %fusion.17), channel_id=1, source_target_pairs={{0,16},{4,20},{8,24},{12,28},{1,17},{5,21},{9,25},{13,29},{2,18},{... | collective-permute-start | bytes 3145736 | tf_op jit(solution)/shard_map/ppermute | solution.py:15
  262.9 2.9 gather_fusion.3
  267.4 6.3 %fusion.1 = f32[4,2,16,64,128]{4,3,2,1,0:T(8,128)} fusion(bf16[4,128,2,16,64]{1,4,3,2,0:T(8,128)(2,1)} %copy-done.2, f32[4,2,16,128]{3,2,1,0:T(8,128)S(1)} %bitcast.142, f32[4,2,128,128]{3,2,1,0:T(8,128)S(1)} %fusion.35, f32[4,2,16,128]{3,2,1,0:T(8,128)S(1)} %bitcast.141, pred[4,128,128]{2,1,0:T(8,128)(4,1)S(1)} %copy-done.8), kind=kOutput, calls=%fused_computation.10 | convolution fusion | flops 278921216 | bytes 7012352 | tf_op jit(solution)/shard_map/bghts,bsghp->btghp/dot_general | solution.py:153
  275.5 5.6 %reshape.290 = f32[4,128,2,16,64]{4,3,2,1,0:T(8,128)} reshape(bf16[32,16,2048]{2,1,0:T(8,128)(2,1)S(1)} %gather_fusion.3) | data formatting | bytes 6291456 | tf_op jit(solution)/shard_map/convert_element_type | solution.py:192
  281.0 8.0 %copy.80 = f32[4,128,2,16,64]{1,4,3,2,0:T(8,128)} copy(f32[4,128,2,16,64]{4,3,2,1,0:T(8,128)} %reshape.290) | data formatting | bytes 8388608 | tf_op jit(solution)/shard_map/convert_element_type | solution.py:192
  291.9 6.5 %multiply_reduce_fusion = (f32[4,128,2]{1,2,0:T(2,128)S(1)}, f32[4,128,2,16,64]{1,4,3,2,0:T(8,128)S(1)}) fusion(f32[4,128,2,16,64]{1,4,3,2,0:T(8,128)} %copy.80, bf16[4,128,2,16,64]{1,4,3,2,0:T(8,128)(2,1)S(1)} %copy-done.3, f32[2,16]{1,0:T(2,128)S(1)} %mul.518, f32[4,128,2,16]{1,3,2,0:T(8,128)S(1)} %copy-done.9, ...), kind=kOutput, calls=%fused_computation.17 | convolution fusion | flops 562035712 | bytes 23663248 | tf_op jit(solution)/shard_map/bqgn,bghpn->bqghp/dot_general | solution.py:180
  301.4 11.1 %convolution_convert_fusion = bf16[512,4096]{1,0:T(8,128)(2,1)} fusion(bf16[2048,4096]{1,0:T(8,128)(2,1)S(1)} %bitcast.151, bf16[256,8,4,128]{3,2,1,0:T(4,128)(2,1)S(1)} %bitcast.135), kind=kOutput, calls=%fused_computation.7 | convolution fusion | flops 8592031744 | bytes 23068672 | tf_op jit(solution)/shard_map/dot_general | solution.py:200
  312.5 45.4 %reduce-scatter.2.cloned.1.call-done = bf16[512,1024]{1,0:T(8,128)(2,1)} async-done(((bf16[512,4096]{1,0:T(8,128)(2,1)}), bf16[512,1024]{1,0:T(8,128)(2,1)}) %reduce-scatter.2.cloned.1.call-update) | async-done | bytes 1048592 | tf_op jit(solution)/shard_map/reduce_scatter | solution.py:201
  (153 shorter events, 41.8 us)
Async XLA Ops:
  6.5 21.3 %copy-start = (bf16[1,512,2048]{2,1,0:T(8,128)(2,1)S(1)}, bf16[1,512,2048]{2,1,0:T(8,128)(2,1)}, u32[]{:S(2)}) copy-start(bf16[1,512,2048]{2,1,0:T(8,128)(2,1)} %param.13) | copy-start | bytes 6291460
  19.0 8.7 %copy-start.11 = (s32[1,512]{1,0:T(1,128)S(1)}, s32[1,512]{1,0:T(1,128)}, u32[]{:S(2)}) copy-start(s32[1,512]{1,0:T(1,128)} %param.21) | copy-start | bytes 6148
  19.0 88.3 %all-to-all-start = ((bf16[32,2,16,3104]{3,2,1,0:T(8,128)(2,1)}), bf16[32,2,16,3104]{3,2,1,0:T(8,128)(2,1)}, u32[]{:S(2)}, u32[]{:S(2)}) async-start(bf16[32,2,16,3104]{3,2,1,0:T(8,128)(2,1)} %bitcast.120), calls=%async_computation | async-start | bytes 13107200 | tf_op jit(solution)/shard_map/all_to_all | solution.py:100
  107.2 73.4 %all-to-all-start.1 = ((bf16[32,2,16,2048]{3,2,1,0:T(8,128)(2,1)}), bf16[32,2,16,2048]{3,2,1,0:T(8,128)(2,1)}, u32[]{:S(2)}, u32[]{:S(2)}) async-start(bf16[32,2,16,2048]{3,2,1,0:T(8,128)(2,1)} %bitcast.121), calls=%async_computation.1 | async-start | bytes 8388608 | tf_op jit(solution)/shard_map/all_to_all | solution.py:103
  123.7 234.1 %reduce-scatter.2.cloned.1.call-start = ((), (), s32[]{:S(2)}) async-start(), calls=%async_computation.3 | async-start | bytes 5242880 | tf_op jit(solution)/shard_map/reduce_scatter | solution.py:201
  131.1 7.9 %copy-start.5 = (f32[512,32]{1,0:T(8,128)}, f32[512,32]{1,0:T(8,128)S(1)}, u32[]{:S(2)}) copy-start(f32[512,32]{1,0:T(8,128)S(1)} %get-tuple-element.28) | copy-start | bytes 196612
  132.2 10.1 %collective-permute-start = (bf16[3,3105]{1,0:T(4,128)(2,1)S(1)}, bf16[3,3105]{1,0:T(4,128)(2,1)S(1)}, u32[]{:S(2)}, u32[]{:S(2)}) collective-permute-start(bf16[3,3105]{1,0:T(4,128)(2,1)S(1)} %pad_maximum_fusion.3), channel_id=1, source_target_pairs={{0,4},{4,8},{8,12},{12,16},{16,20},{20,24},{24,28},{1,5},{5,9},{9,... | collective-permute-start | bytes 55898 | tf_op jit(solution)/shard_map/ppermute | solution.py:15
  170.0 7.8 %copy-start.19 = (f32[32]{0:T(128)S(1)}, f32[32]{0:T(128)}, u32[]{:S(2)}) copy-start(f32[32]{0:T(128)} %get-tuple-element.55) | copy-start | bytes 388
  180.6 31.1 %copy-start.17 = (f32[32]{0:T(128)S(1)}, f32[32]{0:T(128)}, u32[]{:S(2)}) copy-start(f32[32]{0:T(128)} %get-tuple-element.8) | copy-start | bytes 388
  180.8 49.6 %copy-start.31 = (f32[32]{0:T(128)S(1)}, f32[32]{0:T(128)}, u32[]{:S(2)}) copy-start(f32[32]{0:T(128)} %param.17) | copy-start | bytes 388
  180.8 51.7 %copy-start.18 = (f32[2048]{0:T(1024)S(1)}, f32[2048]{0:T(1024)}, u32[]{:S(2)}) copy-start(f32[2048]{0:T(1024)} %param.22) | copy-start | bytes 24580
  180.8 30.9 %collective-permute-start.3 = (bf16[32,64,256]{2,1,0:T(8,128)(2,1)S(1)}, bf16[32,64,256]{2,1,0:T(8,128)(2,1)S(1)}, u32[]{:S(2)}, u32[]{:S(2)}) collective-permute-start(bf16[32,64,256]{2,1,0:T(8,128)(2,1)S(1)} %convert_element_type.126), channel_id=1, source_target_pairs={{0,4},{4,8},{8,12},{12,16},{16,20},{20,24},{24,28},{1,5},{5,9},{9,... | collective-permute-start | bytes 3145736 | tf_op jit(solution)/shard_map/ppermute | solution.py:15
  213.0 38.0 %collective-permute-start.4 = (bf16[32,64,256]{2,1,0:T(8,128)(2,1)}, bf16[32,64,256]{2,1,0:T(8,128)(2,1)}, u32[]{:S(2)}, u32[]{:S(2)}) collective-permute-start(bf16[32,64,256]{2,1,0:T(8,128)(2,1)} %fusion.28), channel_id=1, source_target_pairs={{0,8},{4,12},{8,16},{12,20},{16,24},{20,28},{1,9},{5,13},{9,17},{1... | collective-permute-start | bytes 3145736 | tf_op jit(solution)/shard_map/ppermute | solution.py:15
  231.2 2.1 collective-permute-start.1
  251.1 10.5 %copy-start.24 = (f32[1,32]{1,0:T(1,128)S(1)}, f32[1,32]{1,0:T(1,128)}, u32[]{:S(2)}) copy-start(f32[1,32]{1,0:T(1,128)} %get-tuple-element.44) | copy-start | bytes 388
  251.1 10.5 %copy-start.25 = (f32[1,32]{1,0:T(1,128)S(1)}, f32[1,32]{1,0:T(1,128)}, u32[]{:S(2)}) copy-start(f32[1,32]{1,0:T(1,128)} %get-tuple-element.46) | copy-start | bytes 388
  251.1 10.5 %copy-start.26 = (f32[1,32]{1,0:T(1,128)S(1)}, f32[1,32]{1,0:T(1,128)}, u32[]{:S(2)}) copy-start(f32[1,32]{1,0:T(1,128)} %get-tuple-element.47) | copy-start | bytes 388
  253.8 35.3 %collective-permute-start.5 = (bf16[32,64,256]{2,1,0:T(8,128)(2,1)}, bf16[32,64,256]{2,1,0:T(8,128)(2,1)}, u32[]{:S(2)}, u32[]{:S(2)}) collective-permute-start(bf16[32,64,256]{2,1,0:T(8,128)(2,1)} %fusion.17), channel_id=1, source_target_pairs={{0,16},{4,20},{8,24},{12,28},{1,17},{5,21},{9,25},{13,29},{2,18},{... | collective-permute-start | bytes 3145736 | tf_op jit(solution)/shard_map/ppermute | solution.py:15
  273.6 15.3 %collective-permute-start.2 = (f32[32]{0:T(128)S(1)}, f32[32]{0:T(128)S(1)}, u32[]{:S(2)}, u32[]{:S(2)}) collective-permute-start(f32[32]{0:T(128)S(1)} %get-tuple-element.16), channel_id=1, source_target_pairs={{0,8},{4,12},{8,16},{12,20},{16,24},{20,28},{1,9},{5,13},{9,17},{1... | collective-permute-start | bytes 392 | tf_op jit(solution)/shard_map/ppermute | solution.py:15
  289.0 12.3 %slice-start = ((s8[16777216]{0:T(1024)(128)(4,1)}), s8[4194304]{0:T(1024)(128)(4,1)S(1)}, s32[]{:S(2)}) async-start(s8[16777216]{0:T(1024)(128)(4,1)} %bitcast.150), calls=%async_computation.4 | async-start | bytes 8388608
  291.9 9.4 %slice-start.1 = ((s8[16777216]{0:T(1024)(128)(4,1)}), s8[4194304]{0:T(1024)(128)(4,1)S(1)}, s32[]{:S(2)}) async-start(s8[16777216]{0:T(1024)(128)(4,1)} %bitcast.150), calls=%async_computation.5 | async-start | bytes 8388608
  291.9 9.4 %slice-start.2 = ((s8[16777216]{0:T(1024)(128)(4,1)}), s8[4194304]{0:T(1024)(128)(4,1)S(1)}, s32[]{:S(2)}) async-start(s8[16777216]{0:T(1024)(128)(4,1)} %bitcast.150), calls=%async_computation.6 | async-start | bytes 8388608
  291.9 9.4 %slice-start.3 = ((s8[16777216]{0:T(1024)(128)(4,1)}), s8[4194304]{0:T(1024)(128)(4,1)S(1)}, s32[]{:S(2)}) async-start(s8[16777216]{0:T(1024)(128)(4,1)} %bitcast.150), calls=%async_computation.7 | async-start | bytes 8388608
  312.4 45.4 %copy-start.1 = (bf16[1,512,2048]{2,1,0:T(8,128)(2,1)S(1)}, bf16[1,512,2048]{2,1,0:T(8,128)(2,1)}, u32[]{:S(2)}) copy-start(bf16[1,512,2048]{2,1,0:T(8,128)(2,1)} %param.13) | copy-start | bytes 6291460
  (21 other events, 92.9 us)
Sparse Core Ops, SparseCore 0:
  312.6 45.2 reduce-scatter.1

commit v5 on v4

--- a/solution.py
+++ b/solution.py
@@ -16,29 +16,48 @@
 
 
 def chain(gate, summed, axis):
+    count = lax.axis_size(axis)
     place = lax.axis_index(axis)
+    core = place % 2
+    chip = place // 2
+    chips = count // 2
+    swap = [(i, i ^ 1) for i in range(count)]
 
     def join(earlier, latter):
         return (earlier[0] * latter[0], latter[0][:, None, None] * earlier[1] + latter[1])
 
+    def across(pair, route):
+        gate_in, summed_in = lax.ppermute((pair[0], pair[1].astype(jnp.bfloat16)), axis, route)
+        return gate_in, summed_in.astype(jnp.float32)
+
+    local = (gate, summed)
+    other = across(local, swap)
+    lead = core == 0
+    first = tuple(jnp.where(lead, a, b) for a, b in zip(local, other))
+    second = tuple(jnp.where(lead, b, a) for a, b in zip(local, other))
+    both = join(first, second)
+    half = gate.shape[0] // 2
+    mine = tuple(lax.dynamic_slice_in_dim(a, core * half, half, 0) for a in both)
+
     def fetch(pair, distance):
-        gate_in, summed_in = passed_along(
-            (pair[0], pair[1].astype(jnp.bfloat16)), axis, distance
-        )
-        gate_in = jnp.where(place >= distance, gate_in, 1.0)
-        return gate_in, summed_in.astype(jnp.float32)
-
-    local = (gate, summed)
-    before = fetch(local, 1)
-    window = join(before, local)
+        gate_in, summed_in = across(pair, [(i - 2 * distance, i) for i in range(2 * distance, count)])
+        return jnp.where(chip >= distance, gate_in, 1.0), summed_in
+
+    before = fetch(mine, 1)
+    window = join(before, mine)
     distance = 2
-    while distance < lax.axis_size(axis):
+    while distance < chips:
         received = fetch(window, distance)
         before = join(received, before)
         distance *= 2
-        if distance < lax.axis_size(axis):
+        if distance < chips:
             window = join(received, window)
-    return before[1]
+    partner = across(before, swap)
+    whole = tuple(
+        jnp.where(lead, jnp.concatenate([a, b]), jnp.concatenate([b, a]))
+        for a, b in zip(before, partner)
+    )
+    return jnp.where(lead, whole[1], join(whole, first)[1])
 
 
 def conv_core(ext_values, weight, free_ext, length):

time: 366 us -> 345 us (0.943)
  starting transfers between devices: 84.3 us -> 69.1 us
  waiting for transfers between devices: 141 us -> 134 us
  other arithmetic: 36.1 us -> 40.3 us
  matrix products: 29.9 us -> 26.2 us
    ppermute x6 -> x1, starting transfers between devices: 59.1 us -> 2.19 us  [passed_along(): return lax.ppermute(block, axis, route)]
    ppermute x0 -> x6, starting transfers between devices: none -> 41.8 us  [across(): lax.ppermute((pair[0], pair[1].astype(jnp.bfloat16)), axis, route)]
    ppermute x6 -> x1, waiting for transfers between devices: 20.7 us -> 0.01 us  [passed_along(): return lax.ppermute(block, axis, route)]
    ppermute x0 -> x6, waiting for transfers between devices: none -> 13.4 us  [across(): lax.ppermute((pair[0], pair[1].astype(jnp.bfloat16)), axis, route)]
    convert_element_type x3 -> x6, other arithmetic: 4.12 us -> 8.7 us  [the longest x4 6.36 us: across(): pair[1].astype(jnp.bfloat16)]
  transfers between devices with their start and end apart: 9 -> 10, of which waited for: 5 -> 4; matrix products, arithmetic and copies ran while one was open for 23% -> 24% of each run, Pallas kernels for 0% -> 0%
where the time goes in v5:
time: 345 us; the launch traced here: 343 us
  waiting for transfers between devices  134 us (39%)
  starting transfers between devices  69.1 us (20%)
  local copies, waits for them, and re-layouts  59.7 us (17%)
  other arithmetic  40.3 us (12%)
  matrix products  26.2 us (8%)
  between operations  14 us (4%)
    all_to_all x1, waiting for transfers between devices, body(): lax.all_to_all(outgoing(joined[None]), ('dp', 'ctx'), split_axis=0, conca...  75.1 us
    reduce_scatter x1, waiting for transfers between devices, body(): lax.psum_scatter(partial_value.astype(jnp.bfloat16), 'head', scatter_dime...  45.4 us
    ppermute x6, starting transfers between devices, across(): lax.ppermute((pair[0], pair[1].astype(jnp.bfloat16)), axis, route)  41.8 us
    all_to_all x1, starting transfers between devices, body(): lax.all_to_all(outgoing(gate_values), ('dp', 'ctx'), split_axis=0, concat...  16.5 us
    dot_general x1, matrix products, body(): jnp.dot(normed, out_weight, preferred_element_type=jnp.float32)  13.9 us
    convert_element_type x2, local copies, waits for them, and re-layouts, body(): z_pack.astype(jnp.float32)  13.6 us
    ppermute x6, waiting for transfers between devices, across(): lax.ppermute((pair[0], pair[1].astype(jnp.bfloat16)), axis, route)  13.4 us
    reshape x2, local copies, waits for them, and re-layouts, body(): x_blocks = x_conv.reshape(blocks, span, groups_local, per_group, width)  10.9 us
  transfers between devices with their start and end apart: 10, of which 4 were waited for; matrix products, arithmetic and copies ran while one was open for 24% of the time, Pallas kernels for 0%

profile of v5, /device:TPU:2, one launch (start us, length us, event | category | flops | bytes accessed | tf_op | source)
XLA Modules:
  0.0 343.1 jit_solution(5152755150625023358)
XLA Ops:
  10.0 3.0 pad_maximum_fusion
  13.0 5.9 %gather_fusion = bf16[64,16,3104]{2,1,0:T(8,128)(2,1)} fusion(bf16[32,16,3104]{2,1,0:T(8,128)(2,1)} %pad_maximum_fusion, s32[1024]{0:T(1024)S(1)} %pad_clamp_fusion), kind=kCustom, calls=%fused_computation | custom fusion | bytes 12714240 | tf_op jit(solution)/shard_map/gather | solution.py:111
  18.9 8.6 %all-to-all-start = ((bf16[32,2,16,3104]{3,2,1,0:T(8,128)(2,1)}), bf16[32,2,16,3104]{3,2,1,0:T(8,128)(2,1)}, u32[]{:S(2)}, u32[]{:S(2)}) async-start(bf16[32,2,16,3104]{3,2,1,0:T(8,128)(2,1)} %bitcast.120), calls=%async_computation | async-start | bytes 13107200 | tf_op jit(solution)/shard_map/all_to_all | solution.py:119
  32.1 75.1 %all-to-all-done = bf16[32,2,16,3104]{3,2,1,0:T(8,128)(2,1)} async-done(((bf16[32,2,16,3104]{3,2,1,0:T(8,128)(2,1)}), bf16[32,2,16,3104]{3,2,1,0:T(8,128)(2,1)}, u32[]{:S(2)}, u32[]{:S(2)}) %all-to-all-start) | async-done | bytes 6357024 | tf_op jit(solution)/shard_map/all_to_all | solution.py:119
  107.2 16.5 %all-to-all-start.1 = ((bf16[32,2,16,2048]{3,2,1,0:T(8,128)(2,1)}), bf16[32,2,16,2048]{3,2,1,0:T(8,128)(2,1)}, u32[]{:S(2)}, u32[]{:S(2)}) async-start(bf16[32,2,16,2048]{3,2,1,0:T(8,128)(2,1)} %bitcast.121), calls=%async_computation.1 | async-start | bytes 8388608 | tf_op jit(solution)/shard_map/all_to_all | solution.py:122
  123.7 5.5 %gather_fusion.1 = bf16[32,16,3104]{2,1,0:T(8,128)(2,1)} fusion(bf16[32,2,16,3104]{3,2,1,0:T(8,128)(2,1)} %all-to-all-done, s32[32]{0:T(128)S(1)} %fusion.52), kind=kCustom, calls=%fused_computation.1 | custom fusion | bytes 6357248 | tf_op jit(solution)/shard_map/gather | solution.py:128
  136.0 3.2 slice.170
  142.8 7.6 %multiply_convert_fusion.3 = bf16[512,2048]{1,0:T(8,128)(2,1)S(1)} fusion(bf16[512,2048]{1,0:T(8,128)(2,1)} %slice.170, bf16[3,2048]{1,0:T(4,128)(2,1)S(1)} %slice.173, f32[512]{0:T(512)S(1)} %get-tuple-element.26, f32[2048]{0:T(1024)S(1)} %bitcast.146, f32[512]{0:T(512)S(1)} %get-tuple-element.27, f32[2048]{0:T(1024)S(1)} %bitcast.147, ...), kind=kLoop, calls=%fused_computation.23 | loop fusion | flops 29360128 | bytes 4245504 | tf_op jit(solution)/shard_map/convert_element_type | solution.py:75
  150.5 5.3 %reshape.328 = bf16[4,128,2,16,64]{4,3,2,1,0:T(8,128)(2,1)} reshape(bf16[512,2048]{1,0:T(8,128)(2,1)S(1)} %multiply_convert_fusion.3) | data formatting | bytes 4194304 | tf_op jit(solution)/shard_map/reshape | solution.py:159
  155.8 5.6 %copy.72 = bf16[4,128,2,16,64]{1,4,3,2,0:T(8,128)(2,1)S(1)} copy(bf16[4,128,2,16,64]{4,3,2,1,0:T(8,128)(2,1)} %reshape.328) | data formatting | bytes 4194304 | tf_op jit(solution)/shard_map/reshape | solution.py:159
  164.7 4.6 %fusion.16 = f32[4,2,16,64,256]{4,3,2,1,0:T(8,128)} fusion(bf16[4,128,2,16,64]{1,4,3,2,0:T(8,128)(2,1)S(1)} %copy.72, f32[4,128,2,16]{1,3,2,0:T(8,128)S(1)} %get-tuple-element.39, bf16[4,128,2,256,1]{3,1,0,2,4:T(8,128)(2,1)S(1)} %bitcast.126), kind=kOutput, calls=%fused_computation.31 | convolution fusion | flops 540016640 | bytes 11075584 | tf_op jit(solution)/shard_map/bsghp,bsgn->bghpn/dot_general | solution.py:179
  169.3 7.6 %multiply_add_fusion = (f32[1,2,16,64,256]{4,3,2,1,0:T(8,128)}, f32[1,2,16,64,256]{4,3,2,1,0:T(8,128)}, f32[1,2,16,64,256]{4,3,2,1,0:T(8,128)}, f32[1,2,16,64,25...) fusion(f32[2,16]{1,0:T(2,128)S(1)} %copy-done.35, ...), kind=kLoop, calls=%fused_computation.44 | loop fusion | flops 2621440 | bytes 23069056 | tf_op jit(solution)/shard_map/add | solution.py:187
  180.9 26.6 %collective-permute-start.3 = (bf16[32,64,256]{2,1,0:T(8,128)(2,1)}, bf16[32,64,256]{2,1,0:T(8,128)(2,1)}, u32[]{:S(2)}, u32[]{:S(2)}) collective-permute-start(bf16[32,64,256]{2,1,0:T(8,128)(2,1)} %convert_element_type.132), channel_id=1, source_target_pairs={{0,4},{4,0},{8,12},{12,8},{16,20},{20,16},{24,28},{28,24},{1,5},{5... | collective-permute-start | bytes 3145736 | tf_op jit(solution)/shard_map/ppermute | solution.py:30
  215.4 5.0 %collective-permute-start.4 = (bf16[16,64,256]{2,1,0:T(8,128)(2,1)}, bf16[16,64,256]{2,1,0:T(8,128)(2,1)S(1)}, u32[]{:S(2)}, u32[]{:S(2)}) collective-permute-start(bf16[16,64,256]{2,1,0:T(8,128)(2,1)} %get-tuple-element.21), channel_id=1, source_target_pairs={{0,8},{4,12},{8,16},{12,20},{16,24},{20,28},{1,9},{5,13},{9,17},{1... | collective-permute-start | bytes 1572872 | tf_op jit(solution)/shard_map/ppermute | solution.py:30
  221.4 10.7 %collective-permute-done.4 = bf16[16,64,256]{2,1,0:T(8,128)(2,1)S(1)} collective-permute-done((bf16[16,64,256]{2,1,0:T(8,128)(2,1)}, bf16[16,64,256]{2,1,0:T(8,128)(2,1)S(1)}, u32[]{:S(2)}, u32[]{:S(2)}) %collective-permute-start.4) | collective-permute-done | bytes 524320 | tf_op jit(solution)/shard_map/ppermute | solution.py:30
  234.5 6.4 %collective-permute-start.5 = (bf16[16,64,256]{2,1,0:T(8,128)(2,1)}, bf16[16,64,256]{2,1,0:T(8,128)(2,1)}, u32[]{:S(2)}, u32[]{:S(2)}) collective-permute-start(bf16[16,64,256]{2,1,0:T(8,128)(2,1)} %fusion.27), channel_id=1, source_target_pairs={{0,16},{4,20},{8,24},{12,28},{1,17},{5,21},{9,25},{13,29},{2,18},{... | collective-permute-start | bytes 1572872 | tf_op jit(solution)/shard_map/ppermute | solution.py:30
  241.3 2.9 gather_fusion.3
  244.2 5.6 %reshape.290 = f32[4,128,2,16,64]{4,3,2,1,0:T(8,128)} reshape(bf16[32,16,2048]{2,1,0:T(8,128)(2,1)S(1)} %gather_fusion.3) | data formatting | bytes 6291456 | tf_op jit(solution)/shard_map/convert_element_type | solution.py:211
  250.9 3.8 %collective-permute-start.2 = (f32[16]{0:T(128)S(1)}, f32[16]{0:T(128)S(1)}, u32[]{:S(2)}, u32[]{:S(2)}) collective-permute-start(f32[16]{0:T(128)S(1)} %dynamic_slice.6), channel_id=1, source_target_pairs={{0,8},{4,12},{8,16},{12,20},{16,24},{20,28},{1,9},{5,13},{9,17},{1... | collective-permute-start | bytes 200 | tf_op jit(solution)/shard_map/ppermute | solution.py:30
  254.7 8.0 %copy.80 = f32[4,128,2,16,64]{1,4,3,2,0:T(8,128)} copy(f32[4,128,2,16,64]{4,3,2,1,0:T(8,128)} %reshape.290) | data formatting | bytes 8388608 | tf_op jit(solution)/shard_map/convert_element_type | solution.py:211
  264.5 3.7 %fusion.1 = f32[4,2,16,64,128]{4,3,2,1,0:T(8,128)S(1)} fusion(bf16[4,128,2,16,64]{1,4,3,2,0:T(8,128)(2,1)S(1)} %copy-done.5, f32[4,2,16,128]{3,2,1,0:T(8,128)S(1)} %bitcast.142, f32[4,2,128,128]{3,2,1,0:T(8,128)S(1)} %copy-done.15, f32[4,2,16,128]{3,2,1,0:T(8,128)S(1)} %bitcast.141, pred[4,128,128]{2,1,0:T(8,128)(4,1)S(1)} %copy-done.16), kind=kOutput, calls=%fused_computation.10 | convolution fusion | flops 278921216 | bytes 7012352 | tf_op jit(solution)/shard_map/bghts,bsghp->btghp/dot_general | solution.py:172
  271.2 3.0 multiply_reduce_fusion
  277.0 13.9 %convolution_convert_fusion = bf16[512,4096]{1,0:T(8,128)(2,1)} fusion(bf16[2048,4096]{1,0:T(8,128)(2,1)} %param.23, bf16[256,8,4,128]{3,2,1,0:T(4,128)(2,1)S(1)} %bitcast.135), kind=kOutput, calls=%fused_computation.7 | convolution fusion | flops 8592031744 | bytes 23068672 | tf_op jit(solution)/shard_map/dot_general | solution.py:219
  290.9 45.4 %reduce-scatter.2.cloned.1.call-done = bf16[512,1024]{1,0:T(8,128)(2,1)} async-done(((bf16[512,4096]{1,0:T(8,128)(2,1)}), bf16[512,1024]{1,0:T(8,128)(2,1)}) %reduce-scatter.2.cloned.1.call-update) | async-done | bytes 1048592 | tf_op jit(solution)/shard_map/reduce_scatter | solution.py:220
  (168 shorter events, 45.8 us)
Async XLA Ops:
  6.5 21.3 %copy-start = (bf16[1,512,2048]{2,1,0:T(8,128)(2,1)S(1)}, bf16[1,512,2048]{2,1,0:T(8,128)(2,1)}, u32[]{:S(2)}) copy-start(bf16[1,512,2048]{2,1,0:T(8,128)(2,1)} %param.13) | copy-start | bytes 6291460
  18.9 8.7 %copy-start.19 = (s32[1,512]{1,0:T(1,128)S(1)}, s32[1,512]{1,0:T(1,128)}, u32[]{:S(2)}) copy-start(s32[1,512]{1,0:T(1,128)} %param.21) | copy-start | bytes 6148
  18.9 88.3 %all-to-all-start = ((bf16[32,2,16,3104]{3,2,1,0:T(8,128)(2,1)}), bf16[32,2,16,3104]{3,2,1,0:T(8,128)(2,1)}, u32[]{:S(2)}, u32[]{:S(2)}) async-start(bf16[32,2,16,3104]{3,2,1,0:T(8,128)(2,1)} %bitcast.120), calls=%async_computation | async-start | bytes 13107200 | tf_op jit(solution)/shard_map/all_to_all | solution.py:119
  107.2 72.5 %all-to-all-start.1 = ((bf16[32,2,16,2048]{3,2,1,0:T(8,128)(2,1)}), bf16[32,2,16,2048]{3,2,1,0:T(8,128)(2,1)}, u32[]{:S(2)}, u32[]{:S(2)}) async-start(bf16[32,2,16,2048]{3,2,1,0:T(8,128)(2,1)} %bitcast.121), calls=%async_computation.1 | async-start | bytes 8388608 | tf_op jit(solution)/shard_map/all_to_all | solution.py:122
  123.7 212.6 %reduce-scatter.2.cloned.1.call-start = ((), (), s32[]{:S(2)}) async-start(), calls=%async_computation.3 | async-start | bytes 5242880 | tf_op jit(solution)/shard_map/reduce_scatter | solution.py:220
  131.2 8.0 %copy-start.7 = (f32[512,32]{1,0:T(8,128)}, f32[512,32]{1,0:T(8,128)S(1)}, u32[]{:S(2)}) copy-start(f32[512,32]{1,0:T(8,128)S(1)} %get-tuple-element.33) | copy-start | bytes 196612
  132.3 10.2 %collective-permute-start = (bf16[3,3105]{1,0:T(4,128)(2,1)S(1)}, bf16[3,3105]{1,0:T(4,128)(2,1)S(1)}, u32[]{:S(2)}, u32[]{:S(2)}) collective-permute-start(bf16[3,3105]{1,0:T(4,128)(2,1)S(1)} %pad_maximum_fusion.3), channel_id=1, source_target_pairs={{0,4},{4,8},{8,12},{12,16},{16,20},{20,24},{24,28},{1,5},{5,9},{9,... | collective-permute-start | bytes 55898 | tf_op jit(solution)/shard_map/ppermute | solution.py:15
  169.3 7.7 %copy-start.26 = (f32[32]{0:T(128)S(1)}, f32[32]{0:T(128)}, u32[]{:S(2)}) copy-start(f32[32]{0:T(128)} %get-tuple-element.60) | copy-start | bytes 388
  169.3 7.7 %copy-start.27 = (f32[32]{0:T(128)S(1)}, f32[32]{0:T(128)}, u32[]{:S(2)}) copy-start(f32[32]{0:T(128)} %get-tuple-element.50) | copy-start | bytes 388
  179.7 27.7 %copy-start.31 = (f32[32]{0:T(128)S(1)}, f32[32]{0:T(128)}, u32[]{:S(2)}) copy-start(f32[32]{0:T(128)} %get-tuple-element.8) | copy-start | bytes 388
  180.9 29.3 %collective-permute-start.3 = (bf16[32,64,256]{2,1,0:T(8,128)(2,1)}, bf16[32,64,256]{2,1,0:T(8,128)(2,1)}, u32[]{:S(2)}, u32[]{:S(2)}) collective-permute-start(bf16[32,64,256]{2,1,0:T(8,128)(2,1)} %convert_element_type.132), channel_id=1, source_target_pairs={{0,4},{4,0},{8,12},{12,8},{16,20},{20,16},{24,28},{28,24},{1,5},{5... | collective-permute-start | bytes 3145736 | tf_op jit(solution)/shard_map/ppermute | solution.py:30
  207.5 2.6 collective-permute-start.1
  215.4 25.5 %copy-start.32 = (f32[1,32]{1,0:T(1,128)S(1)}, f32[1,32]{1,0:T(1,128)}, u32[]{:S(2)}) copy-start(f32[1,32]{1,0:T(1,128)} %get-tuple-element.49) | copy-start | bytes 388
  215.4 25.5 %copy-start.33 = (f32[1,32]{1,0:T(1,128)S(1)}, f32[1,32]{1,0:T(1,128)}, u32[]{:S(2)}) copy-start(f32[1,32]{1,0:T(1,128)} %get-tuple-element.51) | copy-start | bytes 388
  215.4 25.5 %copy-start.34 = (f32[1,32]{1,0:T(1,128)S(1)}, f32[1,32]{1,0:T(1,128)}, u32[]{:S(2)}) copy-start(f32[1,32]{1,0:T(1,128)} %get-tuple-element.52) | copy-start | bytes 388
  215.4 25.8 %copy-start.8 = (f32[512,32]{1,0:T(8,128)S(1)}, f32[512,32]{1,0:T(8,128)}, u32[]{:S(2)}) copy-start(f32[512,32]{1,0:T(8,128)} %copy-done.7) | copy-start | bytes 196612
  215.4 16.7 %collective-permute-start.4 = (bf16[16,64,256]{2,1,0:T(8,128)(2,1)}, bf16[16,64,256]{2,1,0:T(8,128)(2,1)S(1)}, u32[]{:S(2)}, u32[]{:S(2)}) collective-permute-start(bf16[16,64,256]{2,1,0:T(8,128)(2,1)} %get-tuple-element.21), channel_id=1, source_target_pairs={{0,8},{4,12},{8,16},{12,20},{16,24},{20,28},{1,9},{5,13},{9,17},{1... | collective-permute-start | bytes 1572872 | tf_op jit(solution)/shard_map/ppermute | solution.py:30
  232.1 9.1 %copy-start.13 = (bf16[16,64,256]{2,1,0:T(8,128)(2,1)}, bf16[16,64,256]{2,1,0:T(8,128)(2,1)S(1)}, u32[]{:S(2)}) copy-start(bf16[16,64,256]{2,1,0:T(8,128)(2,1)S(1)} %collective-permute-done.4) | copy-start | bytes 1572868
  234.5 28.2 %collective-permute-start.5 = (bf16[16,64,256]{2,1,0:T(8,128)(2,1)}, bf16[16,64,256]{2,1,0:T(8,128)(2,1)}, u32[]{:S(2)}, u32[]{:S(2)}) collective-permute-start(bf16[16,64,256]{2,1,0:T(8,128)(2,1)} %fusion.27), channel_id=1, source_target_pairs={{0,16},{4,20},{8,24},{12,28},{1,17},{5,21},{9,25},{13,29},{2,18},{... | collective-permute-start | bytes 1572872 | tf_op jit(solution)/shard_map/ppermute | solution.py:30
  250.9 11.8 %copy-start.14 = (bf16[16,64,256]{2,1,0:T(8,128)(2,1)S(1)}, bf16[16,64,256]{2,1,0:T(8,128)(2,1)}, u32[]{:S(2)}) copy-start(bf16[16,64,256]{2,1,0:T(8,128)(2,1)} %copy-done.13) | copy-start | bytes 1572868
  250.9 11.8 %collective-permute-start.2 = (f32[16]{0:T(128)S(1)}, f32[16]{0:T(128)S(1)}, u32[]{:S(2)}, u32[]{:S(2)}) collective-permute-start(f32[16]{0:T(128)S(1)} %dynamic_slice.6), channel_id=1, source_target_pairs={{0,8},{4,12},{8,16},{12,20},{16,24},{20,28},{1,9},{5,13},{9,17},{1... | collective-permute-start | bytes 200 | tf_op jit(solution)/shard_map/ppermute | solution.py:30
  254.7 9.6 %copy-start.16 = (pred[4,128,128]{2,1,0:T(8,128)(4,1)S(1)}, pred[4,128,128]{2,1,0:T(8,128)(4,1)}, u32[]{:S(2)}) copy-start(pred[4,128,128]{2,1,0:T(8,128)(4,1)} %compare_and_fusion) | copy-start | bytes 196612
  264.1 4.0 %collective-permute-start.6 = (bf16[16,64,256]{2,1,0:T(8,128)(2,1)S(1)}, bf16[16,64,256]{2,1,0:T(8,128)(2,1)S(1)}, u32[]{:S(2)}, u32[]{:S(2)}) collective-permute-start(bf16[16,64,256]{2,1,0:T(8,128)(2,1)S(1)} %get-tuple-element.16), channel_id=1, source_target_pairs={{0,4},{4,0},{8,12},{12,8},{16,20},{20,16},{24,28},{28,24},{1,5},{5... | collective-permute-start | bytes 1572872 | tf_op jit(solution)/shard_map/ppermute | solution.py:30
  290.9 45.4 %copy-start.1 = (bf16[1,512,2048]{2,1,0:T(8,128)(2,1)S(1)}, bf16[1,512,2048]{2,1,0:T(8,128)(2,1)}, u32[]{:S(2)}) copy-start(bf16[1,512,2048]{2,1,0:T(8,128)(2,1)} %param.13) | copy-start | bytes 6291460
  (26 other events, 113.5 us)
Sparse Core Ops, SparseCore 0:
  291.0 45.2 reduce-scatter.1

commit v6 on v5

--- a/solution.py
+++ b/solution.py
@@ -188,7 +188,6 @@
         prior_gates.append(prior_gates[-1] * block_gates[b - 1])
     slab_state = block_gates[-1][:, None, None] * prior_states[-1] + block_states[-1]
     slab_gate = prior_gates[-1] * block_gates[-1]
-    slab_gate, slab_state, incoming_z = lax.optimization_barrier((slab_gate, slab_state, incoming_z))
     z_pack = placed(incoming_z)
     arriving = chain(slab_gate, slab_state, "ctx")
     entering = (

time: 345 us -> 344 us (level)
  local copies, waits for them, and re-layouts: 59.7 us -> 63.3 us
  transfers between devices with their start and end apart: 10 -> 10, of which waited for: 4 -> 4; matrix products, arithmetic and copies ran while one was open for 24% -> 25% of each run, Pallas kernels for 0% -> 0%
where the time goes in v6:
time: 344 us; the launch traced here: 342 us
  waiting for transfers between devices  133 us (39%)
  starting transfers between devices  67.4 us (20%)
  local copies, waits for them, and re-layouts  63.3 us (18%)
  other arithmetic  37.6 us (11%)
  matrix products  26.7 us (8%)
  between operations  13.9 us (4%)
    all_to_all x1, waiting for transfers between devices, body(): lax.all_to_all(outgoing(joined[None]), ('dp', 'ctx'), split_axis=0, conca...  74.5 us
    reduce_scatter x1, waiting for transfers between devices, body(): lax.psum_scatter(partial_value.astype(jnp.bfloat16), 'head', scatter_dime...  47.4 us
    ppermute x6, starting transfers between devices, across(): lax.ppermute((pair[0], pair[1].astype(jnp.bfloat16)), axis, route)  40.1 us
    all_to_all x1, starting transfers between devices, body(): lax.all_to_all(outgoing(gate_values), ('dp', 'ctx'), split_axis=0, concat...  16.5 us
    convert_element_type x2, local copies, waits for them, and re-layouts, body(): z_pack.astype(jnp.float32)  15.4 us
    dot_general x1, matrix products, body(): jnp.dot(normed, out_weight, preferred_element_type=jnp.float32)  14 us
    ppermute x6, waiting for transfers between devices, across(): lax.ppermute((pair[0], pair[1].astype(jnp.bfloat16)), axis, route)  11.5 us
    reshape x2, local copies, waits for them, and re-layouts, body(): x_blocks = x_conv.reshape(blocks, span, groups_local, per_group, width)  10.9 us
  transfers between devices with their start and end apart: 10, of which 4 were waited for; matrix products, arithmetic and copies ran while one was open for 25% of the time, Pallas kernels for 0%

profile of v6, /device:TPU:2, one launch (start us, length us, event | category | flops | bytes accessed | tf_op | source)
XLA Modules:
  0.0 342.3 jit_solution(7322942995187295135)
XLA Ops:
  10.6 3.0 pad_maximum_fusion
  13.6 5.8 %gather_fusion = bf16[64,16,3104]{2,1,0:T(8,128)(2,1)} fusion(bf16[32,16,3104]{2,1,0:T(8,128)(2,1)} %pad_maximum_fusion, s32[1024]{0:T(1024)S(1)} %pad_clamp_fusion), kind=kCustom, calls=%fused_computation | custom fusion | bytes 12714240 | tf_op jit(solution)/shard_map/gather | solution.py:111
  19.4 8.6 %all-to-all-start = ((bf16[32,2,16,3104]{3,2,1,0:T(8,128)(2,1)}), bf16[32,2,16,3104]{3,2,1,0:T(8,128)(2,1)}, u32[]{:S(2)}, u32[]{:S(2)}) async-start(bf16[32,2,16,3104]{3,2,1,0:T(8,128)(2,1)} %bitcast.124), calls=%async_computation | async-start | bytes 13107200 | tf_op jit(solution)/shard_map/all_to_all | solution.py:119
  33.2 74.5 %all-to-all-done = bf16[32,2,16,3104]{3,2,1,0:T(8,128)(2,1)} async-done(((bf16[32,2,16,3104]{3,2,1,0:T(8,128)(2,1)}), bf16[32,2,16,3104]{3,2,1,0:T(8,128)(2,1)}, u32[]{:S(2)}, u32[]{:S(2)}) %all-to-all-start) | async-done | bytes 6357024 | tf_op jit(solution)/shard_map/all_to_all | solution.py:119
  107.7 16.5 %all-to-all-start.1 = ((bf16[32,2,16,2048]{3,2,1,0:T(8,128)(2,1)}), bf16[32,2,16,2048]{3,2,1,0:T(8,128)(2,1)}, u32[]{:S(2)}, u32[]{:S(2)}) async-start(bf16[32,2,16,2048]{3,2,1,0:T(8,128)(2,1)} %bitcast.125), calls=%async_computation.1 | async-start | bytes 8388608 | tf_op jit(solution)/shard_map/all_to_all | solution.py:122
  124.2 5.4 %gather_fusion.1 = bf16[32,16,3104]{2,1,0:T(8,128)(2,1)} fusion(bf16[32,2,16,3104]{3,2,1,0:T(8,128)(2,1)} %all-to-all-done, s32[32]{0:T(128)S(1)} %fusion.52), kind=kCustom, calls=%fused_computation.1 | custom fusion | bytes 6357248 | tf_op jit(solution)/shard_map/gather | solution.py:128
  137.1 3.2 slice.170
  143.2 7.7 %multiply_convert_fusion.3 = bf16[512,2048]{1,0:T(8,128)(2,1)S(1)} fusion(bf16[512,2048]{1,0:T(8,128)(2,1)} %slice.170, bf16[3,2048]{1,0:T(4,128)(2,1)S(1)} %slice.173, f32[512]{0:T(512)S(1)} %get-tuple-element.22, f32[2048]{0:T(1024)} %bitcast.150, f32[512]{0:T(512)S(1)} %get-tuple-element.23, f32[2048]{0:T(1024)} %bitcast.151, ...), kind=kLoop, calls=%fused_computation.23 | loop fusion | flops 29360128 | bytes 4245504 | tf_op jit(solution)/shard_map/convert_element_type | solution.py:75
  150.9 5.3 %reshape.328 = bf16[4,128,2,16,64]{4,3,2,1,0:T(8,128)(2,1)} reshape(bf16[512,2048]{1,0:T(8,128)(2,1)S(1)} %multiply_convert_fusion.3) | data formatting | bytes 4194304 | tf_op jit(solution)/shard_map/reshape | solution.py:159
  156.2 5.6 %copy.72 = bf16[4,128,2,16,64]{1,4,3,2,0:T(8,128)(2,1)S(1)} copy(bf16[4,128,2,16,64]{4,3,2,1,0:T(8,128)(2,1)} %reshape.328) | data formatting | bytes 4194304 | tf_op jit(solution)/shard_map/reshape | solution.py:159
  161.8 3.0 multiply_convert_fusion.4
  165.7 4.6 %fusion.16 = f32[4,2,16,64,256]{4,3,2,1,0:T(8,128)} fusion(bf16[4,128,2,16,64]{1,4,3,2,0:T(8,128)(2,1)S(1)} %copy.72, f32[4,128,2,16]{1,3,2,0:T(8,128)S(1)} %get-tuple-element.34, bf16[4,128,2,256,1]{3,1,0,2,4:T(8,128)(2,1)S(1)} %bitcast.130), kind=kOutput, calls=%fused_computation.31 | convolution fusion | flops 540016640 | bytes 11075584 | tf_op jit(solution)/shard_map/bsghp,bsgn->bghpn/dot_general | solution.py:179
  170.3 7.3 %multiply_add_fusion = (f32[1,2,16,64,256]{4,3,2,1,0:T(8,128)}, f32[1,2,16,64,256]{4,3,2,1,0:T(8,128)}, f32[1,2,16,64,256]{4,3,2,1,0:T(8,128)}, f32[1,2,16,64,25...) fusion(f32[2,16]{1,0:T(2,128)S(1)} %copy-done.33, ...), kind=kLoop, calls=%fused_computation.44 | loop fusion | flops 2621440 | bytes 23069056 | tf_op jit(solution)/shard_map/add | solution.py:187
  180.1 27.1 %collective-permute-start.3 = (bf16[32,64,256]{2,1,0:T(8,128)(2,1)}, bf16[32,64,256]{2,1,0:T(8,128)(2,1)S(1)}, u32[]{:S(2)}, u32[]{:S(2)}) collective-permute-start(bf16[32,64,256]{2,1,0:T(8,128)(2,1)} %get-tuple-element.17), channel_id=1, source_target_pairs={{0,4},{4,0},{8,12},{12,8},{16,20},{20,16},{24,28},{28,24},{1,5},{5... | collective-permute-start | bytes 3145736 | tf_op jit(solution)/shard_map/ppermute | solution.py:30
  213.8 5.6 %collective-permute-start.4 = (bf16[16,64,256]{2,1,0:T(8,128)(2,1)}, bf16[16,64,256]{2,1,0:T(8,128)(2,1)}, u32[]{:S(2)}, u32[]{:S(2)}) collective-permute-start(bf16[16,64,256]{2,1,0:T(8,128)(2,1)} %get-tuple-element.15), channel_id=1, source_target_pairs={{0,8},{4,12},{8,16},{12,20},{16,24},{20,28},{1,9},{5,13},{9,17},{1... | collective-permute-start | bytes 1572872 | tf_op jit(solution)/shard_map/ppermute | solution.py:30
  219.7 4.2 %gather_fusion.3 = bf16[32,16,2048]{2,1,0:T(8,128)(2,1)} fusion(bf16[32,2,16,2048]{3,2,1,0:T(8,128)(2,1)} %all-to-all-done.1, s32[32]{0:T(128)S(1)} %fusion.52), kind=kCustom, calls=%fused_computation.3 | custom fusion | bytes 4194560 | tf_op jit(solution)/shard_map/gather | solution.py:128
  224.0 7.4 %reshape.290 = f32[4,128,2,16,64]{4,3,2,1,0:T(8,128)} reshape(bf16[32,16,2048]{2,1,0:T(8,128)(2,1)} %gather_fusion.3) | data formatting | bytes 6291456 | tf_op jit(solution)/shard_map/convert_element_type | solution.py:210
  231.4 8.0 %copy.80 = f32[4,128,2,16,64]{1,4,3,2,0:T(8,128)} copy(f32[4,128,2,16,64]{4,3,2,1,0:T(8,128)} %reshape.290) | data formatting | bytes 8388608 | tf_op jit(solution)/shard_map/convert_element_type | solution.py:210
  241.9 6.0 %collective-permute-start.5 = (bf16[16,64,256]{2,1,0:T(8,128)(2,1)}, bf16[16,64,256]{2,1,0:T(8,128)(2,1)}, u32[]{:S(2)}, u32[]{:S(2)}) collective-permute-start(bf16[16,64,256]{2,1,0:T(8,128)(2,1)} %fusion.27), channel_id=1, source_target_pairs={{0,16},{4,20},{8,24},{12,28},{1,17},{5,21},{9,25},{13,29},{2,18},{... | collective-permute-start | bytes 1572872 | tf_op jit(solution)/shard_map/ppermute | solution.py:30
  249.5 9.0 %collective-permute-done.2 = f32[16]{0:T(128)S(1)} collective-permute-done((f32[16]{0:T(128)S(1)}, f32[16]{0:T(128)S(1)}, u32[]{:S(2)}, u32[]{:S(2)}) %collective-permute-start.2) | collective-permute-done | bytes 96 | tf_op jit(solution)/shard_map/ppermute | solution.py:30
  261.6 3.7 %fusion.1 = f32[4,2,16,64,128]{4,3,2,1,0:T(8,128)S(1)} fusion(bf16[4,128,2,16,64]{1,4,3,2,0:T(8,128)(2,1)S(1)} %copy-done.4, f32[4,2,16,128]{3,2,1,0:T(8,128)S(1)} %bitcast.146, f32[4,2,128,128]{3,2,1,0:T(8,128)S(1)} %fusion.33, f32[4,2,16,128]{3,2,1,0:T(8,128)S(1)} %bitcast.145, pred[4,128,128]{2,1,0:T(8,128)(4,1)S(1)} %compare_and_fusion), kind=kOutput, calls=%fused_computation.10 | convolution fusion | flops 278921216 | bytes 7012352 | tf_op jit(solution)/shard_map/bghts,bsghp->btghp/dot_general | solution.py:172
  268.3 2.9 multiply_reduce_fusion
  274.1 14.0 %convolution_convert_fusion = bf16[512,4096]{1,0:T(8,128)(2,1)} fusion(bf16[2048,4096]{1,0:T(8,128)(2,1)} %param.23, bf16[256,8,4,128]{3,2,1,0:T(4,128)(2,1)S(1)} %bitcast.139), kind=kOutput, calls=%fused_computation.7 | convolution fusion | flops 8592031744 | bytes 23068672 | tf_op jit(solution)/shard_map/dot_general | solution.py:218
  288.1 47.4 %reduce-scatter.2.cloned.1.call-done = bf16[512,1024]{1,0:T(8,128)(2,1)} async-done(((bf16[512,4096]{1,0:T(8,128)(2,1)}), bf16[512,1024]{1,0:T(8,128)(2,1)}) %reduce-scatter.2.cloned.1.call-update) | async-done | bytes 1048592 | tf_op jit(solution)/shard_map/reduce_scatter | solution.py:219
  (160 shorter events, 42.5 us)
Async XLA Ops:
  6.5 21.8 %copy-start = (bf16[1,512,2048]{2,1,0:T(8,128)(2,1)S(1)}, bf16[1,512,2048]{2,1,0:T(8,128)(2,1)}, u32[]{:S(2)}) copy-start(bf16[1,512,2048]{2,1,0:T(8,128)(2,1)} %param.13) | copy-start | bytes 6291460
  19.4 8.7 %copy-start.19 = (s32[1,512]{1,0:T(1,128)S(1)}, s32[1,512]{1,0:T(1,128)}, u32[]{:S(2)}) copy-start(s32[1,512]{1,0:T(1,128)} %param.21) | copy-start | bytes 6148
  19.4 88.3 %all-to-all-start = ((bf16[32,2,16,3104]{3,2,1,0:T(8,128)(2,1)}), bf16[32,2,16,3104]{3,2,1,0:T(8,128)(2,1)}, u32[]{:S(2)}, u32[]{:S(2)}) async-start(bf16[32,2,16,3104]{3,2,1,0:T(8,128)(2,1)} %bitcast.124), calls=%async_computation | async-start | bytes 13107200 | tf_op jit(solution)/shard_map/all_to_all | solution.py:119
  107.7 112.0 %all-to-all-start.1 = ((bf16[32,2,16,2048]{3,2,1,0:T(8,128)(2,1)}), bf16[32,2,16,2048]{3,2,1,0:T(8,128)(2,1)}, u32[]{:S(2)}, u32[]{:S(2)}) async-start(bf16[32,2,16,2048]{3,2,1,0:T(8,128)(2,1)} %bitcast.125), calls=%async_computation.1 | async-start | bytes 8388608 | tf_op jit(solution)/shard_map/all_to_all | solution.py:122
  124.2 211.3 %reduce-scatter.2.cloned.1.call-start = ((), (), s32[]{:S(2)}) async-start(), calls=%async_computation.3 | async-start | bytes 5242880 | tf_op jit(solution)/shard_map/reduce_scatter | solution.py:219
  130.6 11.7 %collective-permute-start = (bf16[3,3105]{1,0:T(4,128)(2,1)S(1)}, bf16[3,3105]{1,0:T(4,128)(2,1)S(1)}, u32[]{:S(2)}, u32[]{:S(2)}) collective-permute-start(bf16[3,3105]{1,0:T(4,128)(2,1)S(1)} %pad_maximum_fusion.3), channel_id=1, source_target_pairs={{0,4},{4,8},{8,12},{12,16},{16,20},{20,24},{24,28},{1,5},{5,9},{9,... | collective-permute-start | bytes 55898 | tf_op jit(solution)/shard_map/ppermute | solution.py:15
  170.3 7.3 %copy-start.22 = (f32[32]{0:T(128)S(1)}, f32[32]{0:T(128)}, u32[]{:S(2)}) copy-start(f32[32]{0:T(128)} %get-tuple-element.55) | copy-start | bytes 388
  170.3 7.3 %copy-start.23 = (f32[32]{0:T(128)S(1)}, f32[32]{0:T(128)}, u32[]{:S(2)}) copy-start(f32[32]{0:T(128)} %get-tuple-element.46) | copy-start | bytes 388
  170.3 7.3 %copy-start.24 = (f32[32]{0:T(128)S(1)}, f32[32]{0:T(128)}, u32[]{:S(2)}) copy-start(f32[32]{0:T(128)} %get-tuple-element.49) | copy-start | bytes 388
  170.3 7.3 %copy-start.25 = (f32[32]{0:T(128)S(1)}, f32[32]{0:T(128)}, u32[]{:S(2)}) copy-start(f32[32]{0:T(128)} %get-tuple-element.50) | copy-start | bytes 388
  177.6 29.6 %copy-start.27 = (f32[32]{0:T(128)S(1)}, f32[32]{0:T(128)}, u32[]{:S(2)}) copy-start(f32[32]{0:T(128)} %get-tuple-element.54) | copy-start | bytes 388
  180.1 29.7 %collective-permute-start.3 = (bf16[32,64,256]{2,1,0:T(8,128)(2,1)}, bf16[32,64,256]{2,1,0:T(8,128)(2,1)S(1)}, u32[]{:S(2)}, u32[]{:S(2)}) collective-permute-start(bf16[32,64,256]{2,1,0:T(8,128)(2,1)} %get-tuple-element.17), channel_id=1, source_target_pairs={{0,4},{4,0},{8,12},{12,8},{16,20},{20,16},{24,28},{28,24},{1,5},{5... | collective-permute-start | bytes 3145736 | tf_op jit(solution)/shard_map/ppermute | solution.py:30
  207.2 2.5 collective-permute-start.1
  212.4 7.0 %copy-start.35 = (f32[32]{0:T(128)S(1)}, f32[32]{0:T(128)}, u32[]{:S(2)}) copy-start(f32[32]{0:T(128)} %param.17) | copy-start | bytes 388
  212.4 7.1 %copy-start.21 = (f32[2048]{0:T(1024)S(1)}, f32[2048]{0:T(1024)}, u32[]{:S(2)}) copy-start(f32[2048]{0:T(1024)} %param.22) | copy-start | bytes 24580
  213.8 25.7 %collective-permute-start.4 = (bf16[16,64,256]{2,1,0:T(8,128)(2,1)}, bf16[16,64,256]{2,1,0:T(8,128)(2,1)}, u32[]{:S(2)}, u32[]{:S(2)}) collective-permute-start(bf16[16,64,256]{2,1,0:T(8,128)(2,1)} %get-tuple-element.15), channel_id=1, source_target_pairs={{0,8},{4,12},{8,16},{12,20},{16,24},{20,28},{1,9},{5,13},{9,17},{1... | collective-permute-start | bytes 1572872 | tf_op jit(solution)/shard_map/ppermute | solution.py:30
  239.4 8.5 %copy-start.28 = (f32[1,32]{1,0:T(1,128)S(1)}, f32[1,32]{1,0:T(1,128)}, u32[]{:S(2)}) copy-start(f32[1,32]{1,0:T(1,128)} %get-tuple-element.45) | copy-start | bytes 388
  239.4 8.5 %copy-start.29 = (f32[1,32]{1,0:T(1,128)S(1)}, f32[1,32]{1,0:T(1,128)}, u32[]{:S(2)}) copy-start(f32[1,32]{1,0:T(1,128)} %get-tuple-element.47) | copy-start | bytes 388
  239.4 8.5 %copy-start.30 = (f32[1,32]{1,0:T(1,128)S(1)}, f32[1,32]{1,0:T(1,128)}, u32[]{:S(2)}) copy-start(f32[1,32]{1,0:T(1,128)} %get-tuple-element.48) | copy-start | bytes 388
  239.4 8.6 %copy-start.8 = (f32[512,32]{1,0:T(8,128)S(1)}, f32[512,32]{1,0:T(8,128)}, u32[]{:S(2)}) copy-start(f32[512,32]{1,0:T(8,128)} %copy-done.7) | copy-start | bytes 196612
  241.9 18.2 %collective-permute-start.5 = (bf16[16,64,256]{2,1,0:T(8,128)(2,1)}, bf16[16,64,256]{2,1,0:T(8,128)(2,1)}, u32[]{:S(2)}, u32[]{:S(2)}) collective-permute-start(bf16[16,64,256]{2,1,0:T(8,128)(2,1)} %fusion.27), channel_id=1, source_target_pairs={{0,16},{4,20},{8,24},{12,28},{1,17},{5,21},{9,25},{13,29},{2,18},{... | collective-permute-start | bytes 1572872 | tf_op jit(solution)/shard_map/ppermute | solution.py:30
  248.1 10.4 %collective-permute-start.2 = (f32[16]{0:T(128)S(1)}, f32[16]{0:T(128)S(1)}, u32[]{:S(2)}, u32[]{:S(2)}) collective-permute-start(f32[16]{0:T(128)S(1)} %dynamic_slice.6), channel_id=1, source_target_pairs={{0,8},{4,12},{8,16},{12,20},{16,24},{20,28},{1,9},{5,13},{9,17},{1... | collective-permute-start | bytes 200 | tf_op jit(solution)/shard_map/ppermute | solution.py:30
  261.5 3.8 %collective-permute-start.6 = (bf16[16,64,256]{2,1,0:T(8,128)(2,1)S(1)}, bf16[16,64,256]{2,1,0:T(8,128)(2,1)S(1)}, u32[]{:S(2)}, u32[]{:S(2)}) collective-permute-start(bf16[16,64,256]{2,1,0:T(8,128)(2,1)S(1)} %get-tuple-element.10), channel_id=1, source_target_pairs={{0,4},{4,0},{8,12},{12,8},{16,20},{20,16},{24,28},{28,24},{1,5},{5... | collective-permute-start | bytes 1572872 | tf_op jit(solution)/shard_map/ppermute | solution.py:30
  288.1 47.4 %copy-start.1 = (bf16[1,512,2048]{2,1,0:T(8,128)(2,1)S(1)}, bf16[1,512,2048]{2,1,0:T(8,128)(2,1)}, u32[]{:S(2)}) copy-start(bf16[1,512,2048]{2,1,0:T(8,128)(2,1)} %param.13) | copy-start | bytes 6291460
  (23 other events, 73.5 us)
Sparse Core Ops, SparseCore 0:
  288.2 47.2 reduce-scatter.1

commit v7 on v6

--- a/solution.py
+++ b/solution.py
@@ -130,11 +130,19 @@
     joined_pack = placed(incoming)
     margin = conv_values.shape[0] - 1
     flags = doc_start[0].astype(jnp.bfloat16)
-    rim = passed_along(
-        jnp.concatenate([joined_pack[rows - margin :], flags[rows - margin :, None]], axis=1),
-        "ctx",
-        1,
-    )
+    edges = lax.all_gather(
+        jnp.concatenate([joined[rows - margin :], flags[rows - margin :, None]], axis=1),
+        ("dp", "ctx"),
+    )
+    earlier = lax.axis_index("ctx") > 0
+    rim = jnp.concatenate(
+        [
+            edges[(myself - 1 - piece_shift[slots - 1]) % owners, :, :-1],
+            edges[(myself - 1) % owners, :, -1:],
+        ],
+        axis=1,
+    )
+    rim = jnp.where(earlier, rim, jnp.zeros_like(rim))
     rim_x = rim[:, :features]
     rim_maps = rim[:, features : features + map_width].reshape((margin,) + map_shape)
     rim_flags = rim[:, -1]

time: 344 us -> 334 us (0.971)
  blocking collectives: 0 us -> 104 us
  waiting for transfers between devices: 133 us -> 57.2 us
  starting transfers between devices: 67.4 us -> 26 us
    all_gather x0 -> x1, blocking collectives: none -> 104 us  [body(): lax.all_gather(jnp.concatenate([joined[rows - margin:], flags[rows - marg...]
    all_to_all x1, waiting for transfers between devices: 74.5 us -> 0.01 us  [body(): lax.all_to_all(outgoing(joined[None]), ('dp', 'ctx'), split_axis=0, conca...]
    ppermute x6, starting transfers between devices: 40.1 us -> 10.9 us  [across(): lax.ppermute((pair[0], pair[1].astype(jnp.bfloat16)), axis, route)]
    all_to_all x1, starting transfers between devices: 16.5 us -> 6.24 us  [body(): lax.all_to_all(outgoing(gate_values), ('dp', 'ctx'), split_axis=0, concat...]
    ppermute x6, waiting for transfers between devices: 11.5 us -> 7.8 us  [across(): lax.ppermute((pair[0], pair[1].astype(jnp.bfloat16)), axis, route)]
  transfers between devices with their start and end apart: 10 -> 9, of which waited for: 4 -> 3; matrix products, arithmetic and copies ran while one was open for 25% -> 27% of each run, Pallas kernels for 0% -> 0%
where the time goes in v7:
time: 334 us; the launch traced here: 332 us
  blocking collectives  104 us (31%)
  local copies, waits for them, and re-layouts  64.8 us (19%)
  waiting for transfers between devices  57.2 us (17%)
  other arithmetic  38.8 us (12%)
  matrix products  26.6 us (8%)
  starting transfers between devices  26 us (8%)
  between operations  14.5 us (4%)
    all_gather x1, blocking collectives, body(): lax.all_gather(jnp.concatenate([joined[rows - margin:], flags[rows - marg...  104 us
    reduce_scatter x1, waiting for transfers between devices, body(): lax.psum_scatter(partial_value.astype(jnp.bfloat16), 'head', scatter_dime...  49.4 us
    convert_element_type x2, local copies, waits for them, and re-layouts, body(): z_pack.astype(jnp.float32)  15.4 us
    dot_general x1, matrix products, body(): jnp.dot(normed, out_weight, preferred_element_type=jnp.float32)  13.9 us
    reshape x2, local copies, waits for them, and re-layouts, body(): x_blocks = x_conv.reshape(blocks, span, groups_local, per_group, width)  10.9 us
    ppermute x6, starting transfers between devices, across(): lax.ppermute((pair[0], pair[1].astype(jnp.bfloat16)), axis, route)  10.9 us
    convert_element_type x2, other arithmetic, conv_core(): return jax.nn.silu(summed).astype(jnp.bfloat16)  10.2 us
    gather x2, local copies, waits for them, and re-layouts, placed(): return received[source, ranking].reshape((rows,) + received.shape[3:])  9.67 us
  transfers between devices with their start and end apart: 9, of which 3 were waited for; matrix products, arithmetic and copies ran while one was open for 27% of the time, Pallas kernels for 0%

profile of v7, /device:TPU:2, one launch (start us, length us, event | category | flops | bytes accessed | tf_op | source)
XLA Modules:
  0.0 332.2 jit_solution(16725210890099659982)
XLA Ops:
  11.4 3.1 pad_maximum_fusion
  14.5 5.9 %gather_fusion = bf16[64,16,3104]{2,1,0:T(8,128)(2,1)} fusion(bf16[32,16,3104]{2,1,0:T(8,128)(2,1)} %pad_maximum_fusion, s32[1024]{0:T(1024)S(1)} %pad_clamp_fusion), kind=kCustom, calls=%fused_computation | custom fusion | bytes 12714240 | tf_op jit(solution)/shard_map/gather | solution.py:111
  20.4 8.6 %all-to-all-start = ((bf16[32,2,16,3104]{3,2,1,0:T(8,128)(2,1)}), bf16[32,2,16,3104]{3,2,1,0:T(8,128)(2,1)}, u32[]{:S(2)}, u32[]{:S(2)}) async-start(bf16[32,2,16,3104]{3,2,1,0:T(8,128)(2,1)} %bitcast.133), calls=%async_computation | async-start | bytes 13107200 | tf_op jit(solution)/shard_map/all_to_all | solution.py:119
  32.6 104.2 %all-gather.1 = bf16[32,3,3105]{2,1,0:T(4,128)(2,1)S(1)} all-gather(bf16[1,3,3105]{2,1,0:T(4,128)(2,1)S(1)} %fusion.42), channel_id=2, replica_groups=mesh['dp'=4,'ctx'=8,'head'=4] {'dp','ctx'}, dimensions={0}, use_global_device_ids=true | all-gather | bytes 614790 | tf_op jit(solution)/shard_map/all_gather | solution.py:133
  137.6 2.8 gather_fusion.2
  141.2 6.2 %all-to-all-start.1 = ((bf16[32,2,16,2048]{3,2,1,0:T(8,128)(2,1)}), bf16[32,2,16,2048]{3,2,1,0:T(8,128)(2,1)}, u32[]{:S(2)}, u32[]{:S(2)}) async-start(bf16[32,2,16,2048]{3,2,1,0:T(8,128)(2,1)} %bitcast.134), calls=%async_computation.1 | async-start | bytes 8388608 | tf_op jit(solution)/shard_map/all_to_all | solution.py:122
  147.7 5.5 %gather_fusion.1 = bf16[32,16,3104]{2,1,0:T(8,128)(2,1)} fusion(bf16[32,2,16,3104]{3,2,1,0:T(8,128)(2,1)} %all-to-all-done, s32[32]{0:T(128)S(1)} %fusion.55), kind=kCustom, calls=%fused_computation.1 | custom fusion | bytes 6357248 | tf_op jit(solution)/shard_map/gather | solution.py:128
  154.5 3.2 slice.174
  161.8 7.8 %multiply_convert_fusion.3 = bf16[512,2048]{1,0:T(8,128)(2,1)S(1)} fusion(bf16[512,2048]{1,0:T(8,128)(2,1)} %slice.174, bf16[3,2048]{1,0:T(4,128)(2,1)S(1)} %slice-done, f32[512]{0:T(512)S(1)} %get-tuple-element.22, f32[2048]{0:T(1024)S(1)} %bitcast.161, f32[512]{0:T(512)S(1)} %get-tuple-element.23, f32[2048]{0:T(1024)S(1)} %bitcast.162, ...), kind=kLoop, calls=%fused_computation.23 | loop fusion | flops 29360128 | bytes 4245504 | tf_op jit(solution)/shard_map/convert_element_type | solution.py:75
  169.5 5.3 %reshape.334 = bf16[4,128,2,16,64]{4,3,2,1,0:T(8,128)(2,1)} reshape(bf16[512,2048]{1,0:T(8,128)(2,1)S(1)} %multiply_convert_fusion.3) | data formatting | bytes 4194304 | tf_op jit(solution)/shard_map/reshape | solution.py:167
  174.9 5.6 %copy.129 = bf16[4,128,2,16,64]{1,4,3,2,0:T(8,128)(2,1)S(1)} copy(bf16[4,128,2,16,64]{4,3,2,1,0:T(8,128)(2,1)} %reshape.334) | data formatting | bytes 4194304 | tf_op jit(solution)/shard_map/reshape | solution.py:167
  182.8 4.6 %fusion.16 = f32[4,2,16,64,256]{4,3,2,1,0:T(8,128)} fusion(bf16[4,128,2,16,64]{1,4,3,2,0:T(8,128)(2,1)S(1)} %copy.129, f32[4,128,2,16]{1,3,2,0:T(8,128)S(1)} %get-tuple-element.34, bf16[4,128,2,256,1]{3,1,0,2,4:T(8,128)(2,1)S(1)} %bitcast.140), kind=kOutput, calls=%fused_computation.31 | convolution fusion | flops 540016640 | bytes 11075584 | tf_op jit(solution)/shard_map/bsghp,bsgn->bghpn/dot_general | solution.py:187
  187.4 7.9 %multiply_add_fusion = (f32[1,2,16,64,256]{4,3,2,1,0:T(8,128)}, f32[1,2,16,64,256]{4,3,2,1,0:T(8,128)}, f32[1,2,16,64,256]{4,3,2,1,0:T(8,128)}, f32[1,2,16,64,25...) fusion(f32[2,16]{1,0:T(2,128)S(1)} %mul.481, ...), kind=kLoop, calls=%fused_computation.44 | loop fusion | flops 2621440 | bytes 23069056 | tf_op jit(solution)/shard_map/add | solution.py:195
  195.3 3.7 %fusion.62 = (bf16[32,64,256]{2,1,0:T(8,128)(2,1)S(1)}, f32[32,64,256]{2,1,0:T(8,128)}) fusion(f32[1,2,16,64,256]{4,3,2,1,0:T(8,128)} %get-tuple-element.27, f32[1,2,16,64,256]{4,3,2,1,0:T(8,128)S(1)} %get-tuple-element.26, f32[1,2,16,64,256]{4,3,2,1,0:T(8,128)S(1)} %get-tuple-element.25, f32[1,2,16,64,256]{4,3,2,1,0:T(8,128)S(1)} %get-tuple-element.24, ...), kind=kLoop, calls=%fused_computation.155 | loop fusion | flops 4194304 | bytes 11534848 | tf_op jit(solution)/shard_map/convert_element_type | solution.py:30
  205.8 4.4 %collective-permute-start.3 = (bf16[16,64,256]{2,1,0:T(8,128)(2,1)}, bf16[16,64,256]{2,1,0:T(8,128)(2,1)}, u32[]{:S(2)}, u32[]{:S(2)}) collective-permute-start(bf16[16,64,256]{2,1,0:T(8,128)(2,1)} %get-tuple-element.15), channel_id=1, source_target_pairs={{0,8},{4,12},{8,16},{12,20},{16,24},{20,28},{1,9},{5,13},{9,17},{1... | collective-permute-start | bytes 1572872 | tf_op jit(solution)/shard_map/ppermute | solution.py:30
  210.5 4.2 %gather_fusion.3 = bf16[32,16,2048]{2,1,0:T(8,128)(2,1)} fusion(bf16[32,2,16,2048]{3,2,1,0:T(8,128)(2,1)} %all-to-all-done.1, s32[32]{0:T(128)S(1)} %fusion.55), kind=kCustom, calls=%fused_computation.3 | custom fusion | bytes 4194560 | tf_op jit(solution)/shard_map/gather | solution.py:128
  214.7 7.4 %reshape.290 = f32[4,128,2,16,64]{4,3,2,1,0:T(8,128)} reshape(bf16[32,16,2048]{2,1,0:T(8,128)(2,1)} %gather_fusion.3) | data formatting | bytes 6291456 | tf_op jit(solution)/shard_map/convert_element_type | solution.py:218
  222.1 8.0 %copy.137 = f32[4,128,2,16,64]{1,4,3,2,0:T(8,128)} copy(f32[4,128,2,16,64]{4,3,2,1,0:T(8,128)} %reshape.290) | data formatting | bytes 8388608 | tf_op jit(solution)/shard_map/convert_element_type | solution.py:218
  232.6 4.6 %collective-permute-start.4 = (bf16[16,64,256]{2,1,0:T(8,128)(2,1)}, bf16[16,64,256]{2,1,0:T(8,128)(2,1)}, u32[]{:S(2)}, u32[]{:S(2)}) collective-permute-start(bf16[16,64,256]{2,1,0:T(8,128)(2,1)} %fusion.29), channel_id=1, source_target_pairs={{0,16},{4,20},{8,24},{12,28},{1,17},{5,21},{9,25},{13,29},{2,18},{... | collective-permute-start | bytes 1572872 | tf_op jit(solution)/shard_map/ppermute | solution.py:30
  242.3 5.6 %collective-permute-done.1 = f32[16]{0:T(128)S(1)} collective-permute-done((f32[16]{0:T(128)S(1)}, f32[16]{0:T(128)S(1)}, u32[]{:S(2)}, u32[]{:S(2)}) %collective-permute-start.1) | collective-permute-done | bytes 96 | tf_op jit(solution)/shard_map/ppermute | solution.py:30
  249.5 3.7 %fusion.1 = f32[4,2,16,64,128]{4,3,2,1,0:T(8,128)S(1)} fusion(bf16[4,128,2,16,64]{1,4,3,2,0:T(8,128)(2,1)S(1)} %copy-done.4, f32[4,2,16,128]{3,2,1,0:T(8,128)S(1)} %bitcast.158, f32[4,2,128,128]{3,2,1,0:T(8,128)S(1)} %fusion.33, f32[4,2,16,128]{3,2,1,0:T(8,128)S(1)} %bitcast.157, pred[4,128,128]{2,1,0:T(8,128)(4,1)S(1)} %compare_and_fusion), kind=kOutput, calls=%fused_computation.10 | convolution fusion | flops 278921216 | bytes 7012352 | tf_op jit(solution)/shard_map/bghts,bsghp->btghp/dot_general | solution.py:180
  256.2 2.9 multiply_reduce_fusion
  262.0 13.9 %convolution_convert_fusion = bf16[512,4096]{1,0:T(8,128)(2,1)} fusion(bf16[2048,4096]{1,0:T(8,128)(2,1)} %param.23, bf16[256,8,4,128]{3,2,1,0:T(4,128)(2,1)S(1)} %bitcast.151), kind=kOutput, calls=%fused_computation.7 | convolution fusion | flops 8592031744 | bytes 23068672 | tf_op jit(solution)/shard_map/dot_general | solution.py:226
  275.9 49.4 %reduce-scatter.2.cloned.1.call-done = bf16[512,1024]{1,0:T(8,128)(2,1)} async-done(((bf16[512,4096]{1,0:T(8,128)(2,1)}), bf16[512,1024]{1,0:T(8,128)(2,1)}) %reduce-scatter.2.cloned.1.call-update) | async-done | bytes 1048592 | tf_op jit(solution)/shard_map/reduce_scatter | solution.py:227
  (134 shorter events, 38.9 us)
Async XLA Ops:
  6.5 131.0 %copy-start = (bf16[1,512,2048]{2,1,0:T(8,128)(2,1)S(1)}, bf16[1,512,2048]{2,1,0:T(8,128)(2,1)}, u32[]{:S(2)}) copy-start(bf16[1,512,2048]{2,1,0:T(8,128)(2,1)} %param.13) | copy-start | bytes 6291460
  20.4 8.7 %copy-start.17 = (s32[32]{0:T(128)S(1)}, s32[32]{0:T(128)}, u32[]{:S(2)}) copy-start(s32[32]{0:T(128)} %param.20) | copy-start | bytes 388
  20.4 10.0 %copy-start.6 = (bf16[1,512,2,512]{3,2,1,0:T(2,128)(2,1)S(1)}, bf16[1,512,2,512]{3,2,1,0:T(2,128)(2,1)}, u32[]{:S(2)}) copy-start(bf16[1,512,2,512]{3,2,1,0:T(2,128)(2,1)} %param.14) | copy-start | bytes 3145732
  20.4 120.8 %all-to-all-start = ((bf16[32,2,16,3104]{3,2,1,0:T(8,128)(2,1)}), bf16[32,2,16,3104]{3,2,1,0:T(8,128)(2,1)}, u32[]{:S(2)}, u32[]{:S(2)}) async-start(bf16[32,2,16,3104]{3,2,1,0:T(8,128)(2,1)} %bitcast.133), calls=%async_computation | async-start | bytes 13107200 | tf_op jit(solution)/shard_map/all_to_all | solution.py:119
  137.0 3.3 copy-start.12
  137.5 3.4 %copy-start.18 = (f32[32]{0:T(128)S(1)}, f32[32]{0:T(128)}, u32[]{:S(2)}) copy-start(f32[32]{0:T(128)} %param.16) | copy-start | bytes 388
  137.5 3.6 %copy-start.15 = (f32[4,2,512]{2,1,0:T(2,128)S(1)}, f32[4,2,512]{2,1,0:T(2,128)}, u32[]{:S(2)}) copy-start(f32[4,2,512]{2,1,0:T(2,128)} %param.19) | copy-start | bytes 49156
  137.5 3.6 %copy-start.13 = (f32[4,2048]{1,0:T(4,128)S(1)}, f32[4,2048]{1,0:T(4,128)}, u32[]{:S(2)}) copy-start(f32[4,2048]{1,0:T(4,128)} %param.18) | copy-start | bytes 98308
  141.2 69.3 %all-to-all-start.1 = ((bf16[32,2,16,2048]{3,2,1,0:T(8,128)(2,1)}), bf16[32,2,16,2048]{3,2,1,0:T(8,128)(2,1)}, u32[]{:S(2)}, u32[]{:S(2)}) async-start(bf16[32,2,16,2048]{3,2,1,0:T(8,128)(2,1)} %bitcast.134), calls=%async_computation.1 | async-start | bytes 8388608 | tf_op jit(solution)/shard_map/all_to_all | solution.py:122
  147.4 177.9 %reduce-scatter.2.cloned.1.call-start = ((), (), s32[]{:S(2)}) async-start(), calls=%async_computation.3 | async-start | bytes 5242880 | tf_op jit(solution)/shard_map/reduce_scatter | solution.py:227
  180.5 6.9 %copy-start.3 = (bf16[4,128,2,16,64]{1,4,3,2,0:T(8,128)(2,1)}, bf16[4,128,2,16,64]{1,4,3,2,0:T(8,128)(2,1)S(1)}, u32[]{:S(2)}) copy-start(bf16[4,128,2,16,64]{1,4,3,2,0:T(8,128)(2,1)S(1)} %copy.129) | copy-start | bytes 6291460
  199.1 2.7 collective-permute-start.2
  199.2 2.5 collective-permute-start
  199.6 3.2 copy-start.2
  204.4 5.8 %copy-start.19 = (f32[32]{0:T(128)S(1)}, f32[32]{0:T(128)}, u32[]{:S(2)}) copy-start(f32[32]{0:T(128)} %param.17) | copy-start | bytes 388
  204.4 5.9 %copy-start.16 = (f32[2048]{0:T(1024)S(1)}, f32[2048]{0:T(1024)}, u32[]{:S(2)}) copy-start(f32[2048]{0:T(1024)} %param.22) | copy-start | bytes 24580
  205.8 24.4 %collective-permute-start.3 = (bf16[16,64,256]{2,1,0:T(8,128)(2,1)}, bf16[16,64,256]{2,1,0:T(8,128)(2,1)}, u32[]{:S(2)}, u32[]{:S(2)}) collective-permute-start(bf16[16,64,256]{2,1,0:T(8,128)(2,1)} %get-tuple-element.15), channel_id=1, source_target_pairs={{0,8},{4,12},{8,16},{12,20},{16,24},{20,28},{1,9},{5,13},{9,17},{1... | collective-permute-start | bytes 1572872 | tf_op jit(solution)/shard_map/ppermute | solution.py:30
  232.6 15.3 %collective-permute-start.4 = (bf16[16,64,256]{2,1,0:T(8,128)(2,1)}, bf16[16,64,256]{2,1,0:T(8,128)(2,1)}, u32[]{:S(2)}, u32[]{:S(2)}) collective-permute-start(bf16[16,64,256]{2,1,0:T(8,128)(2,1)} %fusion.29), channel_id=1, source_target_pairs={{0,16},{4,20},{8,24},{12,28},{1,17},{5,21},{9,25},{13,29},{2,18},{... | collective-permute-start | bytes 1572872 | tf_op jit(solution)/shard_map/ppermute | solution.py:30
  240.9 7.0 %collective-permute-start.1 = (f32[16]{0:T(128)S(1)}, f32[16]{0:T(128)S(1)}, u32[]{:S(2)}, u32[]{:S(2)}) collective-permute-start(f32[16]{0:T(128)S(1)} %dynamic_slice.14), channel_id=1, source_target_pairs={{0,8},{4,12},{8,16},{12,20},{16,24},{20,28},{1,9},{5,13},{9,17},{1... | collective-permute-start | bytes 200 | tf_op jit(solution)/shard_map/ppermute | solution.py:30
  242.3 7.2 %copy-start.4 = (bf16[4,128,2,16,64]{1,4,3,2,0:T(8,128)(2,1)S(1)}, bf16[4,128,2,16,64]{1,4,3,2,0:T(8,128)(2,1)}, u32[]{:S(2)}) copy-start(bf16[4,128,2,16,64]{1,4,3,2,0:T(8,128)(2,1)} %copy-done.3) | copy-start | bytes 6291460
  249.3 3.8 %collective-permute-start.5 = (bf16[16,64,256]{2,1,0:T(8,128)(2,1)S(1)}, bf16[16,64,256]{2,1,0:T(8,128)(2,1)S(1)}, u32[]{:S(2)}, u32[]{:S(2)}) collective-permute-start(bf16[16,64,256]{2,1,0:T(8,128)(2,1)S(1)} %get-tuple-element.10), channel_id=1, source_target_pairs={{0,4},{4,0},{8,12},{12,8},{16,20},{20,16},{24,28},{28,24},{1,5},{5... | collective-permute-start | bytes 1572872 | tf_op jit(solution)/shard_map/ppermute | solution.py:30
  249.4 4.4 %copy-start.9 = (f32[1,2,16,64,256]{4,3,2,1,0:T(8,128)S(1)}, f32[1,2,16,64,256]{4,3,2,1,0:T(8,128)}, u32[]{:S(2)}) copy-start(f32[1,2,16,64,256]{4,3,2,1,0:T(8,128)} %get-tuple-element.20) | copy-start | bytes 6291460
  249.5 4.4 %copy-start.10 = (f32[1,2,16,64,256]{4,3,2,1,0:T(8,128)S(1)}, f32[1,2,16,64,256]{4,3,2,1,0:T(8,128)}, u32[]{:S(2)}) copy-start(f32[1,2,16,64,256]{4,3,2,1,0:T(8,128)} %get-tuple-element.21) | copy-start | bytes 6291460
  275.9 49.4 %copy-start.1 = (bf16[1,512,2048]{2,1,0:T(8,128)(2,1)S(1)}, bf16[1,512,2048]{2,1,0:T(8,128)(2,1)}, u32[]{:S(2)}) copy-start(bf16[1,512,2048]{2,1,0:T(8,128)(2,1)} %param.13) | copy-start | bytes 6291460
  (6 other events, 10.8 us)
Sparse Core Ops, SparseCore 0:
  276.0 49.2 reduce-scatter.1

commit v8 on v7

--- a/solution.py
+++ b/solution.py
@@ -116,24 +116,33 @@
     joined = jnp.concatenate(
         [token_values[0], state_maps[0].reshape(rows, map_width), step_raw[0]], axis=1
     )
-    incoming = lax.all_to_all(
-        outgoing(joined[None]), ("dp", "ctx"), split_axis=0, concat_axis=0, tiled=True
-    )
-    incoming_z = lax.all_to_all(
-        outgoing(gate_values), ("dp", "ctx"), split_axis=0, concat_axis=0, tiled=True
-    )
-    source = (myself - piece_shift) % owners
-
-    def placed(received):
-        return received[source, ranking].reshape((rows,) + received.shape[3:])
-
-    joined_pack = placed(incoming)
     margin = conv_values.shape[0] - 1
     flags = doc_start[0].astype(jnp.bfloat16)
     edges = lax.all_gather(
-        jnp.concatenate([joined[rows - margin :], flags[rows - margin :, None]], axis=1),
+        jnp.concatenate(
+            [
+                token_values[0, rows - margin :],
+                state_maps[0, rows - margin :].reshape(margin, map_width),
+                step_raw[0, rows - margin :],
+                flags[rows - margin :, None],
+            ],
+            axis=1,
+        ),
         ("dp", "ctx"),
     )
+    edges, joined = lax.optimization_barrier((edges, joined))
+    incoming = lax.all_to_all(
+        outgoing(joined[None]), ("dp", "ctx"), split_axis=0, concat_axis=0, tiled=True
+    )
+    incoming_z = lax.all_to_all(
+        outgoing(gate_values), ("dp", "ctx"), split_axis=0, concat_axis=0, tiled=True
+    )
+    source = (myself - piece_shift) % owners
+
+    def placed(received):
+        return received[source, ranking].reshape((rows,) + received.shape[3:])
+
+    joined_pack = placed(incoming)
     earlier = lax.axis_index("ctx") > 0
     rim = jnp.concatenate(
         [

time: 334 us -> 337 us (level)
  blocking collectives: 104 us -> 28.1 us
  waiting for transfers between devices: 57.2 us -> 130 us
  starting transfers between devices: 26 us -> 33.4 us
    all_gather x1, blocking collectives: 104 us -> 28.1 us  [body(): lax.all_gather(jnp.concatenate([token_values[0, rows - margin:], state_ma...]
    all_to_all x1, waiting for transfers between devices: 0.01 us -> 72.6 us  [body(): lax.all_to_all(outgoing(joined[None]), ('dp', 'ctx'), split_axis=0, conca...]
    all_to_all x1, starting transfers between devices: 6.24 us -> 16.5 us  [body(): lax.all_to_all(outgoing(gate_values), ('dp', 'ctx'), split_axis=0, concat...]
  transfers between devices with their start and end apart: 9 -> 9, of which waited for: 3 -> 4; matrix products, arithmetic and copies ran while one was open for 27% -> 26% of each run, Pallas kernels for 0% -> 0%
where the time goes in v8:
time: 337 us; the launch traced here: 335 us
  waiting for transfers between devices  130 us (39%)
  local copies, waits for them, and re-layouts  65.7 us (19%)
  other arithmetic  36.6 us (11%)
  starting transfers between devices  33.4 us (10%)
  blocking collectives  28.1 us (8%)
  matrix products  26.6 us (8%)
  between operations  14.5 us (4%)
    all_to_all x1, waiting for transfers between devices, body(): lax.all_to_all(outgoing(joined[None]), ('dp', 'ctx'), split_axis=0, conca...  72.6 us
    reduce_scatter x1, waiting for transfers between devices, body(): lax.psum_scatter(partial_value.astype(jnp.bfloat16), 'head', scatter_dime...  49.4 us
    all_gather x1, blocking collectives, body(): lax.all_gather(jnp.concatenate([token_values[0, rows - margin:], state_ma...  28.1 us
    all_to_all x1, starting transfers between devices, body(): lax.all_to_all(outgoing(gate_values), ('dp', 'ctx'), split_axis=0, concat...  16.5 us
    convert_element_type x2, local copies, waits for them, and re-layouts, body(): z_pack.astype(jnp.float32)  15.4 us
    dot_general x1, matrix products, body(): jnp.dot(normed, out_weight, preferred_element_type=jnp.float32)  13.9 us
    reshape x2, local copies, waits for them, and re-layouts, body(): x_blocks = x_conv.reshape(blocks, span, groups_local, per_group, width)  10.9 us
    ppermute x6, starting transfers between devices, across(): lax.ppermute((pair[0], pair[1].astype(jnp.bfloat16)), axis, route)  10.9 us
  transfers between devices with their start and end apart: 9, of which 4 were waited for; matrix products, arithmetic and copies ran while one was open for 26% of the time, Pallas kernels for 0%

profile of v8, /device:TPU:2, one launch (start us, length us, event | category | flops | bytes accessed | tf_op | source)
XLA Modules:
  0.0 334.7 jit_solution(9366638549189763853)
XLA Ops:
  10.2 28.1 %all-gather.1 = bf16[32,3,3105]{2,1,0:T(4,128)(2,1)} all-gather(bf16[1,3,3105]{2,1,0:T(4,128)(2,1)S(1)} %bitcast.160), channel_id=2, replica_groups=mesh['dp'=4,'ctx'=8,'head'=4] {'dp','ctx'}, dimensions={0}, use_global_device_ids=true | all-gather | bytes 614790 | tf_op jit(solution)/shard_map/all_gather | solution.py:121
  38.4 3.1 pad_maximum_fusion
  42.1 5.9 %gather_fusion = bf16[64,16,3104]{2,1,0:T(8,128)(2,1)} fusion(bf16[32,16,3104]{2,1,0:T(8,128)(2,1)} %bitcast.138, s32[1024]{0:T(1024)S(1)} %pad_clamp_fusion), kind=kCustom, calls=%fused_computation | custom fusion | bytes 12714240 | tf_op jit(solution)/shard_map/gather | solution.py:111
  48.0 5.8 %all-to-all-start = ((bf16[32,2,16,3104]{3,2,1,0:T(8,128)(2,1)}), bf16[32,2,16,3104]{3,2,1,0:T(8,128)(2,1)}, u32[]{:S(2)}, u32[]{:S(2)}) async-start(bf16[32,2,16,3104]{3,2,1,0:T(8,128)(2,1)} %bitcast.139), calls=%async_computation | async-start | bytes 13107200 | tf_op jit(solution)/shard_map/all_to_all | solution.py:134
  60.9 72.6 %all-to-all-done = bf16[32,2,16,3104]{3,2,1,0:T(8,128)(2,1)} async-done(((bf16[32,2,16,3104]{3,2,1,0:T(8,128)(2,1)}), bf16[32,2,16,3104]{3,2,1,0:T(8,128)(2,1)}, u32[]{:S(2)}, u32[]{:S(2)}) %all-to-all-start) | async-done | bytes 6357024 | tf_op jit(solution)/shard_map/all_to_all | solution.py:134
  133.5 16.5 %all-to-all-start.1 = ((bf16[32,2,16,2048]{3,2,1,0:T(8,128)(2,1)}), bf16[32,2,16,2048]{3,2,1,0:T(8,128)(2,1)}, u32[]{:S(2)}, u32[]{:S(2)}) async-start(bf16[32,2,16,2048]{3,2,1,0:T(8,128)(2,1)} %bitcast.140), calls=%async_computation.1 | async-start | bytes 8388608 | tf_op jit(solution)/shard_map/all_to_all | solution.py:137
  150.2 5.5 %gather_fusion.1 = bf16[32,16,3104]{2,1,0:T(8,128)(2,1)} fusion(bf16[32,2,16,3104]{3,2,1,0:T(8,128)(2,1)} %all-to-all-done, s32[32]{0:T(128)S(1)} %fusion.53), kind=kCustom, calls=%fused_computation.1 | custom fusion | bytes 6357248 | tf_op jit(solution)/shard_map/gather | solution.py:143
  157.0 3.2 slice.183
  164.3 7.8 %multiply_convert_fusion.3 = bf16[512,2048]{1,0:T(8,128)(2,1)S(1)} fusion(bf16[512,2048]{1,0:T(8,128)(2,1)} %slice.183, bf16[3,2048]{1,0:T(4,128)(2,1)S(1)} %slice-done, f32[512]{0:T(512)S(1)} %get-tuple-element.26, f32[2048]{0:T(1024)S(1)} %bitcast.166, f32[512]{0:T(512)S(1)} %get-tuple-element.27, f32[2048]{0:T(1024)S(1)} %bitcast.167, ...), kind=kLoop, calls=%fused_computation.23 | loop fusion | flops 29360128 | bytes 4245504 | tf_op jit(solution)/shard_map/convert_element_type | solution.py:75
  172.0 5.3 %reshape.326 = bf16[4,128,2,16,64]{4,3,2,1,0:T(8,128)(2,1)} reshape(bf16[512,2048]{1,0:T(8,128)(2,1)S(1)} %multiply_convert_fusion.3) | data formatting | bytes 4194304 | tf_op jit(solution)/shard_map/reshape | solution.py:176
  177.4 5.6 %copy.129 = bf16[4,128,2,16,64]{1,4,3,2,0:T(8,128)(2,1)S(1)} copy(bf16[4,128,2,16,64]{4,3,2,1,0:T(8,128)(2,1)} %reshape.326) | data formatting | bytes 4194304 | tf_op jit(solution)/shard_map/reshape | solution.py:176
  185.3 4.6 %fusion.16 = f32[4,2,16,64,256]{4,3,2,1,0:T(8,128)} fusion(bf16[4,128,2,16,64]{1,4,3,2,0:T(8,128)(2,1)S(1)} %copy.129, f32[4,128,2,16]{1,3,2,0:T(8,128)S(1)} %get-tuple-element.38, bf16[4,128,2,256,1]{3,1,0,2,4:T(8,128)(2,1)S(1)} %bitcast.144), kind=kOutput, calls=%fused_computation.31 | convolution fusion | flops 540016640 | bytes 11075584 | tf_op jit(solution)/shard_map/bsghp,bsgn->bghpn/dot_general | solution.py:196
  189.9 7.9 %multiply_add_fusion = (f32[1,2,16,64,256]{4,3,2,1,0:T(8,128)}, f32[1,2,16,64,256]{4,3,2,1,0:T(8,128)}, f32[1,2,16,64,256]{4,3,2,1,0:T(8,128)}, f32[1,2,16,64,25...) fusion(f32[2,16]{1,0:T(2,128)S(1)} %mul.481, ...), kind=kLoop, calls=%fused_computation.44 | loop fusion | flops 2621440 | bytes 23069056 | tf_op jit(solution)/shard_map/add | solution.py:204
  197.8 3.7 %fusion.60 = (bf16[32,64,256]{2,1,0:T(8,128)(2,1)S(1)}, f32[32,64,256]{2,1,0:T(8,128)}) fusion(f32[1,2,16,64,256]{4,3,2,1,0:T(8,128)} %get-tuple-element.31, f32[1,2,16,64,256]{4,3,2,1,0:T(8,128)S(1)} %get-tuple-element.30, f32[1,2,16,64,256]{4,3,2,1,0:T(8,128)S(1)} %get-tuple-element.29, f32[1,2,16,64,256]{4,3,2,1,0:T(8,128)S(1)} %get-tuple-element.28, ...), kind=kLoop, calls=%fused_computation.153 | loop fusion | flops 4194304 | bytes 11534848 | tf_op jit(solution)/shard_map/convert_element_type | solution.py:30
  208.3 4.4 %collective-permute-start.3 = (bf16[16,64,256]{2,1,0:T(8,128)(2,1)}, bf16[16,64,256]{2,1,0:T(8,128)(2,1)}, u32[]{:S(2)}, u32[]{:S(2)}) collective-permute-start(bf16[16,64,256]{2,1,0:T(8,128)(2,1)} %get-tuple-element.19), channel_id=1, source_target_pairs={{0,8},{4,12},{8,16},{12,20},{16,24},{20,28},{1,9},{5,13},{9,17},{1... | collective-permute-start | bytes 1572872 | tf_op jit(solution)/shard_map/ppermute | solution.py:30
  213.0 4.2 %gather_fusion.3 = bf16[32,16,2048]{2,1,0:T(8,128)(2,1)} fusion(bf16[32,2,16,2048]{3,2,1,0:T(8,128)(2,1)} %all-to-all-done.1, s32[32]{0:T(128)S(1)} %fusion.53), kind=kCustom, calls=%fused_computation.3 | custom fusion | bytes 4194560 | tf_op jit(solution)/shard_map/gather | solution.py:143
  217.2 7.4 %reshape.284 = f32[4,128,2,16,64]{4,3,2,1,0:T(8,128)} reshape(bf16[32,16,2048]{2,1,0:T(8,128)(2,1)} %gather_fusion.3) | data formatting | bytes 6291456 | tf_op jit(solution)/shard_map/convert_element_type | solution.py:227
  224.6 8.0 %copy.137 = f32[4,128,2,16,64]{1,4,3,2,0:T(8,128)} copy(f32[4,128,2,16,64]{4,3,2,1,0:T(8,128)} %reshape.284) | data formatting | bytes 8388608 | tf_op jit(solution)/shard_map/convert_element_type | solution.py:227
  235.1 4.6 %collective-permute-start.4 = (bf16[16,64,256]{2,1,0:T(8,128)(2,1)}, bf16[16,64,256]{2,1,0:T(8,128)(2,1)}, u32[]{:S(2)}, u32[]{:S(2)}) collective-permute-start(bf16[16,64,256]{2,1,0:T(8,128)(2,1)} %fusion.29), channel_id=1, source_target_pairs={{0,16},{4,20},{8,24},{12,28},{1,17},{5,21},{9,25},{13,29},{2,18},{... | collective-permute-start | bytes 1572872 | tf_op jit(solution)/shard_map/ppermute | solution.py:30
  244.8 5.6 %collective-permute-done.1 = f32[16]{0:T(128)S(1)} collective-permute-done((f32[16]{0:T(128)S(1)}, f32[16]{0:T(128)S(1)}, u32[]{:S(2)}, u32[]{:S(2)}) %collective-permute-start.1) | collective-permute-done | bytes 96 | tf_op jit(solution)/shard_map/ppermute | solution.py:30
  252.0 3.7 %fusion.1 = f32[4,2,16,64,128]{4,3,2,1,0:T(8,128)S(1)} fusion(bf16[4,128,2,16,64]{1,4,3,2,0:T(8,128)(2,1)S(1)} %copy-done.4, f32[4,2,16,128]{3,2,1,0:T(8,128)S(1)} %bitcast.162, f32[4,2,128,128]{3,2,1,0:T(8,128)S(1)} %fusion.33, f32[4,2,16,128]{3,2,1,0:T(8,128)S(1)} %bitcast.161, pred[4,128,128]{2,1,0:T(8,128)(4,1)S(1)} %compare_and_fusion), kind=kOutput, calls=%fused_computation.10 | convolution fusion | flops 278921216 | bytes 7012352 | tf_op jit(solution)/shard_map/bghts,bsghp->btghp/dot_general | solution.py:189
  258.7 2.9 multiply_reduce_fusion
  264.5 13.9 %convolution_convert_fusion = bf16[512,4096]{1,0:T(8,128)(2,1)} fusion(bf16[2048,4096]{1,0:T(8,128)(2,1)} %param.23, bf16[256,8,4,128]{3,2,1,0:T(4,128)(2,1)S(1)} %bitcast.155), kind=kOutput, calls=%fused_computation.7 | convolution fusion | flops 8592031744 | bytes 23068672 | tf_op jit(solution)/shard_map/dot_general | solution.py:235
  278.4 49.4 %reduce-scatter.2.cloned.1.call-done = bf16[512,1024]{1,0:T(8,128)(2,1)} async-done(((bf16[512,4096]{1,0:T(8,128)(2,1)}), bf16[512,1024]{1,0:T(8,128)(2,1)}) %reduce-scatter.2.cloned.1.call-update) | async-done | bytes 1048592 | tf_op jit(solution)/shard_map/reduce_scatter | solution.py:236
  (138 shorter events, 40.2 us)
Async XLA Ops:
  6.5 50.7 %copy-start = (bf16[1,512,2048]{2,1,0:T(8,128)(2,1)S(1)}, bf16[1,512,2048]{2,1,0:T(8,128)(2,1)}, u32[]{:S(2)}) copy-start(bf16[1,512,2048]{2,1,0:T(8,128)(2,1)} %param.13) | copy-start | bytes 6291460
  6.5 3.4 %copy-start.14 = (s32[1,512]{1,0:T(1,128)S(1)}, s32[1,512]{1,0:T(1,128)}, u32[]{:S(2)}) copy-start(s32[1,512]{1,0:T(1,128)} %param.21) | copy-start | bytes 6148
  38.4 3.1 copy-start.17
  48.0 85.5 %all-to-all-start = ((bf16[32,2,16,3104]{3,2,1,0:T(8,128)(2,1)}), bf16[32,2,16,3104]{3,2,1,0:T(8,128)(2,1)}, u32[]{:S(2)}, u32[]{:S(2)}) async-start(bf16[32,2,16,3104]{3,2,1,0:T(8,128)(2,1)} %bitcast.139), calls=%async_computation | async-start | bytes 13107200 | tf_op jit(solution)/shard_map/all_to_all | solution.py:134
  56.7 3.3 copy-start.11
  57.2 3.4 %copy-start.18 = (f32[32]{0:T(128)S(1)}, f32[32]{0:T(128)}, u32[]{:S(2)}) copy-start(f32[32]{0:T(128)} %param.16) | copy-start | bytes 388
  57.2 3.6 %copy-start.15 = (f32[4,2,512]{2,1,0:T(2,128)S(1)}, f32[4,2,512]{2,1,0:T(2,128)}, u32[]{:S(2)}) copy-start(f32[4,2,512]{2,1,0:T(2,128)} %param.19) | copy-start | bytes 49156
  57.2 3.6 %copy-start.13 = (f32[4,2048]{1,0:T(4,128)S(1)}, f32[4,2048]{1,0:T(4,128)}, u32[]{:S(2)}) copy-start(f32[4,2048]{1,0:T(4,128)} %param.18) | copy-start | bytes 98308
  133.5 79.5 %all-to-all-start.1 = ((bf16[32,2,16,2048]{3,2,1,0:T(8,128)(2,1)}), bf16[32,2,16,2048]{3,2,1,0:T(8,128)(2,1)}, u32[]{:S(2)}, u32[]{:S(2)}) async-start(bf16[32,2,16,2048]{3,2,1,0:T(8,128)(2,1)} %bitcast.140), calls=%async_computation.1 | async-start | bytes 8388608 | tf_op jit(solution)/shard_map/all_to_all | solution.py:137
  150.0 177.9 %reduce-scatter.2.cloned.1.call-start = ((), (), s32[]{:S(2)}) async-start(), calls=%async_computation.3 | async-start | bytes 5242880 | tf_op jit(solution)/shard_map/reduce_scatter | solution.py:236
  183.0 6.9 %copy-start.3 = (bf16[4,128,2,16,64]{1,4,3,2,0:T(8,128)(2,1)}, bf16[4,128,2,16,64]{1,4,3,2,0:T(8,128)(2,1)S(1)}, u32[]{:S(2)}) copy-start(bf16[4,128,2,16,64]{1,4,3,2,0:T(8,128)(2,1)S(1)} %copy.129) | copy-start | bytes 6291460
  201.6 2.7 collective-permute-start.2
  201.7 2.5 collective-permute-start
  202.1 3.2 copy-start.2
  206.9 5.8 %copy-start.19 = (f32[32]{0:T(128)S(1)}, f32[32]{0:T(128)}, u32[]{:S(2)}) copy-start(f32[32]{0:T(128)} %param.17) | copy-start | bytes 388
  206.9 5.9 %copy-start.16 = (f32[2048]{0:T(1024)S(1)}, f32[2048]{0:T(1024)}, u32[]{:S(2)}) copy-start(f32[2048]{0:T(1024)} %param.22) | copy-start | bytes 24580
  208.3 24.4 %collective-permute-start.3 = (bf16[16,64,256]{2,1,0:T(8,128)(2,1)}, bf16[16,64,256]{2,1,0:T(8,128)(2,1)}, u32[]{:S(2)}, u32[]{:S(2)}) collective-permute-start(bf16[16,64,256]{2,1,0:T(8,128)(2,1)} %get-tuple-element.19), channel_id=1, source_target_pairs={{0,8},{4,12},{8,16},{12,20},{16,24},{20,28},{1,9},{5,13},{9,17},{1... | collective-permute-start | bytes 1572872 | tf_op jit(solution)/shard_map/ppermute | solution.py:30
  235.1 15.3 %collective-permute-start.4 = (bf16[16,64,256]{2,1,0:T(8,128)(2,1)}, bf16[16,64,256]{2,1,0:T(8,128)(2,1)}, u32[]{:S(2)}, u32[]{:S(2)}) collective-permute-start(bf16[16,64,256]{2,1,0:T(8,128)(2,1)} %fusion.29), channel_id=1, source_target_pairs={{0,16},{4,20},{8,24},{12,28},{1,17},{5,21},{9,25},{13,29},{2,18},{... | collective-permute-start | bytes 1572872 | tf_op jit(solution)/shard_map/ppermute | solution.py:30
  243.4 7.0 %collective-permute-start.1 = (f32[16]{0:T(128)S(1)}, f32[16]{0:T(128)S(1)}, u32[]{:S(2)}, u32[]{:S(2)}) collective-permute-start(f32[16]{0:T(128)S(1)} %dynamic_slice.14), channel_id=1, source_target_pairs={{0,8},{4,12},{8,16},{12,20},{16,24},{20,28},{1,9},{5,13},{9,17},{1... | collective-permute-start | bytes 200 | tf_op jit(solution)/shard_map/ppermute | solution.py:30
  244.8 7.2 %copy-start.4 = (bf16[4,128,2,16,64]{1,4,3,2,0:T(8,128)(2,1)S(1)}, bf16[4,128,2,16,64]{1,4,3,2,0:T(8,128)(2,1)}, u32[]{:S(2)}) copy-start(bf16[4,128,2,16,64]{1,4,3,2,0:T(8,128)(2,1)} %copy-done.3) | copy-start | bytes 6291460
  251.8 3.8 %collective-permute-start.5 = (bf16[16,64,256]{2,1,0:T(8,128)(2,1)S(1)}, bf16[16,64,256]{2,1,0:T(8,128)(2,1)S(1)}, u32[]{:S(2)}, u32[]{:S(2)}) collective-permute-start(bf16[16,64,256]{2,1,0:T(8,128)(2,1)S(1)} %get-tuple-element.14), channel_id=1, source_target_pairs={{0,4},{4,0},{8,12},{12,8},{16,20},{20,16},{24,28},{28,24},{1,5},{5... | collective-permute-start | bytes 1572872 | tf_op jit(solution)/shard_map/ppermute | solution.py:30
  251.9 4.4 %copy-start.8 = (f32[1,2,16,64,256]{4,3,2,1,0:T(8,128)S(1)}, f32[1,2,16,64,256]{4,3,2,1,0:T(8,128)}, u32[]{:S(2)}) copy-start(f32[1,2,16,64,256]{4,3,2,1,0:T(8,128)} %get-tuple-element.24) | copy-start | bytes 6291460
  252.0 4.4 %copy-start.9 = (f32[1,2,16,64,256]{4,3,2,1,0:T(8,128)S(1)}, f32[1,2,16,64,256]{4,3,2,1,0:T(8,128)}, u32[]{:S(2)}) copy-start(f32[1,2,16,64,256]{4,3,2,1,0:T(8,128)} %get-tuple-element.25) | copy-start | bytes 6291460
  278.4 49.4 %copy-start.1 = (bf16[1,512,2048]{2,1,0:T(8,128)(2,1)S(1)}, bf16[1,512,2048]{2,1,0:T(8,128)(2,1)}, u32[]{:S(2)}) copy-start(bf16[1,512,2048]{2,1,0:T(8,128)(2,1)} %param.13) | copy-start | bytes 6291460
  (6 other events, 10.6 us)
Sparse Core Ops, SparseCore 0:
  278.5 49.2 reduce-scatter.1

commit v9 on v7

--- a/solution.py
+++ b/solution.py
@@ -116,9 +116,23 @@
     joined = jnp.concatenate(
         [token_values[0], state_maps[0].reshape(rows, map_width), step_raw[0]], axis=1
     )
-    incoming = lax.all_to_all(
-        outgoing(joined[None]), ("dp", "ctx"), split_axis=0, concat_axis=0, tiled=True
-    )
+    margin = conv_values.shape[0] - 1
+    flags = doc_start[0].astype(jnp.bfloat16)
+    halo_to = offsets == (piece_shift[slots - 1] + 1) % owners
+    flags_to = offsets == 1 % owners
+    extra = jnp.concatenate(
+        [
+            jnp.where(halo_to[:, None, None], joined[None, rows - margin :], 0),
+            jnp.where(flags_to[:, None, None], flags[None, rows - margin :, None], 0),
+        ],
+        axis=2,
+    )
+    main = outgoing(jnp.concatenate([joined, jnp.zeros_like(flags)[:, None]], axis=1)[None])
+    sending = jnp.concatenate(
+        [main.reshape((owners, most * piece_rows) + main.shape[3:]), extra], axis=1
+    )
+    received = lax.all_to_all(sending, ("dp", "ctx"), split_axis=0, concat_axis=0, tiled=True)
+    incoming = received[:, : most * piece_rows, :-1].reshape(main.shape[:3] + (-1,))
     incoming_z = lax.all_to_all(
         outgoing(gate_values), ("dp", "ctx"), split_axis=0, concat_axis=0, tiled=True
     )
@@ -128,17 +142,11 @@
         return received[source, ranking].reshape((rows,) + received.shape[3:])
 
     joined_pack = placed(incoming)
-    margin = conv_values.shape[0] - 1
-    flags = doc_start[0].astype(jnp.bfloat16)
-    edges = lax.all_gather(
-        jnp.concatenate([joined[rows - margin :], flags[rows - margin :, None]], axis=1),
-        ("dp", "ctx"),
-    )
     earlier = lax.axis_index("ctx") > 0
     rim = jnp.concatenate(
         [
-            edges[(myself - 1 - piece_shift[slots - 1]) % owners, :, :-1],
-            edges[(myself - 1) % owners, :, -1:],
+            received[(myself - 1 - piece_shift[slots - 1]) % owners, most * piece_rows :, :-1],
+            received[(myself - 1) % owners, most * piece_rows :, -1:],
         ],
         axis=1,
     )

time: 334 us -> 362 us (1.084)
  blocking collectives: 104 us -> 0 us
  waiting for transfers between devices: 57.2 us -> 156 us
  starting transfers between devices: 26 us -> 47 us
  local copies, waits for them, and re-layouts: 64.8 us -> 75 us
    all_gather x1 -> x0, blocking collectives: 104 us -> none  [body(): lax.all_gather(jnp.concatenate([joined[rows - margin:], flags[rows - marg...]
    all_to_all x1, waiting for transfers between devices: 0.01 us -> 96.6 us  [body(): lax.all_to_all(sending, ('dp', 'ctx'), split_axis=0, concat_axis=0, tiled...]
    all_to_all x1, starting transfers between devices: 6.24 us -> 27.4 us  [body(): lax.all_to_all(outgoing(gate_values), ('dp', 'ctx'), split_axis=0, concat...]
    concatenate x0 -> x1, other arithmetic: none -> 7.74 us  [body(): jnp.concatenate([main.reshape((owners, most * piece_rows) + main.shape[3:...]
    slice x2 -> x3, local copies, waits for them, and re-layouts: 0.78 us -> 7.63 us  [the longest x1 6.16 us: body(): received[:, :most * piece_rows, :-1].reshape(main.shape[:3] + (-1,))]
    concatenate x1 -> x2, local copies, waits for them, and re-layouts: 1.79 us -> 7.35 us  [body(): jnp.concatenate([joined, jnp.zeros_like(flags)[:, None]], axis=1)[None]]
    convert_element_type x2, other arithmetic: 10.2 us -> 6.21 us  [conv_core(): return jax.nn.silu(summed).astype(jnp.bfloat16)]
  transfers between devices with their start and end apart: 9 -> 9, of which waited for: 3 -> 4; matrix products, arithmetic and copies ran while one was open for 27% -> 24% of each run, Pallas kernels for 0% -> 0%
where the time goes in v9:
time: 362 us; the launch traced here: 360 us
  waiting for transfers between devices  156 us (43%)
  local copies, waits for them, and re-layouts  75 us (21%)
  starting transfers between devices  47 us (13%)
  other arithmetic  40.1 us (11%)
  matrix products  26.7 us (7%)
  between operations  15.1 us (4%)
    all_to_all x1, waiting for transfers between devices, body(): lax.all_to_all(sending, ('dp', 'ctx'), split_axis=0, concat_axis=0, tiled...  96.6 us
    reduce_scatter x1, waiting for transfers between devices, body(): lax.psum_scatter(partial_value.astype(jnp.bfloat16), 'head', scatter_dime...  49.4 us
    all_to_all x1, starting transfers between devices, body(): lax.all_to_all(outgoing(gate_values), ('dp', 'ctx'), split_axis=0, concat...  27.4 us
    convert_element_type x2, local copies, waits for them, and re-layouts, body(): z_pack.astype(jnp.float32)  15.5 us
    dot_general x1, matrix products, body(): jnp.dot(normed, out_weight, preferred_element_type=jnp.float32)  14.1 us
    ppermute x6, starting transfers between devices, across(): lax.ppermute((pair[0], pair[1].astype(jnp.bfloat16)), axis, route)  10.9 us
    reshape x2, local copies, waits for them, and re-layouts, body(): x_blocks = x_conv.reshape(blocks, span, groups_local, per_group, width)  10.9 us
    ppermute x6, waiting for transfers between devices, across(): lax.ppermute((pair[0], pair[1].astype(jnp.bfloat16)), axis, route)  9.82 us
  transfers between devices with their start and end apart: 9, of which 4 were waited for; matrix products, arithmetic and copies ran while one was open for 24% of the time, Pallas kernels for 0%

profile of v9, /device:TPU:2, one launch (start us, length us, event | category | flops | bytes accessed | tf_op | source)
XLA Modules:
  0.0 359.7 jit_solution(12067513601075617504)
XLA Ops:
  16.7 5.6 %concatenate.46 = bf16[32,16,3105]{2,1,0:T(8,128)(2,1)} concatenate(bf16[32,16,2048]{2,1,0:T(8,128)(2,1)} %bitcast.142, bf16[32,16,1024]{2,1,0:T(8,128)(2,1)S(1)} %concatenate.44, bf16[32,16,32]{2,1,0:T(8,128)(2,1)S(1)} %bitcast.157, bf16[32,16,1]{2,1,0:T(8,128)(2,1)S(1)} %broadcast_in_dim_broadcast_in_dim.3), dimensions={2} | concatenate | bytes 6359040 | tf_op jit(solution)/shard_map/concatenate | solution.py:130
  22.3 6.0 %gather_fusion = bf16[64,16,3105]{2,1,0:T(8,128)(2,1)} fusion(bf16[32,16,3105]{2,1,0:T(8,128)(2,1)} %concatenate.46, s32[1024]{0:T(1024)S(1)} %pad_clamp_fusion), kind=kCustom, calls=%fused_computation | custom fusion | bytes 12718336 | tf_op jit(solution)/shard_map/gather | solution.py:111
  28.3 7.7 %fusion.1 = bf16[32,35,3105]{2,1,0:T(8,128)(2,1)} fusion(bf16[32,3,1]{2,1,0:T(4,128)(2,1)S(1)} %broadcast_select_fusion.2, bf16[32,3,3104]{2,1,0:T(4,128)(2,1)S(1)} %copy-done.7, bf16[32,32,3105]{2,1,0:T(8,128)(2,1)} %bitcast.135), kind=kLoop, calls=%fused_computation.8 | loop fusion | flops 20865600 | bytes 13910400 | tf_op jit(solution)/shard_map/concatenate | solution.py:131
  36.0 8.5 %all-to-all-start = ((bf16[32,35,3105]{2,1,0:T(8,128)(2,1)}), bf16[32,35,3105]{2,1,0:T(8,128)(2,1)}, u32[]{:S(2)}, u32[]{:S(2)}) async-start(bf16[32,35,3105]{2,1,0:T(8,128)(2,1)} %fusion.1), calls=%async_computation | async-start | bytes 16384000 | tf_op jit(solution)/shard_map/all_to_all | solution.py:134
  48.9 96.6 %all-to-all-done = bf16[32,35,3105]{2,1,0:T(8,128)(2,1)} async-done(((bf16[32,35,3105]{2,1,0:T(8,128)(2,1)}), bf16[32,35,3105]{2,1,0:T(8,128)(2,1)}, u32[]{:S(2)}, u32[]{:S(2)}) %all-to-all-start) | async-done | bytes 6955232 | tf_op jit(solution)/shard_map/all_to_all | solution.py:134
  145.5 27.4 %all-to-all-start.1 = ((bf16[32,2,16,2048]{3,2,1,0:T(8,128)(2,1)}), bf16[32,2,16,2048]{3,2,1,0:T(8,128)(2,1)}, u32[]{:S(2)}, u32[]{:S(2)}) async-start(bf16[32,2,16,2048]{3,2,1,0:T(8,128)(2,1)} %bitcast.136), calls=%async_computation.1 | async-start | bytes 8388608 | tf_op jit(solution)/shard_map/all_to_all | solution.py:136
  174.9 6.2 %slice.183 = bf16[32,32,3104]{2,1,0:T(8,128)(2,1)} slice(bf16[32,35,3105]{2,1,0:T(8,128)(2,1)} %all-to-all-done), slice={[0:32], [0:32], [0:3104]} | slice | bytes 12713984 | tf_op jit(solution)/shard_map/slice | solution.py:135
  181.1 5.4 %gather_fusion.1 = bf16[32,16,3104]{2,1,0:T(8,128)(2,1)} fusion(bf16[32,2,16,3104]{3,2,1,0:T(8,128)(2,1)} %bitcast.137, s32[32]{0:T(128)S(1)} %fusion.53), kind=kCustom, calls=%fused_computation.1 | custom fusion | bytes 6357248 | tf_op jit(solution)/shard_map/gather | solution.py:142
  193.0 3.9 %multiply_convert_fusion.3 = bf16[512,2048]{1,0:T(8,128)(2,1)S(1)} fusion(bf16[512,2048]{1,0:T(8,128)(2,1)S(1)} %slice.184, bf16[3,2048]{1,0:T(4,128)(2,1)S(1)} %slice-done.1, f32[512]{0:T(512)S(1)} %get-tuple-element.22, f32[2048]{0:T(1024)S(1)} %bitcast.165, f32[512]{0:T(512)S(1)} %get-tuple-element.23, f32[2048]{0:T(1024)S(1)} %bitcast.166, ...), kind=kLoop, calls=%fused_computation.25 | loop fusion | flops 29360128 | bytes 4245504 | tf_op jit(solution)/shard_map/convert_element_type | solution.py:75
  196.9 5.3 %reshape.391 = bf16[4,128,2,16,64]{4,3,2,1,0:T(8,128)(2,1)} reshape(bf16[512,2048]{1,0:T(8,128)(2,1)S(1)} %multiply_convert_fusion.3) | data formatting | bytes 4194304 | tf_op jit(solution)/shard_map/reshape | solution.py:175
  202.2 5.6 %copy.77 = bf16[4,128,2,16,64]{1,4,3,2,0:T(8,128)(2,1)S(1)} copy(bf16[4,128,2,16,64]{4,3,2,1,0:T(8,128)(2,1)} %reshape.391) | data formatting | bytes 4194304 | tf_op jit(solution)/shard_map/reshape | solution.py:175
  210.1 4.6 %fusion.17 = f32[4,2,16,64,256]{4,3,2,1,0:T(8,128)} fusion(bf16[4,128,2,16,64]{1,4,3,2,0:T(8,128)(2,1)S(1)} %copy.77, f32[4,128,2,16]{1,3,2,0:T(8,128)S(1)} %get-tuple-element.34, bf16[4,128,2,256,1]{3,1,0,2,4:T(8,128)(2,1)S(1)} %bitcast.143), kind=kOutput, calls=%fused_computation.32 | convolution fusion | flops 540016640 | bytes 11075584 | tf_op jit(solution)/shard_map/bsghp,bsgn->bghpn/dot_general | solution.py:195
  214.7 7.9 %multiply_add_fusion = (f32[1,2,16,64,256]{4,3,2,1,0:T(8,128)}, f32[1,2,16,64,256]{4,3,2,1,0:T(8,128)}, f32[1,2,16,64,256]{4,3,2,1,0:T(8,128)}, f32[1,2,16,64,25...) fusion(f32[2,16]{1,0:T(2,128)S(1)} %mul.481, ...), kind=kLoop, calls=%fused_computation.45 | loop fusion | flops 2621440 | bytes 23069056 | tf_op jit(solution)/shard_map/add | solution.py:203
  222.6 3.7 %fusion.60 = (bf16[32,64,256]{2,1,0:T(8,128)(2,1)S(1)}, f32[32,64,256]{2,1,0:T(8,128)}) fusion(f32[1,2,16,64,256]{4,3,2,1,0:T(8,128)} %get-tuple-element.27, f32[1,2,16,64,256]{4,3,2,1,0:T(8,128)S(1)} %get-tuple-element.26, f32[1,2,16,64,256]{4,3,2,1,0:T(8,128)S(1)} %get-tuple-element.25, f32[1,2,16,64,256]{4,3,2,1,0:T(8,128)S(1)} %get-tuple-element.24, ...), kind=kLoop, calls=%fused_computation.156 | loop fusion | flops 4194304 | bytes 11534848 | tf_op jit(solution)/shard_map/convert_element_type | solution.py:30
  233.1 4.2 %collective-permute-start.3 = (bf16[16,64,256]{2,1,0:T(8,128)(2,1)}, bf16[16,64,256]{2,1,0:T(8,128)(2,1)}, u32[]{:S(2)}, u32[]{:S(2)}) collective-permute-start(bf16[16,64,256]{2,1,0:T(8,128)(2,1)} %get-tuple-element.15), channel_id=1, source_target_pairs={{0,8},{4,12},{8,16},{12,20},{16,24},{20,28},{1,9},{5,13},{9,17},{1... | collective-permute-start | bytes 1572872 | tf_op jit(solution)/shard_map/ppermute | solution.py:30
  237.6 4.2 %gather_fusion.3 = bf16[32,16,2048]{2,1,0:T(8,128)(2,1)} fusion(bf16[32,2,16,2048]{3,2,1,0:T(8,128)(2,1)} %all-to-all-done.1, s32[32]{0:T(128)S(1)} %fusion.53), kind=kCustom, calls=%fused_computation.3 | custom fusion | bytes 4194560 | tf_op jit(solution)/shard_map/gather | solution.py:142
  241.8 7.4 %reshape.352 = f32[4,128,2,16,64]{4,3,2,1,0:T(8,128)} reshape(bf16[32,16,2048]{2,1,0:T(8,128)(2,1)} %gather_fusion.3) | data formatting | bytes 6291456 | tf_op jit(solution)/shard_map/convert_element_type | solution.py:226
  249.2 8.1 %copy.85 = f32[4,128,2,16,64]{1,4,3,2,0:T(8,128)} copy(f32[4,128,2,16,64]{4,3,2,1,0:T(8,128)} %reshape.352) | data formatting | bytes 8388608 | tf_op jit(solution)/shard_map/convert_element_type | solution.py:226
  259.7 4.9 %collective-permute-start.4 = (bf16[16,64,256]{2,1,0:T(8,128)(2,1)}, bf16[16,64,256]{2,1,0:T(8,128)(2,1)}, u32[]{:S(2)}, u32[]{:S(2)}) collective-permute-start(bf16[16,64,256]{2,1,0:T(8,128)(2,1)} %fusion.28), channel_id=1, source_target_pairs={{0,16},{4,20},{8,24},{12,28},{1,17},{5,21},{9,25},{13,29},{2,18},{... | collective-permute-start | bytes 1572872 | tf_op jit(solution)/shard_map/ppermute | solution.py:30
  267.6 7.7 %collective-permute-done.1 = f32[16]{0:T(128)S(1)} collective-permute-done((f32[16]{0:T(128)S(1)}, f32[16]{0:T(128)S(1)}, u32[]{:S(2)}, u32[]{:S(2)}) %collective-permute-start.1) | collective-permute-done | bytes 96 | tf_op jit(solution)/shard_map/ppermute | solution.py:30
  276.8 3.7 %fusion.2 = f32[4,2,16,64,128]{4,3,2,1,0:T(8,128)S(1)} fusion(bf16[4,128,2,16,64]{1,4,3,2,0:T(8,128)(2,1)S(1)} %copy-done.4, f32[4,2,16,128]{3,2,1,0:T(8,128)S(1)} %bitcast.162, f32[4,2,128,128]{3,2,1,0:T(8,128)S(1)} %fusion.34, f32[4,2,16,128]{3,2,1,0:T(8,128)S(1)} %bitcast.161, pred[4,128,128]{2,1,0:T(8,128)(4,1)S(1)} %compare_and_fusion), kind=kOutput, calls=%fused_computation.12 | convolution fusion | flops 278921216 | bytes 7012352 | tf_op jit(solution)/shard_map/bghts,bsghp->btghp/dot_general | solution.py:188
  283.5 2.9 multiply_reduce_fusion
  289.3 14.1 %convolution_convert_fusion = bf16[512,4096]{1,0:T(8,128)(2,1)} fusion(bf16[2048,4096]{1,0:T(8,128)(2,1)} %param.23, bf16[256,8,4,128]{3,2,1,0:T(4,128)(2,1)S(1)} %bitcast.153), kind=kOutput, calls=%fused_computation.9 | convolution fusion | flops 8592031744 | bytes 23068672 | tf_op jit(solution)/shard_map/dot_general | solution.py:234
  303.4 49.4 %reduce-scatter.2.cloned.1.call-done = bf16[512,1024]{1,0:T(8,128)(2,1)} async-done(((bf16[512,4096]{1,0:T(8,128)(2,1)}), bf16[512,1024]{1,0:T(8,128)(2,1)}) %reduce-scatter.2.cloned.1.call-update) | async-done | bytes 1048592 | tf_op jit(solution)/shard_map/reduce_scatter | solution.py:235
  (139 shorter events, 43.7 us)
Async XLA Ops:
  6.5 38.9 %copy-start = (bf16[1,512,2048]{2,1,0:T(8,128)(2,1)S(1)}, bf16[1,512,2048]{2,1,0:T(8,128)(2,1)}, u32[]{:S(2)}) copy-start(bf16[1,512,2048]{2,1,0:T(8,128)(2,1)} %param.13) | copy-start | bytes 6291460
  6.5 7.2 %copy-start.12 = (bf16[1,512,32]{1,2,0:T(8,128)(2,1)S(1)}, bf16[1,512,32]{1,2,0:T(8,128)(2,1)}, u32[]{:S(2)}) copy-start(bf16[1,512,32]{1,2,0:T(8,128)(2,1)} %param.15) | copy-start | bytes 98308
  9.5 4.5 %copy-start.15 = (s32[1,512]{1,0:T(1,128)S(1)}, s32[1,512]{1,0:T(1,128)}, u32[]{:S(2)}) copy-start(s32[1,512]{1,0:T(1,128)} %param.21) | copy-start | bytes 6148
  9.5 4.6 %copy-start.18 = (s32[32]{0:T(128)S(1)}, s32[32]{0:T(128)}, u32[]{:S(2)}) copy-start(s32[32]{0:T(128)} %param.20) | copy-start | bytes 388
  22.3 6.0 %copy-start.7 = (bf16[32,3,3104]{2,1,0:T(4,128)(2,1)S(1)}, bf16[32,3,3104]{2,1,0:T(4,128)(2,1)}, u32[]{:S(2)}) copy-start(bf16[32,3,3104]{2,1,0:T(4,128)(2,1)} %broadcast_select_fusion.1) | copy-start | bytes 1787908
  36.0 109.5 %all-to-all-start = ((bf16[32,35,3105]{2,1,0:T(8,128)(2,1)}), bf16[32,35,3105]{2,1,0:T(8,128)(2,1)}, u32[]{:S(2)}, u32[]{:S(2)}) async-start(bf16[32,35,3105]{2,1,0:T(8,128)(2,1)} %fusion.1), calls=%async_computation | async-start | bytes 16384000 | tf_op jit(solution)/shard_map/all_to_all | solution.py:134
  45.4 3.4 copy-start.16
  45.5 3.4 copy-start.14
  145.5 92.1 %all-to-all-start.1 = ((bf16[32,2,16,2048]{3,2,1,0:T(8,128)(2,1)}), bf16[32,2,16,2048]{3,2,1,0:T(8,128)(2,1)}, u32[]{:S(2)}, u32[]{:S(2)}) async-start(bf16[32,2,16,2048]{3,2,1,0:T(8,128)(2,1)} %bitcast.136), calls=%async_computation.1 | async-start | bytes 8388608 | tf_op jit(solution)/shard_map/all_to_all | solution.py:136
  172.8 180.0 %reduce-scatter.2.cloned.1.call-start = ((), (), s32[]{:S(2)}) async-start(), calls=%async_computation.3 | async-start | bytes 5242880 | tf_op jit(solution)/shard_map/reduce_scatter | solution.py:235
  174.7 6.4 %copy-start.13 = (bf16[3,3105]{1,0:T(4,128)(2,1)}, bf16[3,3105]{1,0:T(4,128)(2,1)S(1)}, u32[]{:S(2)}) copy-start(bf16[3,3105]{1,0:T(4,128)(2,1)S(1)} %maximum_select_fusion.1) | copy-start | bytes 55894
  207.8 6.9 %copy-start.3 = (bf16[4,128,2,16,64]{1,4,3,2,0:T(8,128)(2,1)}, bf16[4,128,2,16,64]{1,4,3,2,0:T(8,128)(2,1)S(1)}, u32[]{:S(2)}) copy-start(bf16[4,128,2,16,64]{1,4,3,2,0:T(8,128)(2,1)S(1)} %copy.77) | copy-start | bytes 6291460
  226.3 2.7 collective-permute-start.2
  226.5 2.5 collective-permute-start
  231.7 5.6 %copy-start.20 = (f32[32]{0:T(128)S(1)}, f32[32]{0:T(128)}, u32[]{:S(2)}) copy-start(f32[32]{0:T(128)} %param.17) | copy-start | bytes 388
  231.7 5.7 %copy-start.17 = (f32[2048]{0:T(1024)S(1)}, f32[2048]{0:T(1024)}, u32[]{:S(2)}) copy-start(f32[2048]{0:T(1024)} %param.22) | copy-start | bytes 24580
  233.1 24.3 %collective-permute-start.3 = (bf16[16,64,256]{2,1,0:T(8,128)(2,1)}, bf16[16,64,256]{2,1,0:T(8,128)(2,1)}, u32[]{:S(2)}, u32[]{:S(2)}) collective-permute-start(bf16[16,64,256]{2,1,0:T(8,128)(2,1)} %get-tuple-element.15), channel_id=1, source_target_pairs={{0,8},{4,12},{8,16},{12,20},{16,24},{20,28},{1,9},{5,13},{9,17},{1... | collective-permute-start | bytes 1572872 | tf_op jit(solution)/shard_map/ppermute | solution.py:30
  259.7 15.6 %collective-permute-start.4 = (bf16[16,64,256]{2,1,0:T(8,128)(2,1)}, bf16[16,64,256]{2,1,0:T(8,128)(2,1)}, u32[]{:S(2)}, u32[]{:S(2)}) collective-permute-start(bf16[16,64,256]{2,1,0:T(8,128)(2,1)} %fusion.28), channel_id=1, source_target_pairs={{0,16},{4,20},{8,24},{12,28},{1,17},{5,21},{9,25},{13,29},{2,18},{... | collective-permute-start | bytes 1572872 | tf_op jit(solution)/shard_map/ppermute | solution.py:30
  266.2 9.0 %collective-permute-start.1 = (f32[16]{0:T(128)S(1)}, f32[16]{0:T(128)S(1)}, u32[]{:S(2)}, u32[]{:S(2)}) collective-permute-start(f32[16]{0:T(128)S(1)} %dynamic_slice.14), channel_id=1, source_target_pairs={{0,8},{4,12},{8,16},{12,20},{16,24},{20,28},{1,9},{5,13},{9,17},{1... | collective-permute-start | bytes 200 | tf_op jit(solution)/shard_map/ppermute | solution.py:30
  267.6 9.2 %copy-start.4 = (bf16[4,128,2,16,64]{1,4,3,2,0:T(8,128)(2,1)S(1)}, bf16[4,128,2,16,64]{1,4,3,2,0:T(8,128)(2,1)}, u32[]{:S(2)}) copy-start(bf16[4,128,2,16,64]{1,4,3,2,0:T(8,128)(2,1)} %copy-done.3) | copy-start | bytes 6291460
  276.7 3.8 %collective-permute-start.5 = (bf16[16,64,256]{2,1,0:T(8,128)(2,1)S(1)}, bf16[16,64,256]{2,1,0:T(8,128)(2,1)S(1)}, u32[]{:S(2)}, u32[]{:S(2)}) collective-permute-start(bf16[16,64,256]{2,1,0:T(8,128)(2,1)S(1)} %get-tuple-element.10), channel_id=1, source_target_pairs={{0,4},{4,0},{8,12},{12,8},{16,20},{20,16},{24,28},{28,24},{1,5},{5... | collective-permute-start | bytes 1572872 | tf_op jit(solution)/shard_map/ppermute | solution.py:30
  276.8 4.4 %copy-start.9 = (f32[1,2,16,64,256]{4,3,2,1,0:T(8,128)S(1)}, f32[1,2,16,64,256]{4,3,2,1,0:T(8,128)}, u32[]{:S(2)}) copy-start(f32[1,2,16,64,256]{4,3,2,1,0:T(8,128)} %get-tuple-element.20) | copy-start | bytes 6291460
  276.8 4.4 %copy-start.10 = (f32[1,2,16,64,256]{4,3,2,1,0:T(8,128)S(1)}, f32[1,2,16,64,256]{4,3,2,1,0:T(8,128)}, u32[]{:S(2)}) copy-start(f32[1,2,16,64,256]{4,3,2,1,0:T(8,128)} %get-tuple-element.21) | copy-start | bytes 6291460
  289.3 63.5 %copy-start.1 = (bf16[1,512,2048]{2,1,0:T(8,128)(2,1)S(1)}, bf16[1,512,2048]{2,1,0:T(8,128)(2,1)}, u32[]{:S(2)}) copy-start(bf16[1,512,2048]{2,1,0:T(8,128)(2,1)} %param.13) | copy-start | bytes 6291460
  (8 other events, 18.9 us)
Sparse Core Ops, SparseCore 0:
  303.5 49.2 reduce-scatter.1
